TPU v7x, 512 devices: a whole 4x8x8 slice. The times are simulated.
512 devices in a mesh: gx: 32 (over x, z), gy: 16 (over y, core).
Axes of the slice: x: 4, y: 8, z: 8, core: 2. Of those that a mesh axis runs over, the one named last changes fastest.
Arguments:
- start_disp: float32 [6, 3, 128, 128, 128], P(None, None, 'gx', 'gy'), may hold values from -6 to 6
- bone_mask: int32 [128, 128, 128], P('gx', 'gy'), may hold values from 0 to 1, as said below
- density: float32 [128, 128, 128], P('gx', 'gy'), may hold values from 0.3 to 1
- load_nodes: int32 [32, 16, 6, 32], P('gx', 'gy'), may hold values from 0 to 31
- load_forces: float32 [32, 16, 6, 3, 32], P('gx', 'gy'), may hold values from -12 to 12
Outputs:
- displacement: float32 [6, 3, 128, 128, 128], P(None, None, 'gx', 'gy')
- new_density: float32 [128, 128, 128], P('gx', 'gy')
Inputs may be any that keep to these rules, and one draw needn't show every extreme that they name: `bone_mask`: 1 marks a bone voxel.
All inputs are finite; a program needn't handle non-finite values.
Results may differ from a plain program's by a relative error of at most 0.0001.
Values sent between devices are 32-bit elements; how exact they have to be, the bound alone decides.
No kernel may reach another device: no remote copies, remote signals or barrier semaphores. Data moves between devices by JAX's collectives and lax.ppermute only.
A program may use at most 64 MiB of HBM per device.

v0:
```python
import jax
import jax.numpy as jnp
import numpy as np
from jax import lax
from jax.sharding import PartitionSpec as P

spring = 0.1
poisson = 0.3
blur_sigma = 2.0
density_cap = 1.0
mean_eps = 1e-06
highest = lax.Precision.HIGHEST


def from_behind(block, axis, distance):
    devices = range(lax.axis_size(axis))
    route = [(i - distance, i) for i in devices if i - distance in devices]
    return lax.ppermute(block, axis, route)


def with_halo(cells, sides, width):
    for axis, dim in sides:
        count = lax.axis_size(axis)
        ends = count - 1
        head = lax.slice_in_dim(cells, 0, width, axis=dim)
        tail = lax.slice_in_dim(cells, cells.shape[dim] - width, cells.shape[dim], axis=dim)
        cells = jnp.concatenate(
            [
                lax.ppermute(tail, axis, [(i, (i + 1) % count) for i in range(ends)]),
                cells,
                lax.ppermute(head, axis, [((i + 1) % count, i) for i in range(ends)]),
            ],
            axis=dim,
        )
    return cells


def hex_stiffness():
    lame_first = poisson / ((1.0 + poisson) * (1.0 - 2.0 * poisson))
    shear_mod = 1.0 / (2.0 * (1.0 + poisson))
    elastic = np.zeros((6, 6))
    elastic[:3, :3] = lame_first
    for axis_id in range(3):
        elastic[axis_id, axis_id] = lame_first + 2.0 * shear_mod
        elastic[axis_id + 3, axis_id + 3] = shear_mod
    points = [0.5 - 0.5 / np.sqrt(3.0), 0.5 + 0.5 / np.sqrt(3.0)]
    stiffness = np.zeros((24, 24))
    for point_x in points:
        for point_y in points:
            for point_z in points:
                coords = (point_x, point_y, point_z)
                strain = np.zeros((6, 24))
                for corner in range(8):
                    offsets = (corner // 4, corner // 2 % 2, corner % 2)
                    shapes = [
                        coords[axis_id] if offsets[axis_id] == 1 else 1.0 - coords[axis_id]
                        for axis_id in range(3)
                    ]
                    slopes = [1.0 if offsets[axis_id] == 1 else -1.0 for axis_id in range(3)]
                    grad_x = slopes[0] * shapes[1] * shapes[2]
                    grad_y = shapes[0] * slopes[1] * shapes[2]
                    grad_z = shapes[0] * shapes[1] * slopes[2]
                    column = 3 * corner
                    strain[0, column] = grad_x
                    strain[1, column + 1] = grad_y
                    strain[2, column + 2] = grad_z
                    strain[3, column] = grad_y
                    strain[3, column + 1] = grad_x
                    strain[4, column + 1] = grad_z
                    strain[4, column + 2] = grad_y
                    strain[5, column] = grad_z
                    strain[5, column + 2] = grad_x
                stiffness += 0.125 * strain.T @ elastic @ strain
    return stiffness


def blur_weights():
    offsets = np.arange(9) - 4.0
    unscaled = np.exp(-offsets * offsets / (2.0 * blur_sigma * blur_sigma))
    return [float(entry) for entry in unscaled / unscaled.sum()]


def blur_valid(values, axis_id, extent):
    weights = blur_weights()
    summed = weights[0] * lax.slice_in_dim(values, 0, extent, axis=axis_id)
    for tap_index in range(1, 9):
        summed = summed + weights[tap_index] * lax.slice_in_dim(
            values, tap_index, tap_index + extent, axis=axis_id
        )
    return summed


def element_disp(node_field):
    size_x = node_field.shape[1] - 1
    size_y = node_field.shape[2] - 1
    size_z = node_field.shape[3] - 1
    corners = []
    for corner in range(8):
        off_x, off_y, off_z = (corner // 4, corner // 2 % 2, corner % 2)
        corners.append(
            node_field[:, off_x : off_x + size_x, off_y : off_y + size_y, off_z : off_z + size_z]
        )
    return jnp.stack(corners).reshape(24, size_x, size_y, size_z)


def cases_disp(node_field):
    size_x = node_field.shape[2] - 1
    size_y = node_field.shape[3] - 1
    size_z = node_field.shape[4] - 1
    corners = []
    for corner in range(8):
        off_x, off_y, off_z = (corner // 4, corner // 2 % 2, corner % 2)
        corners.append(
            node_field[:, :, off_x : off_x + size_x, off_y : off_y + size_y, off_z : off_z + size_z]
        )
    return jnp.stack(corners, axis=1).reshape(
        (node_field.shape[0], 24, size_x, size_y, size_z)
    )


def element_forces(node_field, modulus, stiffness):
    local_disp = cases_disp(node_field)
    local_force = jnp.einsum("ij,cjabd->ciabd", stiffness, local_disp, precision=highest) * modulus
    local_force = local_force.reshape((node_field.shape[0], 8, 3) + modulus.shape)
    summed = jnp.zeros_like(node_field)
    for corner in range(8):
        off_x, off_y, off_z = (corner // 4, corner // 2 % 2, corner % 2)
        summed = summed + jnp.pad(
            local_force[:, corner],
            ((0, 0), (0, 0), (off_x, 1 - off_x), (off_y, 1 - off_y), (off_z, 1 - off_z)),
        )
    return summed


def element_energy(node_field, stiffness):
    local_disp = cases_disp(node_field)
    local_force = jnp.einsum("ij,cjabd->ciabd", stiffness, local_disp, precision=highest)
    return jnp.sum(local_disp * local_force, axis=(0, 1))


def local_gram(left_field, right_field):
    return jnp.einsum("iabcd,jabcd->ij", left_field, right_field, precision=highest)


def tree_sum(value):
    for axis in ("gy", "gx"):
        count = lax.axis_size(axis)
        if count & (count - 1):
            value = lax.psum(value, axis)
            continue
        step = 1
        while step < count:
            value = value + lax.ppermute(value, axis, [(i, i ^ step) for i in range(count)])
            step *= 2
    return value


def mix_cases(field, coeffs):
    return jnp.einsum("kabcd,kj->jabcd", field, coeffs, precision=highest)


def solve_spd(matrix, rhs_matrix):
    factor = jnp.linalg.cholesky(matrix)
    forward = lax.linalg.triangular_solve(factor, rhs_matrix, left_side=True, lower=True)
    return lax.linalg.triangular_solve(
        factor, forward, left_side=True, lower=True, transpose_a=True
    )


def solve_spd_rows(matrix, rhs_matrix):
    factor = jnp.linalg.cholesky(matrix)
    matrix_order = matrix.shape[0]
    forward = []
    for row_index in range(matrix_order):
        partial_sum = rhs_matrix[row_index]
        for col_index in range(row_index):
            partial_sum = partial_sum - factor[row_index, col_index] * forward[col_index]
        forward.append(partial_sum / factor[row_index, row_index])
    backward = [None] * matrix_order
    for row_index in reversed(range(matrix_order)):
        partial_sum = forward[row_index]
        for col_index in range(row_index + 1, matrix_order):
            partial_sum = partial_sum - factor[col_index, row_index] * backward[col_index]
        backward[row_index] = partial_sum / factor[row_index, row_index]
    return jnp.stack(backward)


def pad_upper_z(field):
    return jnp.pad(field, ((0, 0), (0, 0), (0, 0), (0, 0), (0, 1)))


def gather_upper(field):
    from_x = from_behind(field[:, :, :1], "gx", -1)
    widened = jnp.concatenate([field, from_x], axis=2)
    from_y = from_behind(widened[:, :, :, :1], "gy", -1)
    return jnp.concatenate([widened, from_y], axis=3)


def return_lower(forces):
    size_x = forces.shape[2] - 1
    size_y = forces.shape[3] - 1
    to_y = from_behind(forces[:, :, :, size_y:], "gy", 1)
    kept = forces[:, :, :, :size_y]
    kept = jnp.concatenate([kept[:, :, :, :1] + to_y, kept[:, :, :, 1:]], axis=3)
    to_x = from_behind(kept[:, :, size_x:], "gx", 1)
    kept = kept[:, :, :size_x]
    return jnp.concatenate([kept[:, :, :1] + to_x, kept[:, :, 1:]], axis=2)


def on_device(start_disp, bone_mask, density, load_nodes, load_forces):
    stiffness = jnp.asarray(hex_stiffness(), jnp.float32)
    modulus = bone_mask.astype(jnp.float32) * density * density
    case_count = start_disp.shape[0]
    size_x = start_disp.shape[2]
    size_y = start_disp.shape[3]
    size_z = start_disp.shape[4]

    def apply_operator(field):
        node_field = pad_upper_z(gather_upper(field))
        forces = element_forces(node_field, modulus, stiffness)
        return return_lower(forces[..., :-1]) + spring * field, node_field

    slot_ids = jnp.arange(size_x * size_y, dtype=jnp.int32)
    matches = (load_nodes[0, 0][:, :, None] == slot_ids).astype(jnp.float32)
    top_plane = jnp.einsum("cls,ckl->cks", matches, load_forces[0, 0], precision=highest).reshape(
        case_count, 3, size_x, size_y
    )
    applied, start_nodes = apply_operator(start_disp)
    residual = jnp.concatenate(
        [-applied[..., :-1], (top_plane - applied[..., -1])[..., None]], axis=4
    )
    applied, residual_nodes = apply_operator(residual)
    blur_mass = modulus
    for dim, axis in ((0, "gx"), (1, "gy"), (2, None)):
        extent = modulus.shape[dim]
        count = 1 if axis is None else lax.axis_size(axis)
        places = np.arange(extent * count)
        kept = np.zeros(extent * count)
        for tap_index, weight in enumerate(blur_weights()):
            inside = (places + 4 - tap_index >= 0) & (places + 4 - tap_index < extent * count)
            kept = kept + np.where(inside, weight, 0.0)
        kept = jnp.asarray(kept, jnp.float32)
        if axis is not None:
            kept = lax.dynamic_slice_in_dim(kept, lax.axis_index(axis) * extent, extent)
        shape = [1, 1, 1]
        shape[dim] = extent
        blur_mass = blur_mass * kept.reshape(shape)
    start_elems = cases_disp(start_nodes)
    start_loads = jnp.einsum("ij,cjabd->ciabd", stiffness, start_elems, precision=highest)
    residual_elems = cases_disp(residual_nodes)
    residual_loads = jnp.einsum(
        "ij,cjabd->ciabd", stiffness, residual_elems, precision=highest
    )
    start_energy = jnp.sum(start_elems * start_loads * blur_mass, axis=(1, 2, 3, 4))
    start_weighted = start_loads * blur_mass
    residual_weighted = residual_loads * blur_mass
    cross_energy = jnp.sum(
        residual_elems[:, None] * start_weighted[None, :], axis=(2, 3, 4, 5)
    )
    residual_energy = jnp.sum(
        residual_elems[:, None] * residual_weighted[None, :], axis=(2, 3, 4, 5)
    )
    grams = tree_sum(
        jnp.stack(
            [
                local_gram(residual, residual),
                local_gram(residual, applied),
                cross_energy,
                residual_energy,
                jnp.diag(start_energy),
            ]
        )
    )
    norm_now = grams[0]
    step_alpha = solve_spd(grams[1], norm_now)
    summed = (
        jnp.sum(grams[4])
        + 2.0 * jnp.sum(step_alpha * grams[2])
        + jnp.sum(step_alpha[:, None, :] * grams[3][:, :, None] * step_alpha[None, :, :])
    )
    solution = start_disp + mix_cases(residual, step_alpha)
    node_field = start_nodes + mix_cases(residual_nodes, step_alpha)
    energy = element_energy(node_field, stiffness)
    stimulus = modulus * energy
    smooth = blur_valid(with_halo(stimulus, (("gx", 0),), 4), 0, size_x)
    smooth = blur_valid(with_halo(smooth, (("gy", 1),), 4), 1, size_y)
    smooth = blur_valid(jnp.pad(smooth, ((0, 0), (0, 0), (4, 4))), 2, size_z)
    mean_stim = summed / (size_x * size_y * size_z * lax.axis_size("gx") * lax.axis_size("gy"))
    new_density = jnp.minimum(density * (0.5 + 0.5 * smooth / (mean_stim + mean_eps)), density_cap)
    return (solution, new_density)


def solution(mesh):
    return jax.shard_map(
        on_device,
        mesh=mesh,
        in_specs=(
            P(None, None, "gx", "gy", None),
            P("gx", "gy", None),
            P("gx", "gy", None),
            P("gx", "gy", None, None),
            P("gx", "gy", None, None, None),
        ),
        out_specs=(P(None, None, "gx", "gy", None), P("gx", "gy", None)),
        check_vma=False,
    )
```

profile of v0, /device:TPU:31, one launch (start us, length us, event | category | flops | bytes accessed | tf_op | source)
XLA Modules:
  0.0 182.9 jit_solution(18027441092692831554)
XLA Ops:
  1.5 10.9 %collective-permute-start = (f32[6,3,1,8,128]{4,0,3,2,1:T(8,128)S(1)}, f32[6,3,1,8,128]{4,0,3,2,1:T(8,128)S(1)}, u32[]{:S(2)}, u32[]{:S(2)}) collective-permute-start(f32[6,3,1,8,128]{4,0,3,2,1:T(8,128)S(1)} %copy.136), channel_id=1, source_target_pairs={{16,0},{32,16},{48,32},{64,48},{80,64},{96,80},{112,96},{128,112},... | collective-permute-start | bytes 221192 | tf_op jit(solution)/shard_map/ppermute | solution.py:18
  12.5 1.1 copy_dynamic-update-slice_fusion
  13.6 1.9 %bitcast_dynamic-update-slice_fusion.1 = f32[6,8,3,4,8,128]{5,0,4,3,2,1:T(8,128)} fusion(f32[6,3,4,8,128]{4,3,2,1,0:T(8,128)} %param.9), kind=kLoop, calls=%fused_computation.120 | loop fusion | bytes 688128
  17.0 2.9 %collective-permute-start.1 = (f32[6,3,5,1,128]{4,0,3,2,1:T(8,128)S(1)}, f32[6,3,5,1,128]{4,0,3,2,1:T(8,128)S(1)}, u32[]{:S(2)}, u32[]{:S(2)}) collective-permute-start(f32[6,3,5,1,128]{4,0,3,2,1:T(8,128)S(1)} %slice.418), channel_id=1, source_target_pairs={{1,0},{2,1},{3,2},{4,3},{5,4},{6,5},{7,6},{8,7},{9,8},{10,9},{11,1... | collective-permute-start | bytes 138248 | tf_op jit(solution)/shard_map/ppermute | solution.py:18
  20.7 3.5 %collective-permute-done.1 = f32[6,3,5,1,128]{4,0,3,2,1:T(8,128)S(1)} collective-permute-done((f32[6,3,5,1,128]{4,0,3,2,1:T(8,128)S(1)}, f32[6,3,5,1,128]{4,0,3,2,1:T(8,128)S(1)}, u32[]{:S(2)}, u32[]{:S(2)}) %collective-permute-start.1) | collective-permute-done | bytes 46112 | tf_op jit(solution)/shard_map/ppermute | solution.py:18
  30.3 7.7 %fusion.2 = (f32[6]{0:T(128)S(1)}, f32[6,24,4,8,128]{4,1,3,2,0:T(8,128)S(1)}, f32[6,24,4,8,128]{4,1,3,2,0:T(8,128)S(1)}) fusion(f32[6,24,4,8,128]{4,0,3,2,1:T(8,128)} %bitcast.235, f32[4,8,128]{2,1,0:T(8,128)S(1)} %get-tuple-element.10, f32[4,8,128]{2,1,0:T(8,128)S(1)} %get-tuple-element.11, f32[24,24,1,1,1]{1,0,4,3,2:T(8,128)S(1)} %copy-done.2), kind=kOutput, calls=%fused_computation.8 | convolution fusion | flops 172818432 | bytes 7112984 | tf_op jit(solution)/shard_map/ij,cjabd->ciabd/dot_general | solution.py:123
  37.9 1.4 copy.104
  40.7 1.9 %collective-permute-start.2 = (f32[6,3,5,1,128]{4,0,3,2,1:T(8,128)S(1)}, f32[6,3,5,1,128]{4,0,3,2,1:T(8,128)S(1)}, u32[]{:S(2)}, u32[]{:S(2)}) collective-permute-start(f32[6,3,5,1,128]{4,0,3,2,1:T(8,128)S(1)} %slice.433), channel_id=1, source_target_pairs={{0,1},{1,2},{2,3},{3,4},{4,5},{5,6},{6,7},{7,8},{8,9},{9,10},{10,1... | collective-permute-start | bytes 138248 | tf_op jit(solution)/shard_map/ppermute | solution.py:18
  42.7 1.2 collective-permute-done.2
  44.5 1.9 %collective-permute-start.3 = (f32[6,3,1,8,128]{4,0,3,2,1:T(8,128)}, f32[6,3,1,8,128]{4,0,3,2,1:T(8,128)}, u32[]{:S(2)}, u32[]{:S(2)}) collective-permute-start(f32[6,3,1,8,128]{4,0,3,2,1:T(8,128)} %pad_maximum_fusion.6), channel_id=1, source_target_pairs={{0,16},{16,32},{32,48},{48,64},{64,80},{80,96},{96,112},{112,128},... | collective-permute-start | bytes 221192 | tf_op jit(solution)/shard_map/ppermute | solution.py:18
  46.8 1.2 copy.83
  48.1 5.2 %collective-permute-done.3 = f32[6,3,1,8,128]{4,0,3,2,1:T(8,128)} collective-permute-done((f32[6,3,1,8,128]{4,0,3,2,1:T(8,128)}, f32[6,3,1,8,128]{4,0,3,2,1:T(8,128)}, u32[]{:S(2)}, u32[]{:S(2)}) %collective-permute-start.3) | collective-permute-done | bytes 73760 | tf_op jit(solution)/shard_map/ppermute | solution.py:18
  54.1 1.2 fusion.58
  55.6 1.9 %collective-permute-start.4 = (f32[6,3,1,8,128]{4,0,3,2,1:T(8,128)S(1)}, f32[6,3,1,8,128]{4,0,3,2,1:T(8,128)S(1)}, u32[]{:S(2)}, u32[]{:S(2)}) collective-permute-start(f32[6,3,1,8,128]{4,0,3,2,1:T(8,128)S(1)} %fusion.65), channel_id=1, source_target_pairs={{16,0},{32,16},{48,32},{64,48},{80,64},{96,80},{112,96},{128,112},... | collective-permute-start | bytes 221192 | tf_op jit(solution)/shard_map/ppermute | solution.py:18
  58.0 3.0 %collective-permute-done.4 = f32[6,3,1,8,128]{4,0,3,2,1:T(8,128)S(1)} collective-permute-done((f32[6,3,1,8,128]{4,0,3,2,1:T(8,128)S(1)}, f32[6,3,1,8,128]{4,0,3,2,1:T(8,128)S(1)}, u32[]{:S(2)}, u32[]{:S(2)}) %collective-permute-start.4) | collective-permute-done | bytes 73760 | tf_op jit(solution)/shard_map/ppermute | solution.py:18
  61.1 4.1 %collective-permute-start.5 = (f32[6,3,5,1,128]{4,0,3,2,1:T(8,128)S(1)}, f32[6,3,5,1,128]{4,0,3,2,1:T(8,128)S(1)}, u32[]{:S(2)}, u32[]{:S(2)}) collective-permute-start(f32[6,3,5,1,128]{4,0,3,2,1:T(8,128)S(1)} %pad_maximum_fusion.7), channel_id=1, source_target_pairs={{1,0},{2,1},{3,2},{4,3},{5,4},{6,5},{7,6},{8,7},{9,8},{10,9},{11,1... | collective-permute-start | bytes 138248 | tf_op jit(solution)/shard_map/ppermute | solution.py:18
  65.4 4.5 %collective-permute-done.5 = f32[6,3,5,1,128]{4,0,3,2,1:T(8,128)S(1)} collective-permute-done((f32[6,3,5,1,128]{4,0,3,2,1:T(8,128)S(1)}, f32[6,3,5,1,128]{4,0,3,2,1:T(8,128)S(1)}, u32[]{:S(2)}, u32[]{:S(2)}) %collective-permute-start.5) | collective-permute-done | bytes 46112 | tf_op jit(solution)/shard_map/ppermute | solution.py:18
  70.9 3.6 %multiply_bitcast_fusion = (f32[6,24,4,8,128]{4,1,3,2,0:T(8,128)S(1)}, f32[6,24,4,8,128]{4,1,3,2,0:T(8,128)S(1)}) fusion(f32[4,8,128]{2,1,0:T(8,128)S(1)} %get-tuple-element.10, f32[4,8,128]{2,1,0:T(8,128)S(1)} %get-tuple-element.11, f32[24,24,1,1,1]{1,0,4,3,2:T(8,128)S(1)} %copy-done.2, f32[6,24,4,8,128]{4,0,3,2,1:T(8,128)S(1)} %bitcast.232), kind=kOutput, calls=%fused_computation.11 | convolution fusion | flops 171048960 | bytes 7112960 | tf_op jit(solution)/shard_map/ij,cjabd->ciabd/dot_general | solution.py:123
  74.6 1.4 copy.85
  77.3 1.9 %collective-permute-start.6 = (f32[6,3,5,1,128]{4,0,3,2,1:T(8,128)S(1)}, f32[6,3,5,1,128]{4,0,3,2,1:T(8,128)S(1)}, u32[]{:S(2)}, u32[]{:S(2)}) collective-permute-start(f32[6,3,5,1,128]{4,0,3,2,1:T(8,128)S(1)} %slice.450), channel_id=1, source_target_pairs={{0,1},{1,2},{2,3},{3,4},{4,5},{5,6},{6,7},{7,8},{8,9},{9,10},{10,1... | collective-permute-start | bytes 138248 | tf_op jit(solution)/shard_map/ppermute | solution.py:18
  79.3 1.0 fusion.16
  81.2 2.1 %collective-permute-start.7 = (f32[6,3,1,8,128]{4,0,3,2,1:T(8,128)S(1)}, f32[6,3,1,8,128]{4,0,3,2,1:T(8,128)S(1)}, u32[]{:S(2)}, u32[]{:S(2)}) collective-permute-start(f32[6,3,1,8,128]{4,0,3,2,1:T(8,128)S(1)} %pad_maximum_fusion.5), channel_id=1, source_target_pairs={{0,16},{16,32},{32,48},{48,64},{64,80},{80,96},{96,112},{112,128},... | collective-permute-start | bytes 221192 | tf_op jit(solution)/shard_map/ppermute | solution.py:18
  83.4 3.3 %multiply_reduce_fusion = (f32[6,6]{1,0:T(8,128)S(1)}, f32[6,6]{1,0:T(8,128)S(1)}) fusion(f32[6,24,4,8,128]{4,3,2,1,0:T(8,128)S(1)} %copy.88, f32[6,24,4,8,128]{4,3,2,1,0:T(8,128)S(1)} %copy.86, f32[6,24,4,8,128]{4,3,2,1,0:T(8,128)S(1)} %copy.87), kind=kLoop, calls=%fused_computation | loop fusion | flops 14155704 | bytes 7078176 | tf_op jit(solution)/shard_map/reduce_sum | solution.py:260
  86.7 2.4 %collective-permute-done.7 = f32[6,3,1,8,128]{4,0,3,2,1:T(8,128)S(1)} collective-permute-done((f32[6,3,1,8,128]{4,0,3,2,1:T(8,128)S(1)}, f32[6,3,1,8,128]{4,0,3,2,1:T(8,128)S(1)}, u32[]{:S(2)}, u32[]{:S(2)}) %collective-permute-start.7) | collective-permute-done | bytes 73760 | tf_op jit(solution)/shard_map/ppermute | solution.py:18
  89.1 1.0 fusion.15
  90.2 3.3 %collective-permute-start.8 = (f32[5,6,6]{2,1,0:T(8,128)S(1)}, f32[5,6,6]{2,1,0:T(8,128)S(1)}, u32[]{:S(2)}, u32[]{:S(2)}) collective-permute-start(f32[5,6,6]{2,1,0:T(8,128)S(1)} %constant_dynamic-update-slice_fusion.1), channel_id=1, source_target_pairs={{0,1},{1,0},{2,3},{3,2},{4,5},{5,4},{6,7},{7,6},{8,9},{9,8},{10,11... | collective-permute-start | bytes 2168 | tf_op jit(solution)/shard_map/ppermute | solution.py:153
  94.3 1.9 %collective-permute-start.9 = (f32[5,6,6]{2,1,0:T(8,128)S(1)}, f32[5,6,6]{2,1,0:T(8,128)S(1)}, u32[]{:S(2)}, u32[]{:S(2)}) collective-permute-start(f32[5,6,6]{2,1,0:T(8,128)S(1)} %add.256), channel_id=1, source_target_pairs={{0,2},{1,3},{2,0},{3,1},{4,6},{5,7},{6,4},{7,5},{8,10},{9,11},{10,... | collective-permute-start | bytes 2168 | tf_op jit(solution)/shard_map/ppermute | solution.py:153
  96.2 2.6 %collective-permute-done.9 = f32[5,6,6]{2,1,0:T(8,128)S(1)} collective-permute-done((f32[5,6,6]{2,1,0:T(8,128)S(1)}, f32[5,6,6]{2,1,0:T(8,128)S(1)}, u32[]{:S(2)}, u32[]{:S(2)}) %collective-permute-start.9) | collective-permute-done | bytes 752 | tf_op jit(solution)/shard_map/ppermute | solution.py:153
  98.8 1.9 %collective-permute-start.10 = (f32[5,6,6]{2,1,0:T(8,128)S(1)}, f32[5,6,6]{2,1,0:T(8,128)S(1)}, u32[]{:S(2)}, u32[]{:S(2)}) collective-permute-start(f32[5,6,6]{2,1,0:T(8,128)S(1)} %add.257), channel_id=1, source_target_pairs={{0,4},{1,5},{2,6},{3,7},{4,0},{5,1},{6,2},{7,3},{8,12},{9,13},{10,... | collective-permute-start | bytes 2168 | tf_op jit(solution)/shard_map/ppermute | solution.py:153
  100.7 3.5 %collective-permute-done.10 = f32[5,6,6]{2,1,0:T(8,128)S(1)} collective-permute-done((f32[5,6,6]{2,1,0:T(8,128)S(1)}, f32[5,6,6]{2,1,0:T(8,128)S(1)}, u32[]{:S(2)}, u32[]{:S(2)}) %collective-permute-start.10) | collective-permute-done | bytes 752 | tf_op jit(solution)/shard_map/ppermute | solution.py:153
  104.2 3.8 %collective-permute-start.11 = (f32[5,6,6]{2,1,0:T(8,128)S(1)}, f32[5,6,6]{2,1,0:T(8,128)S(1)}, u32[]{:S(2)}, u32[]{:S(2)}) collective-permute-start(f32[5,6,6]{2,1,0:T(8,128)S(1)} %add.258), channel_id=1, source_target_pairs={{0,8},{1,9},{2,10},{3,11},{4,12},{5,13},{6,14},{7,15},{8,0},{9,1},... | collective-permute-start | bytes 2168 | tf_op jit(solution)/shard_map/ppermute | solution.py:153
  108.0 4.6 %collective-permute-done.11 = f32[5,6,6]{2,1,0:T(8,128)S(1)} collective-permute-done((f32[5,6,6]{2,1,0:T(8,128)S(1)}, f32[5,6,6]{2,1,0:T(8,128)S(1)}, u32[]{:S(2)}, u32[]{:S(2)}) %collective-permute-start.11) | collective-permute-done | bytes 752 | tf_op jit(solution)/shard_map/ppermute | solution.py:153
  112.6 1.9 %collective-permute-start.12 = (f32[5,6,6]{2,1,0:T(8,128)S(1)}, f32[5,6,6]{2,1,0:T(8,128)S(1)}, u32[]{:S(2)}, u32[]{:S(2)}) collective-permute-start(f32[5,6,6]{2,1,0:T(8,128)S(1)} %add.259), channel_id=1, source_target_pairs={{0,16},{16,0},{32,48},{48,32},{64,80},{80,64},{96,112},{112,96},{1... | collective-permute-start | bytes 2168 | tf_op jit(solution)/shard_map/ppermute | solution.py:153
  114.6 2.6 %collective-permute-done.12 = f32[5,6,6]{2,1,0:T(8,128)S(1)} collective-permute-done((f32[5,6,6]{2,1,0:T(8,128)S(1)}, f32[5,6,6]{2,1,0:T(8,128)S(1)}, u32[]{:S(2)}, u32[]{:S(2)}) %collective-permute-start.12) | collective-permute-done | bytes 752 | tf_op jit(solution)/shard_map/ppermute | solution.py:153
  117.2 1.9 %collective-permute-start.13 = (f32[5,6,6]{2,1,0:T(8,128)S(1)}, f32[5,6,6]{2,1,0:T(8,128)S(1)}, u32[]{:S(2)}, u32[]{:S(2)}) collective-permute-start(f32[5,6,6]{2,1,0:T(8,128)S(1)} %add.260), channel_id=1, source_target_pairs={{0,32},{16,48},{32,0},{48,16},{64,96},{80,112},{96,64},{112,80},{1... | collective-permute-start | bytes 2168 | tf_op jit(solution)/shard_map/ppermute | solution.py:153
  119.1 3.5 %collective-permute-done.13 = f32[5,6,6]{2,1,0:T(8,128)S(1)} collective-permute-done((f32[5,6,6]{2,1,0:T(8,128)S(1)}, f32[5,6,6]{2,1,0:T(8,128)S(1)}, u32[]{:S(2)}, u32[]{:S(2)}) %collective-permute-start.13) | collective-permute-done | bytes 752 | tf_op jit(solution)/shard_map/ppermute | solution.py:153
  122.6 1.9 %collective-permute-start.14 = (f32[5,6,6]{2,1,0:T(8,128)S(1)}, f32[5,6,6]{2,1,0:T(8,128)S(1)}, u32[]{:S(2)}, u32[]{:S(2)}) collective-permute-start(f32[5,6,6]{2,1,0:T(8,128)S(1)} %add.261), channel_id=1, source_target_pairs={{0,64},{16,80},{32,96},{48,112},{64,0},{80,16},{96,32},{112,48},{1... | collective-permute-start | bytes 2168 | tf_op jit(solution)/shard_map/ppermute | solution.py:153
  124.5 6.5 %collective-permute-done.14 = f32[5,6,6]{2,1,0:T(8,128)S(1)} collective-permute-done((f32[5,6,6]{2,1,0:T(8,128)S(1)}, f32[5,6,6]{2,1,0:T(8,128)S(1)}, u32[]{:S(2)}, u32[]{:S(2)}) %collective-permute-start.14) | collective-permute-done | bytes 752 | tf_op jit(solution)/shard_map/ppermute | solution.py:153
  131.0 2.4 %collective-permute-start.15 = (f32[5,6,6]{2,1,0:T(8,128)S(1)}, f32[5,6,6]{2,1,0:T(8,128)S(1)}, u32[]{:S(2)}, u32[]{:S(2)}) collective-permute-start(f32[5,6,6]{2,1,0:T(8,128)S(1)} %add.262), channel_id=1, source_target_pairs={{0,128},{16,144},{32,160},{48,176},{64,192},{80,208},{96,224},{112... | collective-permute-start | bytes 2168 | tf_op jit(solution)/shard_map/ppermute | solution.py:153
  133.4 2.1 %collective-permute-done.15 = f32[5,6,6]{2,1,0:T(8,128)S(1)} collective-permute-done((f32[5,6,6]{2,1,0:T(8,128)S(1)}, f32[5,6,6]{2,1,0:T(8,128)S(1)}, u32[]{:S(2)}, u32[]{:S(2)}) %collective-permute-start.15) | collective-permute-done | bytes 752 | tf_op jit(solution)/shard_map/ppermute | solution.py:153
  135.5 3.2 %collective-permute-start.16 = (f32[5,6,6]{2,1,0:T(8,128)S(1)}, f32[5,6,6]{2,1,0:T(8,128)S(1)}, u32[]{:S(2)}, u32[]{:S(2)}) collective-permute-start(f32[5,6,6]{2,1,0:T(8,128)S(1)} %add.263), channel_id=1, source_target_pairs={{0,256},{16,272},{32,288},{48,304},{64,320},{80,336},{96,352},{112... | collective-permute-start | bytes 2168 | tf_op jit(solution)/shard_map/ppermute | solution.py:153
  138.8 2.8 %collective-permute-done.16 = f32[5,6,6]{2,1,0:T(8,128)S(1)} collective-permute-done((f32[5,6,6]{2,1,0:T(8,128)S(1)}, f32[5,6,6]{2,1,0:T(8,128)S(1)}, u32[]{:S(2)}, u32[]{:S(2)}) %collective-permute-start.16) | collective-permute-done | bytes 752 | tf_op jit(solution)/shard_map/ppermute | solution.py:153
  145.6 1.3 pad_add_fusion
  147.7 5.0 %fusion = f32[4,8,128]{2,1,0:T(8,128)S(1)} fusion(f32[6,24,4,8,128]{4,0,3,2,1:T(8,128)S(1)} %bitcast.234, f32[24,24,1,1,1]{1,0,4,3,2:T(8,128)S(1)} %copy-done.2), kind=kOutput, calls=%fused_computation.3 | convolution fusion | flops 171044864 | bytes 2377984 | tf_op jit(solution)/shard_map/ij,cjabd->ciabd/dot_general | solution.py:137
  152.7 2.5 %collective-permute-start.17 = (f32[4,8,128]{2,1,0:T(8,128)S(1)}, f32[4,8,128]{2,1,0:T(8,128)S(1)}, u32[]{:S(2)}, u32[]{:S(2)}) collective-permute-start(f32[4,8,128]{2,1,0:T(8,128)S(1)} %mul.262), channel_id=1, source_target_pairs={{0,16},{16,32},{32,48},{48,64},{64,80},{80,96},{96,112},{112,128},... | collective-permute-start | bytes 49160 | tf_op jit(solution)/shard_map/ppermute | solution.py:29
  155.2 4.9 %collective-permute-start.18 = (f32[4,8,128]{2,1,0:T(8,128)S(1)}, f32[4,8,128]{2,1,0:T(8,128)S(1)}, u32[]{:S(2)}, u32[]{:S(2)}) collective-permute-start(f32[4,8,128]{2,1,0:T(8,128)S(1)} %mul.262), channel_id=1, source_target_pairs={{16,0},{32,16},{48,32},{64,48},{80,64},{96,80},{112,96},{128,112},... | collective-permute-start | bytes 49160 | tf_op jit(solution)/shard_map/ppermute | solution.py:31
  161.0 14.9 %collective-permute-start.19 = (f32[4,4,128]{2,1,0:T(4,128)S(1)}, f32[4,4,128]{2,1,0:T(4,128)S(1)}, u32[]{:S(2)}, u32[]{:S(2)}) collective-permute-start(f32[4,4,128]{2,1,0:T(4,128)S(1)} %get-tuple-element.38), channel_id=1, source_target_pairs={{0,1},{1,2},{2,3},{3,4},{4,5},{5,6},{6,7},{7,8},{8,9},{9,10},{10,1... | collective-permute-start | bytes 24584 | tf_op jit(solution)/shard_map/ppermute | solution.py:29
  175.9 1.9 %collective-permute-start.20 = (f32[4,4,128]{2,1,0:T(4,128)S(1)}, f32[4,4,128]{2,1,0:T(4,128)S(1)}, u32[]{:S(2)}, u32[]{:S(2)}) collective-permute-start(f32[4,4,128]{2,1,0:T(4,128)S(1)} %get-tuple-element.39), channel_id=1, source_target_pairs={{1,0},{2,1},{3,2},{4,3},{5,4},{6,5},{7,6},{8,7},{9,8},{10,9},{11,1... | collective-permute-start | bytes 24584 | tf_op jit(solution)/shard_map/ppermute | solution.py:31
  (105 shorter events, 26.5 us)
Async XLA Ops:
  1.5 15.4 %collective-permute-start = (f32[6,3,1,8,128]{4,0,3,2,1:T(8,128)S(1)}, f32[6,3,1,8,128]{4,0,3,2,1:T(8,128)S(1)}, u32[]{:S(2)}, u32[]{:S(2)}) collective-permute-start(f32[6,3,1,8,128]{4,0,3,2,1:T(8,128)S(1)} %copy.136), channel_id=1, source_target_pairs={{16,0},{32,16},{48,32},{64,48},{80,64},{96,80},{112,96},{128,112},... | collective-permute-start | bytes 221192 | tf_op jit(solution)/shard_map/ppermute | solution.py:18
  17.0 7.2 %collective-permute-start.1 = (f32[6,3,5,1,128]{4,0,3,2,1:T(8,128)S(1)}, f32[6,3,5,1,128]{4,0,3,2,1:T(8,128)S(1)}, u32[]{:S(2)}, u32[]{:S(2)}) collective-permute-start(f32[6,3,5,1,128]{4,0,3,2,1:T(8,128)S(1)} %slice.418), channel_id=1, source_target_pairs={{1,0},{2,1},{3,2},{4,3},{5,4},{6,5},{7,6},{8,7},{9,8},{10,9},{11,1... | collective-permute-start | bytes 138248 | tf_op jit(solution)/shard_map/ppermute | solution.py:18
  25.9 4.4 %copy-start.2 = (f32[24,24,1,1,1]{1,0,4,3,2:T(8,128)S(1)}, f32[24,24,1,1,1]{1,0,4,3,2:T(8,128)}, u32[]{:S(2)}) copy-start(f32[24,24,1,1,1]{1,0,4,3,2:T(8,128)} %constant.137) | copy-start | bytes 6916
  39.8 2.8 %copy-start.4 = (s32[1,1,6,32]{3,1,2,0:T(1,128)S(1)}, s32[1,1,6,32]{3,1,2,0:T(1,128)}, u32[]{:S(2)}) copy-start(s32[1,1,6,32]{3,1,2,0:T(1,128)} %param.12) | copy-start | bytes 2308
  39.8 6.7 %copy-start.5 = (f32[1,1,6,3,32]{4,1,3,2,0:T(1,128)S(1)}, f32[1,1,6,3,32]{4,1,3,2,0:T(1,128)}, u32[]{:S(2)}) copy-start(f32[1,1,6,3,32]{4,1,3,2,0:T(1,128)} %param.13) | copy-start | bytes 6916
  40.7 3.2 %collective-permute-start.2 = (f32[6,3,5,1,128]{4,0,3,2,1:T(8,128)S(1)}, f32[6,3,5,1,128]{4,0,3,2,1:T(8,128)S(1)}, u32[]{:S(2)}, u32[]{:S(2)}) collective-permute-start(f32[6,3,5,1,128]{4,0,3,2,1:T(8,128)S(1)} %slice.433), channel_id=1, source_target_pairs={{0,1},{1,2},{2,3},{3,4},{4,5},{5,6},{6,7},{7,8},{8,9},{9,10},{10,1... | collective-permute-start | bytes 138248 | tf_op jit(solution)/shard_map/ppermute | solution.py:18
  44.5 8.7 %collective-permute-start.3 = (f32[6,3,1,8,128]{4,0,3,2,1:T(8,128)}, f32[6,3,1,8,128]{4,0,3,2,1:T(8,128)}, u32[]{:S(2)}, u32[]{:S(2)}) collective-permute-start(f32[6,3,1,8,128]{4,0,3,2,1:T(8,128)} %pad_maximum_fusion.6), channel_id=1, source_target_pairs={{0,16},{16,32},{32,48},{48,64},{64,80},{80,96},{96,112},{112,128},... | collective-permute-start | bytes 221192 | tf_op jit(solution)/shard_map/ppermute | solution.py:18
  48.1 7.3 %copy-start.1 = (f32[6,3,4,8,1]{4,0,3,2,1:T(8,128)S(1)}, f32[6,3,4,8,1]{4,0,3,2,1:T(8,128)}, u32[]{:S(2)}) copy-start(f32[6,3,4,8,1]{4,0,3,2,1:T(8,128)} %copy.83) | copy-start | bytes 6916
  55.6 5.4 %collective-permute-start.4 = (f32[6,3,1,8,128]{4,0,3,2,1:T(8,128)S(1)}, f32[6,3,1,8,128]{4,0,3,2,1:T(8,128)S(1)}, u32[]{:S(2)}, u32[]{:S(2)}) collective-permute-start(f32[6,3,1,8,128]{4,0,3,2,1:T(8,128)S(1)} %fusion.65), channel_id=1, source_target_pairs={{16,0},{32,16},{48,32},{64,48},{80,64},{96,80},{112,96},{128,112},... | collective-permute-start | bytes 221192 | tf_op jit(solution)/shard_map/ppermute | solution.py:18
  61.1 8.8 %collective-permute-start.5 = (f32[6,3,5,1,128]{4,0,3,2,1:T(8,128)S(1)}, f32[6,3,5,1,128]{4,0,3,2,1:T(8,128)S(1)}, u32[]{:S(2)}, u32[]{:S(2)}) collective-permute-start(f32[6,3,5,1,128]{4,0,3,2,1:T(8,128)S(1)} %pad_maximum_fusion.7), channel_id=1, source_target_pairs={{1,0},{2,1},{3,2},{4,3},{5,4},{6,5},{7,6},{8,7},{9,8},{10,9},{11,1... | collective-permute-start | bytes 138248 | tf_op jit(solution)/shard_map/ppermute | solution.py:18
  77.3 3.8 %collective-permute-start.6 = (f32[6,3,5,1,128]{4,0,3,2,1:T(8,128)S(1)}, f32[6,3,5,1,128]{4,0,3,2,1:T(8,128)S(1)}, u32[]{:S(2)}, u32[]{:S(2)}) collective-permute-start(f32[6,3,5,1,128]{4,0,3,2,1:T(8,128)S(1)} %slice.450), channel_id=1, source_target_pairs={{0,1},{1,2},{2,3},{3,4},{4,5},{5,6},{6,7},{7,8},{8,9},{9,10},{10,1... | collective-permute-start | bytes 138248 | tf_op jit(solution)/shard_map/ppermute | solution.py:18
  81.2 7.9 %collective-permute-start.7 = (f32[6,3,1,8,128]{4,0,3,2,1:T(8,128)S(1)}, f32[6,3,1,8,128]{4,0,3,2,1:T(8,128)S(1)}, u32[]{:S(2)}, u32[]{:S(2)}) collective-permute-start(f32[6,3,1,8,128]{4,0,3,2,1:T(8,128)S(1)} %pad_maximum_fusion.5), channel_id=1, source_target_pairs={{0,16},{16,32},{32,48},{48,64},{64,80},{80,96},{96,112},{112,128},... | collective-permute-start | bytes 221192 | tf_op jit(solution)/shard_map/ppermute | solution.py:18
  90.2 4.1 %collective-permute-start.8 = (f32[5,6,6]{2,1,0:T(8,128)S(1)}, f32[5,6,6]{2,1,0:T(8,128)S(1)}, u32[]{:S(2)}, u32[]{:S(2)}) collective-permute-start(f32[5,6,6]{2,1,0:T(8,128)S(1)} %constant_dynamic-update-slice_fusion.1), channel_id=1, source_target_pairs={{0,1},{1,0},{2,3},{3,2},{4,5},{5,4},{6,7},{7,6},{8,9},{9,8},{10,11... | collective-permute-start | bytes 2168 | tf_op jit(solution)/shard_map/ppermute | solution.py:153
  94.3 4.5 %collective-permute-start.9 = (f32[5,6,6]{2,1,0:T(8,128)S(1)}, f32[5,6,6]{2,1,0:T(8,128)S(1)}, u32[]{:S(2)}, u32[]{:S(2)}) collective-permute-start(f32[5,6,6]{2,1,0:T(8,128)S(1)} %add.256), channel_id=1, source_target_pairs={{0,2},{1,3},{2,0},{3,1},{4,6},{5,7},{6,4},{7,5},{8,10},{9,11},{10,... | collective-permute-start | bytes 2168 | tf_op jit(solution)/shard_map/ppermute | solution.py:153
  98.8 5.4 %collective-permute-start.10 = (f32[5,6,6]{2,1,0:T(8,128)S(1)}, f32[5,6,6]{2,1,0:T(8,128)S(1)}, u32[]{:S(2)}, u32[]{:S(2)}) collective-permute-start(f32[5,6,6]{2,1,0:T(8,128)S(1)} %add.257), channel_id=1, source_target_pairs={{0,4},{1,5},{2,6},{3,7},{4,0},{5,1},{6,2},{7,3},{8,12},{9,13},{10,... | collective-permute-start | bytes 2168 | tf_op jit(solution)/shard_map/ppermute | solution.py:153
  104.2 8.4 %collective-permute-start.11 = (f32[5,6,6]{2,1,0:T(8,128)S(1)}, f32[5,6,6]{2,1,0:T(8,128)S(1)}, u32[]{:S(2)}, u32[]{:S(2)}) collective-permute-start(f32[5,6,6]{2,1,0:T(8,128)S(1)} %add.258), channel_id=1, source_target_pairs={{0,8},{1,9},{2,10},{3,11},{4,12},{5,13},{6,14},{7,15},{8,0},{9,1},... | collective-permute-start | bytes 2168 | tf_op jit(solution)/shard_map/ppermute | solution.py:153
  112.6 4.5 %collective-permute-start.12 = (f32[5,6,6]{2,1,0:T(8,128)S(1)}, f32[5,6,6]{2,1,0:T(8,128)S(1)}, u32[]{:S(2)}, u32[]{:S(2)}) collective-permute-start(f32[5,6,6]{2,1,0:T(8,128)S(1)} %add.259), channel_id=1, source_target_pairs={{0,16},{16,0},{32,48},{48,32},{64,80},{80,64},{96,112},{112,96},{1... | collective-permute-start | bytes 2168 | tf_op jit(solution)/shard_map/ppermute | solution.py:153
  117.2 5.4 %collective-permute-start.13 = (f32[5,6,6]{2,1,0:T(8,128)S(1)}, f32[5,6,6]{2,1,0:T(8,128)S(1)}, u32[]{:S(2)}, u32[]{:S(2)}) collective-permute-start(f32[5,6,6]{2,1,0:T(8,128)S(1)} %add.260), channel_id=1, source_target_pairs={{0,32},{16,48},{32,0},{48,16},{64,96},{80,112},{96,64},{112,80},{1... | collective-permute-start | bytes 2168 | tf_op jit(solution)/shard_map/ppermute | solution.py:153
  122.6 8.4 %collective-permute-start.14 = (f32[5,6,6]{2,1,0:T(8,128)S(1)}, f32[5,6,6]{2,1,0:T(8,128)S(1)}, u32[]{:S(2)}, u32[]{:S(2)}) collective-permute-start(f32[5,6,6]{2,1,0:T(8,128)S(1)} %add.261), channel_id=1, source_target_pairs={{0,64},{16,80},{32,96},{48,112},{64,0},{80,16},{96,32},{112,48},{1... | collective-permute-start | bytes 2168 | tf_op jit(solution)/shard_map/ppermute | solution.py:153
  131.0 4.5 %collective-permute-start.15 = (f32[5,6,6]{2,1,0:T(8,128)S(1)}, f32[5,6,6]{2,1,0:T(8,128)S(1)}, u32[]{:S(2)}, u32[]{:S(2)}) collective-permute-start(f32[5,6,6]{2,1,0:T(8,128)S(1)} %add.262), channel_id=1, source_target_pairs={{0,128},{16,144},{32,160},{48,176},{64,192},{80,208},{96,224},{112... | collective-permute-start | bytes 2168 | tf_op jit(solution)/shard_map/ppermute | solution.py:153
  135.5 6.0 %collective-permute-start.16 = (f32[5,6,6]{2,1,0:T(8,128)S(1)}, f32[5,6,6]{2,1,0:T(8,128)S(1)}, u32[]{:S(2)}, u32[]{:S(2)}) collective-permute-start(f32[5,6,6]{2,1,0:T(8,128)S(1)} %add.263), channel_id=1, source_target_pairs={{0,256},{16,272},{32,288},{48,304},{64,320},{80,336},{96,352},{112... | collective-permute-start | bytes 2168 | tf_op jit(solution)/shard_map/ppermute | solution.py:153
  147.3 12.9 %copy-start = (f32[6,3,4,8,128]{4,3,2,1,0:T(8,128)S(1)}, f32[6,3,4,8,128]{4,3,2,1,0:T(8,128)}, u32[]{:S(2)}) copy-start(f32[6,3,4,8,128]{4,3,2,1,0:T(8,128)} %param.9) | copy-start | bytes 884740
  147.7 34.5 %copy-start.3 = (f32[4,8,128]{2,1,0:T(8,128)S(1)}, f32[4,8,128]{2,1,0:T(8,128)}, u32[]{:S(2)}) copy-start(f32[4,8,128]{2,1,0:T(8,128)} %param.11) | copy-start | bytes 49156
  152.7 8.1 %collective-permute-start.17 = (f32[4,8,128]{2,1,0:T(8,128)S(1)}, f32[4,8,128]{2,1,0:T(8,128)S(1)}, u32[]{:S(2)}, u32[]{:S(2)}) collective-permute-start(f32[4,8,128]{2,1,0:T(8,128)S(1)} %mul.262), channel_id=1, source_target_pairs={{0,16},{16,32},{32,48},{48,64},{64,80},{80,96},{96,112},{112,128},... | collective-permute-start | bytes 49160 | tf_op jit(solution)/shard_map/ppermute | solution.py:29
  155.2 5.8 %collective-permute-start.18 = (f32[4,8,128]{2,1,0:T(8,128)S(1)}, f32[4,8,128]{2,1,0:T(8,128)S(1)}, u32[]{:S(2)}, u32[]{:S(2)}) collective-permute-start(f32[4,8,128]{2,1,0:T(8,128)S(1)} %mul.262), channel_id=1, source_target_pairs={{16,0},{32,16},{48,32},{64,48},{80,64},{96,80},{112,96},{128,112},... | collective-permute-start | bytes 49160 | tf_op jit(solution)/shard_map/ppermute | solution.py:31
  161.0 20.2 %collective-permute-start.19 = (f32[4,4,128]{2,1,0:T(4,128)S(1)}, f32[4,4,128]{2,1,0:T(4,128)S(1)}, u32[]{:S(2)}, u32[]{:S(2)}) collective-permute-start(f32[4,4,128]{2,1,0:T(4,128)S(1)} %get-tuple-element.38), channel_id=1, source_target_pairs={{0,1},{1,2},{2,3},{3,4},{4,5},{5,6},{6,7},{7,8},{8,9},{9,10},{10,1... | collective-permute-start | bytes 24584 | tf_op jit(solution)/shard_map/ppermute | solution.py:29
  175.9 6.2 %collective-permute-start.20 = (f32[4,4,128]{2,1,0:T(4,128)S(1)}, f32[4,4,128]{2,1,0:T(4,128)S(1)}, u32[]{:S(2)}, u32[]{:S(2)}) collective-permute-start(f32[4,4,128]{2,1,0:T(4,128)S(1)} %get-tuple-element.39), channel_id=1, source_target_pairs={{1,0},{2,1},{3,2},{4,3},{5,4},{6,5},{7,6},{8,7},{9,8},{10,9},{11,1... | collective-permute-start | bytes 24584 | tf_op jit(solution)/shard_map/ppermute | solution.py:31
where the time goes:
time: 184 us; the launch traced here: 183 us
  starting transfers between devices  74.1 us (40%)
  waiting for transfers between devices  49.8 us (27%)
  matrix products  21.4 us (12%)
  local copies, waits for them, and re-layouts  18.7 us (10%)
  other arithmetic  15.8 us (9%)
  between operations  3.12 us (2%)
    ppermute x9, waiting for transfers between devices, tree_sum(): lax.ppermute(value, axis, [(i, i ^ step) for i in range(count)])  29.1 us
    ppermute x8, starting transfers between devices, from_behind(): return lax.ppermute(block, axis, route)  27.7 us
    ppermute x9, starting transfers between devices, tree_sum(): lax.ppermute(value, axis, [(i, i ^ step) for i in range(count)])  22.2 us
    ppermute x8, waiting for transfers between devices, from_behind(): return lax.ppermute(block, axis, route)  19.8 us
    ppermute x2, starting transfers between devices, with_halo(): lax.ppermute(tail, axis, [(i, (i + 1) % count) for i in range(ends)])  17.4 us
    dot_general x2, matrix products, element_forces(): jnp.einsum('ij,cjabd->ciabd', stiffness, local_disp, precision=highest)  11.3 us
    unnamed x35, local copies, waits for them, and re-layouts  8.6 us
    ppermute x2, starting transfers between devices, with_halo(): lax.ppermute(head, axis, [((i + 1) % count, i) for i in range(ends)])  6.85 us
  transfers between devices with their start and end apart: 21, of which 17 were waited for; matrix products, arithmetic and copies ran while one was open for 8% of the time, Pallas kernels for 0%

commit v1 on v0

--- a/solution.py
+++ b/solution.py
@@ -207,6 +207,35 @@
     return jnp.concatenate([kept[:, :, :1] + to_x, kept[:, :, 1:]], axis=2)
 
 
+def halo_both(cells, axis, dim, width):
+    count = lax.axis_size(axis)
+    head = lax.slice_in_dim(cells, 0, width, axis=dim)
+    tail = lax.slice_in_dim(cells, cells.shape[dim] - width, cells.shape[dim], axis=dim)
+    below = lax.ppermute(tail, axis, [(i, i + 1) for i in range(count - 1)])
+    above = lax.ppermute(head, axis, [(i + 1, i) for i in range(count - 1)])
+    return jnp.concatenate([below, cells, above], axis=dim)
+
+
+def inside_mask(axis, extent, width, total):
+    places = np.arange(extent + 2 * width) - width
+    own = jnp.asarray(places, jnp.int32) + lax.axis_index(axis) * extent
+    return ((own >= 0) & (own < total)).astype(jnp.float32)
+
+
+def node_forces(node_field, modulus, stiffness):
+    local_disp = cases_disp(node_field)
+    local_load = jnp.einsum("ij,cjabd->ciabd", stiffness, local_disp, precision=highest)
+    local_force = (local_load * modulus).reshape((node_field.shape[0], 8, 3) + modulus.shape)
+    summed = jnp.zeros_like(node_field)
+    for corner in range(8):
+        off_x, off_y, off_z = (corner // 4, corner // 2 % 2, corner % 2)
+        summed = summed + jnp.pad(
+            local_force[:, corner],
+            ((0, 0), (0, 0), (off_x, 1 - off_x), (off_y, 1 - off_y), (off_z, 1 - off_z)),
+        )
+    return summed[..., :-1], local_disp, local_load
+
+
 def on_device(start_disp, bone_mask, density, load_nodes, load_forces):
     stiffness = jnp.asarray(hex_stiffness(), jnp.float32)
     modulus = bone_mask.astype(jnp.float32) * density * density
@@ -214,22 +243,49 @@
     size_x = start_disp.shape[2]
     size_y = start_disp.shape[3]
     size_z = start_disp.shape[4]
-
-    def apply_operator(field):
-        node_field = pad_upper_z(gather_upper(field))
-        forces = element_forces(node_field, modulus, stiffness)
-        return return_lower(forces[..., :-1]) + spring * field, node_field
+    count_x = lax.axis_size("gx")
+    count_y = lax.axis_size("gy")
+    fields = case_count * 3
 
     slot_ids = jnp.arange(size_x * size_y, dtype=jnp.int32)
     matches = (load_nodes[0, 0][:, :, None] == slot_ids).astype(jnp.float32)
     top_plane = jnp.einsum("cls,ckl->cks", matches, load_forces[0, 0], precision=highest).reshape(
-        case_count, 3, size_x, size_y
-    )
-    applied, start_nodes = apply_operator(start_disp)
-    residual = jnp.concatenate(
-        [-applied[..., :-1], (top_plane - applied[..., -1])[..., None]], axis=4
-    )
-    applied, residual_nodes = apply_operator(residual)
+        fields, size_x, size_y
+    )
+    packed_loads = jnp.pad(top_plane.transpose(1, 2, 0), ((0, 0), (0, 0), (0, size_z - fields)))
+    packed = jnp.concatenate(
+        [start_disp.reshape(fields, size_x, size_y, size_z), modulus[None], packed_loads[None]],
+        axis=0,
+    )
+    packed = halo_both(halo_both(packed, "gx", 1, 2), "gy", 2, 2)
+    wide_start = packed[:fields].reshape(case_count, 3, size_x + 4, size_y + 4, size_z)
+    wide_modulus = packed[fields]
+    wide_loads = packed[fields + 1, 1:-1, 1:-1, :fields].transpose(2, 0, 1)
+    wide_loads = wide_loads.reshape(case_count, 3, size_x + 2, size_y + 2)
+
+    start_nodes = pad_upper_z(wide_start)
+    forces, start_elems, start_loads = node_forces(
+        start_nodes, wide_modulus[:-1, :-1], stiffness
+    )
+    applied = forces[:, :, 1:-1, 1:-1] + spring * wide_start[:, :, 1:-1, 1:-1]
+    keep = (
+        inside_mask("gx", size_x, 1, size_x * count_x)[:, None, None]
+        * inside_mask("gy", size_y, 1, size_y * count_y)[None, :, None]
+    )
+    residual_wide = (
+        jnp.concatenate(
+            [-applied[..., :-1], (wide_loads - applied[..., -1])[..., None]], axis=4
+        )
+        * keep
+    )
+
+    residual_nodes = pad_upper_z(residual_wide)
+    forces, residual_elems, residual_loads = node_forces(
+        residual_nodes, wide_modulus[1:-2, 1:-2], stiffness
+    )
+    residual = residual_wide[:, :, 1:-1, 1:-1]
+    applied = forces[:, :, 1:-1, 1:-1] + spring * residual
+
     blur_mass = modulus
     for dim, axis in ((0, "gx"), (1, "gy"), (2, None)):
         extent = modulus.shape[dim]
@@ -245,12 +301,10 @@
         shape = [1, 1, 1]
         shape[dim] = extent
         blur_mass = blur_mass * kept.reshape(shape)
-    start_elems = cases_disp(start_nodes)
-    start_loads = jnp.einsum("ij,cjabd->ciabd", stiffness, start_elems, precision=highest)
-    residual_elems = cases_disp(residual_nodes)
-    residual_loads = jnp.einsum(
-        "ij,cjabd->ciabd", stiffness, residual_elems, precision=highest
-    )
+    start_elems = start_elems[:, :, 2:-1, 2:-1]
+    start_loads = start_loads[:, :, 2:-1, 2:-1]
+    residual_elems = residual_elems[:, :, 1:, 1:]
+    residual_loads = residual_loads[:, :, 1:, 1:]
     start_energy = jnp.sum(start_elems * start_loads * blur_mass, axis=(1, 2, 3, 4))
     start_weighted = start_loads * blur_mass
     residual_weighted = residual_loads * blur_mass
@@ -279,13 +333,15 @@
         + jnp.sum(step_alpha[:, None, :] * grams[3][:, :, None] * step_alpha[None, :, :])
     )
     solution = start_disp + mix_cases(residual, step_alpha)
-    node_field = start_nodes + mix_cases(residual_nodes, step_alpha)
+    node_field = start_nodes[:, :, 2:-1, 2:-1] + mix_cases(
+        residual_nodes[:, :, 1:, 1:], step_alpha
+    )
     energy = element_energy(node_field, stiffness)
     stimulus = modulus * energy
     smooth = blur_valid(with_halo(stimulus, (("gx", 0),), 4), 0, size_x)
     smooth = blur_valid(with_halo(smooth, (("gy", 1),), 4), 1, size_y)
     smooth = blur_valid(jnp.pad(smooth, ((0, 0), (0, 0), (4, 4))), 2, size_z)
-    mean_stim = summed / (size_x * size_y * size_z * lax.axis_size("gx") * lax.axis_size("gy"))
+    mean_stim = summed / (size_x * size_y * size_z * count_x * count_y)
     new_density = jnp.minimum(density * (0.5 + 0.5 * smooth / (mean_stim + mean_eps)), density_cap)
     return (solution, new_density)
 

time: 184 us -> 161 us (0.88)
  the two profiles are of different devices: /device:TPU:31 before, /device:TPU:23 now
where the time goes in v1:
time: 161 us; the launch traced here: 160 us
  starting transfers between devices  71.4 us (44%)
  waiting for transfers between devices  34.7 us (22%)
  matrix products  21.3 us (13%)
  local copies, waits for them, and re-layouts  15.4 us (10%)
  other arithmetic  14.3 us (9%)
  between operations  3.14 us (2%)
    ppermute x9, starting transfers between devices, tree_sum(): lax.ppermute(value, axis, [(i, i ^ step) for i in range(count)])  28.3 us
    ppermute x9, waiting for transfers between devices, tree_sum(): lax.ppermute(value, axis, [(i, i ^ step) for i in range(count)])  24.6 us
    ppermute x2, starting transfers between devices, with_halo(): lax.ppermute(tail, axis, [(i, (i + 1) % count) for i in range(ends)])  15.7 us
    ppermute x2, starting transfers between devices, halo_both(): above = lax.ppermute(head, axis, [(i + 1, i) for i in range(count - 1)])  10.8 us
    dot_general x2, matrix products, node_forces(): jnp.einsum('ij,cjabd->ciabd', stiffness, local_disp, precision=highest)  10.2 us
    ppermute x2, starting transfers between devices, halo_both(): below = lax.ppermute(tail, axis, [(i, i + 1) for i in range(count - 1)])  8.64 us
    ppermute x2, starting transfers between devices, with_halo(): lax.ppermute(head, axis, [((i + 1) % count, i) for i in range(ends)])  8.05 us
    ppermute x2, waiting for transfers between devices, halo_both(): above = lax.ppermute(head, axis, [(i + 1, i) for i in range(count - 1)])  5.26 us
  transfers between devices with their start and end apart: 17, of which 14 were waited for; matrix products, arithmetic and copies ran while one was open for 2% of the time, Pallas kernels for 0%

profile of v1, /device:TPU:23, one launch (start us, length us, event | category | flops | bytes accessed | tf_op | source)
XLA Modules:
  0.0 160.2 jit_solution(8892609685325438482)
XLA Ops:
  0.6 0.7 dynamic_slice.6
  2.8 0.9 convolution_bitcast_fusion.1
  3.8 0.8 multiply_multiply_fusion.1
  4.8 1.1 copy.138
  6.1 4.0 %collective-permute-start = (f32[20,2,8,128]{3,1,2,0:T(2,128)S(1)}, f32[20,2,8,128]{3,1,2,0:T(2,128)S(1)}, u32[]{:S(2)}, u32[]{:S(2)}) collective-permute-start(f32[20,2,8,128]{3,1,2,0:T(2,128)S(1)} %get-tuple-element.32), channel_id=1, source_target_pairs={{0,16},{16,32},{32,48},{48,64},{64,80},{80,96},{96,112},{112,128},... | collective-permute-start | bytes 491528 | tf_op jit(solution)/shard_map/ppermute | solution.py:214
  10.1 8.9 %collective-permute-start.1 = (f32[20,2,8,128]{3,1,2,0:T(2,128)S(1)}, f32[20,2,8,128]{3,1,2,0:T(2,128)S(1)}, u32[]{:S(2)}, u32[]{:S(2)}) collective-permute-start(f32[20,2,8,128]{3,1,2,0:T(2,128)S(1)} %get-tuple-element.33), channel_id=1, source_target_pairs={{16,0},{32,16},{48,32},{64,48},{80,64},{96,80},{112,96},{128,112},... | collective-permute-start | bytes 491528 | tf_op jit(solution)/shard_map/ppermute | solution.py:215
  20.9 0.9 collective-permute-done.1
  21.9 4.6 %collective-permute-start.2 = (f32[20,8,2,128]{3,1,2,0:T(8,128)S(1)}, f32[20,8,2,128]{3,1,2,0:T(8,128)S(1)}, u32[]{:S(2)}, u32[]{:S(2)}) collective-permute-start(f32[20,8,2,128]{3,1,2,0:T(8,128)S(1)} %get-tuple-element.30), channel_id=1, source_target_pairs={{0,1},{1,2},{2,3},{3,4},{4,5},{5,6},{6,7},{7,8},{8,9},{9,10},{10,1... | collective-permute-start | bytes 491528 | tf_op jit(solution)/shard_map/ppermute | solution.py:214
  26.6 1.9 %collective-permute-start.3 = (f32[20,8,2,128]{3,1,2,0:T(8,128)S(1)}, f32[20,8,2,128]{3,1,2,0:T(8,128)S(1)}, u32[]{:S(2)}, u32[]{:S(2)}) collective-permute-start(f32[20,8,2,128]{3,1,2,0:T(8,128)S(1)} %get-tuple-element.31), channel_id=1, source_target_pairs={{1,0},{2,1},{3,2},{4,3},{5,4},{6,5},{7,6},{8,7},{9,8},{10,9},{11,1... | collective-permute-start | bytes 491528 | tf_op jit(solution)/shard_map/ppermute | solution.py:215
  28.8 4.4 %collective-permute-done.3 = f32[20,8,2,128]{3,1,2,0:T(8,128)S(1)} collective-permute-done((f32[20,8,2,128]{3,1,2,0:T(8,128)S(1)}, f32[20,8,2,128]{3,1,2,0:T(8,128)S(1)}, u32[]{:S(2)}, u32[]{:S(2)}) %collective-permute-start.3) | collective-permute-done | bytes 163872 | tf_op jit(solution)/shard_map/ppermute | solution.py:215
  34.2 1.0 copy.160
  36.8 1.1 copy.147
  37.9 7.0 %broadcast_multiply_fusion = (f32[6,24,7,11,128]{4,1,3,2,0:T(8,128)S(1)}, f32[6,24,7,11,128]{4,1,3,2,0:T(8,128)}) fusion(f32[7,11,128]{2,1,0:T(8,128)S(1)} %copy.148, f32[6,24,7,11,128]{4,1,3,2,0:T(8,128)S(1)} %copy.147, f32[24,24,1,1,1]{1,0,4,3,2:T(8,128)S(1)} %copy-done.2), kind=kOutput, calls=%fused_computation.9 | convolution fusion | flops 410167296 | bytes 17072896 | tf_op jit(solution)/shard_map/ij,cjabd->ciabd/dot_general | solution.py:227
  44.9 1.5 copy.189
  46.8 0.9 fusion.33
  48.4 1.0 fusion.13
  51.3 3.2 %broadcast_multiply_fusion.1 = (f32[6,24,5,9,128]{4,1,3,2,0:T(8,128)S(1)}, f32[6,24,5,9,128]{4,1,3,2,0:T(8,128)S(1)}) fusion(f32[5,9,128]{2,1,0:T(8,128)S(1)} %copy.162, f32[24,24,1,1,1]{1,0,4,3,2:T(8,128)S(1)} %copy-done.2, f32[6,24,5,9,128]{4,0,3,2,1:T(8,128)S(1)} %bitcast.242), kind=kOutput, calls=%fused_computation.28 | convolution fusion | flops 239708160 | bytes 9978624 | tf_op jit(solution)/shard_map/ij,cjabd->ciabd/dot_general | solution.py:227
  54.5 0.9 copy.200
  55.7 2.6 %fusion.3 = (f32[6]{0:T(128)S(1)}, f32[6,24,4,8,128]{4,1,3,2,0:T(8,128)S(1)}, f32[6,24,4,8,128]{4,1,3,2,0:T(8,128)S(1)}) fusion(f32[6,24,7,11,128]{4,1,3,2,0:T(8,128)S(1)} %copy.147, f32[6,24,7,11,128]{4,1,3,2,0:T(8,128)} %get-tuple-element.43, f32[4,8,128]{2,1,0:T(8,128)S(1)} %get-tuple-element.34, f32[6,24,5,9,128]{4,1,3,2,0:T(8,128)S(1)} %get-tuple-element.45), kind=kLoop, calls=%fused_computation.18 | loop fusion | flops 2949114 | bytes 11812888 | tf_op jit(solution)/shard_map/reduce_sum | solution.py:308
  59.2 2.9 %multiply_reduce_fusion = (f32[6,6]{1,0:T(8,128)S(1)}, f32[6,6]{1,0:T(8,128)S(1)}) fusion(f32[6,24,4,8,128]{4,3,2,1,0:T(8,128)S(1)} %copy.173, f32[6,24,4,8,128]{4,3,2,1,0:T(8,128)S(1)} %copy.171, f32[6,24,4,8,128]{4,3,2,1,0:T(8,128)S(1)} %copy.172), kind=kLoop, calls=%fused_computation | loop fusion | flops 14155704 | bytes 7078176 | tf_op jit(solution)/shard_map/reduce_sum | solution.py:314
  62.1 1.2 fusion.12
  63.3 1.9 %collective-permute-start.4 = (f32[5,6,6]{2,1,0:T(8,128)S(1)}, f32[5,6,6]{2,1,0:T(8,128)S(1)}, u32[]{:S(2)}, u32[]{:S(2)}) collective-permute-start(f32[5,6,6]{2,1,0:T(8,128)S(1)} %constant_dynamic-update-slice_fusion), channel_id=1, source_target_pairs={{0,1},{1,0},{2,3},{3,2},{4,5},{5,4},{6,7},{7,6},{8,9},{9,8},{10,11... | collective-permute-start | bytes 2168 | tf_op jit(solution)/shard_map/ppermute | solution.py:153
  65.3 1.2 collective-permute-done.4
  66.4 5.6 %collective-permute-start.5 = (f32[5,6,6]{2,1,0:T(8,128)S(1)}, f32[5,6,6]{2,1,0:T(8,128)S(1)}, u32[]{:S(2)}, u32[]{:S(2)}) collective-permute-start(f32[5,6,6]{2,1,0:T(8,128)S(1)} %add.258), channel_id=1, source_target_pairs={{0,2},{1,3},{2,0},{3,1},{4,6},{5,7},{6,4},{7,5},{8,10},{9,11},{10,... | collective-permute-start | bytes 2168 | tf_op jit(solution)/shard_map/ppermute | solution.py:153
  72.0 1.2 collective-permute-done.5
  73.2 1.9 %collective-permute-start.6 = (f32[5,6,6]{2,1,0:T(8,128)S(1)}, f32[5,6,6]{2,1,0:T(8,128)S(1)}, u32[]{:S(2)}, u32[]{:S(2)}) collective-permute-start(f32[5,6,6]{2,1,0:T(8,128)S(1)} %add.259), channel_id=1, source_target_pairs={{0,4},{1,5},{2,6},{3,7},{4,0},{5,1},{6,2},{7,3},{8,12},{9,13},{10,... | collective-permute-start | bytes 2168 | tf_op jit(solution)/shard_map/ppermute | solution.py:153
  75.1 3.5 %collective-permute-done.6 = f32[5,6,6]{2,1,0:T(8,128)S(1)} collective-permute-done((f32[5,6,6]{2,1,0:T(8,128)S(1)}, f32[5,6,6]{2,1,0:T(8,128)S(1)}, u32[]{:S(2)}, u32[]{:S(2)}) %collective-permute-start.6) | collective-permute-done | bytes 752 | tf_op jit(solution)/shard_map/ppermute | solution.py:153
  78.6 2.5 %collective-permute-start.7 = (f32[5,6,6]{2,1,0:T(8,128)S(1)}, f32[5,6,6]{2,1,0:T(8,128)S(1)}, u32[]{:S(2)}, u32[]{:S(2)}) collective-permute-start(f32[5,6,6]{2,1,0:T(8,128)S(1)} %add.260), channel_id=1, source_target_pairs={{0,8},{1,9},{2,10},{3,11},{4,12},{5,13},{6,14},{7,15},{8,0},{9,1},... | collective-permute-start | bytes 2168 | tf_op jit(solution)/shard_map/ppermute | solution.py:153
  81.1 5.9 %collective-permute-done.7 = f32[5,6,6]{2,1,0:T(8,128)S(1)} collective-permute-done((f32[5,6,6]{2,1,0:T(8,128)S(1)}, f32[5,6,6]{2,1,0:T(8,128)S(1)}, u32[]{:S(2)}, u32[]{:S(2)}) %collective-permute-start.7) | collective-permute-done | bytes 752 | tf_op jit(solution)/shard_map/ppermute | solution.py:153
  87.0 1.9 %collective-permute-start.8 = (f32[5,6,6]{2,1,0:T(8,128)S(1)}, f32[5,6,6]{2,1,0:T(8,128)S(1)}, u32[]{:S(2)}, u32[]{:S(2)}) collective-permute-start(f32[5,6,6]{2,1,0:T(8,128)S(1)} %add.261), channel_id=1, source_target_pairs={{0,16},{16,0},{32,48},{48,32},{64,80},{80,64},{96,112},{112,96},{1... | collective-permute-start | bytes 2168 | tf_op jit(solution)/shard_map/ppermute | solution.py:153
  89.0 2.6 %collective-permute-done.8 = f32[5,6,6]{2,1,0:T(8,128)S(1)} collective-permute-done((f32[5,6,6]{2,1,0:T(8,128)S(1)}, f32[5,6,6]{2,1,0:T(8,128)S(1)}, u32[]{:S(2)}, u32[]{:S(2)}) %collective-permute-start.8) | collective-permute-done | bytes 752 | tf_op jit(solution)/shard_map/ppermute | solution.py:153
  91.6 4.1 %collective-permute-start.9 = (f32[5,6,6]{2,1,0:T(8,128)S(1)}, f32[5,6,6]{2,1,0:T(8,128)S(1)}, u32[]{:S(2)}, u32[]{:S(2)}) collective-permute-start(f32[5,6,6]{2,1,0:T(8,128)S(1)} %add.262), channel_id=1, source_target_pairs={{0,32},{16,48},{32,0},{48,16},{64,96},{80,112},{96,64},{112,80},{1... | collective-permute-start | bytes 2168 | tf_op jit(solution)/shard_map/ppermute | solution.py:153
  95.7 1.3 collective-permute-done.9
  97.0 5.0 %collective-permute-start.10 = (f32[5,6,6]{2,1,0:T(8,128)S(1)}, f32[5,6,6]{2,1,0:T(8,128)S(1)}, u32[]{:S(2)}, u32[]{:S(2)}) collective-permute-start(f32[5,6,6]{2,1,0:T(8,128)S(1)} %add.263), channel_id=1, source_target_pairs={{0,64},{16,80},{32,96},{48,112},{64,0},{80,16},{96,32},{112,48},{1... | collective-permute-start | bytes 2168 | tf_op jit(solution)/shard_map/ppermute | solution.py:153
  102.0 3.4 %collective-permute-done.10 = f32[5,6,6]{2,1,0:T(8,128)S(1)} collective-permute-done((f32[5,6,6]{2,1,0:T(8,128)S(1)}, f32[5,6,6]{2,1,0:T(8,128)S(1)}, u32[]{:S(2)}, u32[]{:S(2)}) %collective-permute-start.10) | collective-permute-done | bytes 752 | tf_op jit(solution)/shard_map/ppermute | solution.py:153
  105.4 2.4 %collective-permute-start.11 = (f32[5,6,6]{2,1,0:T(8,128)S(1)}, f32[5,6,6]{2,1,0:T(8,128)S(1)}, u32[]{:S(2)}, u32[]{:S(2)}) collective-permute-start(f32[5,6,6]{2,1,0:T(8,128)S(1)} %add.264), channel_id=1, source_target_pairs={{0,128},{16,144},{32,160},{48,176},{64,192},{80,208},{96,224},{112... | collective-permute-start | bytes 2168 | tf_op jit(solution)/shard_map/ppermute | solution.py:153
  107.8 2.4 %collective-permute-done.11 = f32[5,6,6]{2,1,0:T(8,128)S(1)} collective-permute-done((f32[5,6,6]{2,1,0:T(8,128)S(1)}, f32[5,6,6]{2,1,0:T(8,128)S(1)}, u32[]{:S(2)}, u32[]{:S(2)}) %collective-permute-start.11) | collective-permute-done | bytes 752 | tf_op jit(solution)/shard_map/ppermute | solution.py:153
  110.2 3.0 %collective-permute-start.12 = (f32[5,6,6]{2,1,0:T(8,128)S(1)}, f32[5,6,6]{2,1,0:T(8,128)S(1)}, u32[]{:S(2)}, u32[]{:S(2)}) collective-permute-start(f32[5,6,6]{2,1,0:T(8,128)S(1)} %add.265), channel_id=1, source_target_pairs={{0,256},{16,272},{32,288},{48,304},{64,320},{80,336},{96,352},{112... | collective-permute-start | bytes 2168 | tf_op jit(solution)/shard_map/ppermute | solution.py:153
  113.2 3.1 %collective-permute-done.12 = f32[5,6,6]{2,1,0:T(8,128)S(1)} collective-permute-done((f32[5,6,6]{2,1,0:T(8,128)S(1)}, f32[5,6,6]{2,1,0:T(8,128)S(1)}, u32[]{:S(2)}, u32[]{:S(2)}) %collective-permute-start.12) | collective-permute-done | bytes 752 | tf_op jit(solution)/shard_map/ppermute | solution.py:153
  119.6 0.8 fusion.137
  120.4 1.2 convolution_add_fusion
  122.5 5.0 %fusion.4 = f32[4,8,128]{2,1,0:T(8,128)S(1)} fusion(f32[6,24,4,8,128]{4,0,3,2,1:T(8,128)S(1)} %bitcast.250, f32[24,24,1,1,1]{1,0,4,3,2:T(8,128)S(1)} %copy-done.2), kind=kOutput, calls=%fused_computation.21 | convolution fusion | flops 171044864 | bytes 2377984 | tf_op jit(solution)/shard_map/ij,cjabd->ciabd/dot_general | solution.py:137
  127.6 6.1 %collective-permute-start.14 = (f32[4,8,128]{2,1,0:T(8,128)S(1)}, f32[4,8,128]{2,1,0:T(8,128)S(1)}, u32[]{:S(2)}, u32[]{:S(2)}) collective-permute-start(f32[4,8,128]{2,1,0:T(8,128)S(1)} %fusion.148), channel_id=1, source_target_pairs={{16,0},{32,16},{48,32},{64,48},{80,64},{96,80},{112,96},{128,112},... | collective-permute-start | bytes 49160 | tf_op jit(solution)/shard_map/ppermute | solution.py:31
  133.8 1.9 %collective-permute-start.13 = (f32[4,8,128]{2,1,0:T(8,128)S(1)}, f32[4,8,128]{2,1,0:T(8,128)S(1)}, u32[]{:S(2)}, u32[]{:S(2)}) collective-permute-start(f32[4,8,128]{2,1,0:T(8,128)S(1)} %fusion.148), channel_id=1, source_target_pairs={{0,16},{16,32},{32,48},{48,64},{64,80},{80,96},{96,112},{112,128},... | collective-permute-start | bytes 49160 | tf_op jit(solution)/shard_map/ppermute | solution.py:29
  136.4 3.9 %collective-permute-done.13 = f32[4,8,128]{2,1,0:T(8,128)S(1)} collective-permute-done((f32[4,8,128]{2,1,0:T(8,128)S(1)}, f32[4,8,128]{2,1,0:T(8,128)S(1)}, u32[]{:S(2)}, u32[]{:S(2)}) %collective-permute-start.13) | collective-permute-done | bytes 16416 | tf_op jit(solution)/shard_map/ppermute | solution.py:29
  140.4 13.7 %collective-permute-start.15 = (f32[4,4,128]{2,1,0:T(4,128)S(1)}, f32[4,4,128]{2,1,0:T(4,128)S(1)}, u32[]{:S(2)}, u32[]{:S(2)}) collective-permute-start(f32[4,4,128]{2,1,0:T(4,128)S(1)} %get-tuple-element.39), channel_id=1, source_target_pairs={{0,1},{1,2},{2,3},{3,4},{4,5},{5,6},{6,7},{7,8},{8,9},{9,10},{10,1... | collective-permute-start | bytes 24584 | tf_op jit(solution)/shard_map/ppermute | solution.py:29
  154.1 1.9 %collective-permute-start.16 = (f32[4,4,128]{2,1,0:T(4,128)S(1)}, f32[4,4,128]{2,1,0:T(4,128)S(1)}, u32[]{:S(2)}, u32[]{:S(2)}) collective-permute-start(f32[4,4,128]{2,1,0:T(4,128)S(1)} %get-tuple-element.40), channel_id=1, source_target_pairs={{1,0},{2,1},{3,2},{4,3},{5,4},{6,5},{7,6},{8,7},{9,8},{10,9},{11,1... | collective-permute-start | bytes 24584 | tf_op jit(solution)/shard_map/ppermute | solution.py:31
  156.7 0.8 copy.182
  (96 shorter events, 17.2 us)
Async XLA Ops:
  6.1 14.9 %collective-permute-start = (f32[20,2,8,128]{3,1,2,0:T(2,128)S(1)}, f32[20,2,8,128]{3,1,2,0:T(2,128)S(1)}, u32[]{:S(2)}, u32[]{:S(2)}) collective-permute-start(f32[20,2,8,128]{3,1,2,0:T(2,128)S(1)} %get-tuple-element.32), channel_id=1, source_target_pairs={{0,16},{16,32},{32,48},{48,64},{64,80},{80,96},{96,112},{112,128},... | collective-permute-start | bytes 491528 | tf_op jit(solution)/shard_map/ppermute | solution.py:214
  10.1 11.7 %collective-permute-start.1 = (f32[20,2,8,128]{3,1,2,0:T(2,128)S(1)}, f32[20,2,8,128]{3,1,2,0:T(2,128)S(1)}, u32[]{:S(2)}, u32[]{:S(2)}) collective-permute-start(f32[20,2,8,128]{3,1,2,0:T(2,128)S(1)} %get-tuple-element.33), channel_id=1, source_target_pairs={{16,0},{32,16},{48,32},{64,48},{80,64},{96,80},{112,96},{128,112},... | collective-permute-start | bytes 491528 | tf_op jit(solution)/shard_map/ppermute | solution.py:215
  21.9 6.9 %collective-permute-start.2 = (f32[20,8,2,128]{3,1,2,0:T(8,128)S(1)}, f32[20,8,2,128]{3,1,2,0:T(8,128)S(1)}, u32[]{:S(2)}, u32[]{:S(2)}) collective-permute-start(f32[20,8,2,128]{3,1,2,0:T(8,128)S(1)} %get-tuple-element.30), channel_id=1, source_target_pairs={{0,1},{1,2},{2,3},{3,4},{4,5},{5,6},{6,7},{7,8},{8,9},{9,10},{10,1... | collective-permute-start | bytes 491528 | tf_op jit(solution)/shard_map/ppermute | solution.py:214
  26.6 6.6 %collective-permute-start.3 = (f32[20,8,2,128]{3,1,2,0:T(8,128)S(1)}, f32[20,8,2,128]{3,1,2,0:T(8,128)S(1)}, u32[]{:S(2)}, u32[]{:S(2)}) collective-permute-start(f32[20,8,2,128]{3,1,2,0:T(8,128)S(1)} %get-tuple-element.31), channel_id=1, source_target_pairs={{1,0},{2,1},{3,2},{4,3},{5,4},{6,5},{7,6},{8,7},{9,8},{10,9},{11,1... | collective-permute-start | bytes 491528 | tf_op jit(solution)/shard_map/ppermute | solution.py:215
  36.8 1.1 copy-start.2
  63.3 3.1 %collective-permute-start.4 = (f32[5,6,6]{2,1,0:T(8,128)S(1)}, f32[5,6,6]{2,1,0:T(8,128)S(1)}, u32[]{:S(2)}, u32[]{:S(2)}) collective-permute-start(f32[5,6,6]{2,1,0:T(8,128)S(1)} %constant_dynamic-update-slice_fusion), channel_id=1, source_target_pairs={{0,1},{1,0},{2,3},{3,2},{4,5},{5,4},{6,7},{7,6},{8,9},{9,8},{10,11... | collective-permute-start | bytes 2168 | tf_op jit(solution)/shard_map/ppermute | solution.py:153
  66.4 6.8 %collective-permute-start.5 = (f32[5,6,6]{2,1,0:T(8,128)S(1)}, f32[5,6,6]{2,1,0:T(8,128)S(1)}, u32[]{:S(2)}, u32[]{:S(2)}) collective-permute-start(f32[5,6,6]{2,1,0:T(8,128)S(1)} %add.258), channel_id=1, source_target_pairs={{0,2},{1,3},{2,0},{3,1},{4,6},{5,7},{6,4},{7,5},{8,10},{9,11},{10,... | collective-permute-start | bytes 2168 | tf_op jit(solution)/shard_map/ppermute | solution.py:153
  73.2 5.4 %collective-permute-start.6 = (f32[5,6,6]{2,1,0:T(8,128)S(1)}, f32[5,6,6]{2,1,0:T(8,128)S(1)}, u32[]{:S(2)}, u32[]{:S(2)}) collective-permute-start(f32[5,6,6]{2,1,0:T(8,128)S(1)} %add.259), channel_id=1, source_target_pairs={{0,4},{1,5},{2,6},{3,7},{4,0},{5,1},{6,2},{7,3},{8,12},{9,13},{10,... | collective-permute-start | bytes 2168 | tf_op jit(solution)/shard_map/ppermute | solution.py:153
  78.6 8.4 %collective-permute-start.7 = (f32[5,6,6]{2,1,0:T(8,128)S(1)}, f32[5,6,6]{2,1,0:T(8,128)S(1)}, u32[]{:S(2)}, u32[]{:S(2)}) collective-permute-start(f32[5,6,6]{2,1,0:T(8,128)S(1)} %add.260), channel_id=1, source_target_pairs={{0,8},{1,9},{2,10},{3,11},{4,12},{5,13},{6,14},{7,15},{8,0},{9,1},... | collective-permute-start | bytes 2168 | tf_op jit(solution)/shard_map/ppermute | solution.py:153
  87.0 4.5 %collective-permute-start.8 = (f32[5,6,6]{2,1,0:T(8,128)S(1)}, f32[5,6,6]{2,1,0:T(8,128)S(1)}, u32[]{:S(2)}, u32[]{:S(2)}) collective-permute-start(f32[5,6,6]{2,1,0:T(8,128)S(1)} %add.261), channel_id=1, source_target_pairs={{0,16},{16,0},{32,48},{48,32},{64,80},{80,64},{96,112},{112,96},{1... | collective-permute-start | bytes 2168 | tf_op jit(solution)/shard_map/ppermute | solution.py:153
  91.6 5.4 %collective-permute-start.9 = (f32[5,6,6]{2,1,0:T(8,128)S(1)}, f32[5,6,6]{2,1,0:T(8,128)S(1)}, u32[]{:S(2)}, u32[]{:S(2)}) collective-permute-start(f32[5,6,6]{2,1,0:T(8,128)S(1)} %add.262), channel_id=1, source_target_pairs={{0,32},{16,48},{32,0},{48,16},{64,96},{80,112},{96,64},{112,80},{1... | collective-permute-start | bytes 2168 | tf_op jit(solution)/shard_map/ppermute | solution.py:153
  97.0 8.4 %collective-permute-start.10 = (f32[5,6,6]{2,1,0:T(8,128)S(1)}, f32[5,6,6]{2,1,0:T(8,128)S(1)}, u32[]{:S(2)}, u32[]{:S(2)}) collective-permute-start(f32[5,6,6]{2,1,0:T(8,128)S(1)} %add.263), channel_id=1, source_target_pairs={{0,64},{16,80},{32,96},{48,112},{64,0},{80,16},{96,32},{112,48},{1... | collective-permute-start | bytes 2168 | tf_op jit(solution)/shard_map/ppermute | solution.py:153
  105.4 4.8 %collective-permute-start.11 = (f32[5,6,6]{2,1,0:T(8,128)S(1)}, f32[5,6,6]{2,1,0:T(8,128)S(1)}, u32[]{:S(2)}, u32[]{:S(2)}) collective-permute-start(f32[5,6,6]{2,1,0:T(8,128)S(1)} %add.264), channel_id=1, source_target_pairs={{0,128},{16,144},{32,160},{48,176},{64,192},{80,208},{96,224},{112... | collective-permute-start | bytes 2168 | tf_op jit(solution)/shard_map/ppermute | solution.py:153
  110.2 6.1 %collective-permute-start.12 = (f32[5,6,6]{2,1,0:T(8,128)S(1)}, f32[5,6,6]{2,1,0:T(8,128)S(1)}, u32[]{:S(2)}, u32[]{:S(2)}) collective-permute-start(f32[5,6,6]{2,1,0:T(8,128)S(1)} %add.265), channel_id=1, source_target_pairs={{0,256},{16,272},{32,288},{48,304},{64,320},{80,336},{96,352},{112... | collective-permute-start | bytes 2168 | tf_op jit(solution)/shard_map/ppermute | solution.py:153
  121.9 5.7 %copy-start.1 = (f32[4,8,128]{2,1,0:T(8,128)S(1)}, f32[4,8,128]{2,1,0:T(8,128)}, u32[]{:S(2)}) copy-start(f32[4,8,128]{2,1,0:T(8,128)} %param.13) | copy-start | bytes 49156
  121.9 5.7 %copy-start.3 = (s32[4,8,128]{2,1,0:T(8,128)S(1)}, s32[4,8,128]{2,1,0:T(8,128)}, u32[]{:S(2)}) copy-start(s32[4,8,128]{2,1,0:T(8,128)} %param.12) | copy-start | bytes 49156
  121.9 13.8 %copy-start = (f32[6,3,4,8,128]{4,3,2,1,0:T(8,128)S(1)}, f32[6,3,4,8,128]{4,3,2,1,0:T(8,128)}, u32[]{:S(2)}) copy-start(f32[6,3,4,8,128]{4,3,2,1,0:T(8,128)} %param.11) | copy-start | bytes 884740
  127.6 8.8 %collective-permute-start.14 = (f32[4,8,128]{2,1,0:T(8,128)S(1)}, f32[4,8,128]{2,1,0:T(8,128)S(1)}, u32[]{:S(2)}, u32[]{:S(2)}) collective-permute-start(f32[4,8,128]{2,1,0:T(8,128)S(1)} %fusion.148), channel_id=1, source_target_pairs={{16,0},{32,16},{48,32},{64,48},{80,64},{96,80},{112,96},{128,112},... | collective-permute-start | bytes 49160 | tf_op jit(solution)/shard_map/ppermute | solution.py:31
  133.8 6.6 %collective-permute-start.13 = (f32[4,8,128]{2,1,0:T(8,128)S(1)}, f32[4,8,128]{2,1,0:T(8,128)S(1)}, u32[]{:S(2)}, u32[]{:S(2)}) collective-permute-start(f32[4,8,128]{2,1,0:T(8,128)S(1)} %fusion.148), channel_id=1, source_target_pairs={{0,16},{16,32},{32,48},{48,64},{64,80},{80,96},{96,112},{112,128},... | collective-permute-start | bytes 49160 | tf_op jit(solution)/shard_map/ppermute | solution.py:29
  140.4 19.0 %collective-permute-start.15 = (f32[4,4,128]{2,1,0:T(4,128)S(1)}, f32[4,4,128]{2,1,0:T(4,128)S(1)}, u32[]{:S(2)}, u32[]{:S(2)}) collective-permute-start(f32[4,4,128]{2,1,0:T(4,128)S(1)} %get-tuple-element.39), channel_id=1, source_target_pairs={{0,1},{1,2},{2,3},{3,4},{4,5},{5,6},{6,7},{7,8},{8,9},{9,10},{10,1... | collective-permute-start | bytes 24584 | tf_op jit(solution)/shard_map/ppermute | solution.py:29
  154.1 5.3 %collective-permute-start.16 = (f32[4,4,128]{2,1,0:T(4,128)S(1)}, f32[4,4,128]{2,1,0:T(4,128)S(1)}, u32[]{:S(2)}, u32[]{:S(2)}) collective-permute-start(f32[4,4,128]{2,1,0:T(4,128)S(1)} %get-tuple-element.40), channel_id=1, source_target_pairs={{1,0},{2,1},{3,2},{4,3},{5,4},{6,5},{7,6},{8,7},{9,8},{10,9},{11,1... | collective-permute-start | bytes 24584 | tf_op jit(solution)/shard_map/ppermute | solution.py:31

commit v2 on v1

--- a/solution.py
+++ b/solution.py
@@ -145,13 +145,8 @@
 def tree_sum(value):
     for axis in ("gy", "gx"):
         count = lax.axis_size(axis)
-        if count & (count - 1):
-            value = lax.psum(value, axis)
-            continue
-        step = 1
-        while step < count:
-            value = value + lax.ppermute(value, axis, [(i, i ^ step) for i in range(count)])
-            step *= 2
+        copies = jnp.broadcast_to(value[None], (count,) + value.shape)
+        value = jnp.sum(lax.all_to_all(copies, axis, 0, 0, tiled=False), axis=0)
     return value
 
 

time: 161 us -> 130 us (0.81)
  the two profiles are of different devices: /device:TPU:23 before, /device:TPU:3 now
where the time goes in v2:
time: 130 us; the launch traced here: 129 us
  starting transfers between devices  31.4 us (24%)
  blocking collectives  30.6 us (24%)
  matrix products  21.3 us (16%)
  local copies, waits for them, and re-layouts  16.8 us (13%)
  other arithmetic  15.8 us (12%)
  waiting for transfers between devices  10 us (8%)
  between operations  3.13 us (2%)
    all_to_all x2, blocking collectives, tree_sum(): value = jnp.sum(lax.all_to_all(copies, axis, 0, 0, tiled=False), axis=0)  30.6 us
    ppermute x2, starting transfers between devices, halo_both(): above = lax.ppermute(head, axis, [(i + 1, i) for i in range(count - 1)])  10.5 us
    dot_general x2, matrix products, node_forces(): jnp.einsum('ij,cjabd->ciabd', stiffness, local_disp, precision=highest)  10.2 us
    ppermute x2, starting transfers between devices, halo_both(): below = lax.ppermute(tail, axis, [(i, i + 1) for i in range(count - 1)])  8.64 us
    ppermute x2, starting transfers between devices, with_halo(): lax.ppermute(tail, axis, [(i, (i + 1) % count) for i in range(ends)])  7.09 us
    unnamed x38, local copies, waits for them, and re-layouts  5.99 us
    ppermute x2, waiting for transfers between devices, halo_both(): above = lax.ppermute(head, axis, [(i + 1, i) for i in range(count - 1)])  5.26 us
    ppermute x2, starting transfers between devices, with_halo(): lax.ppermute(head, axis, [((i + 1) % count, i) for i in range(ends)])  5.19 us
  transfers between devices with their start and end apart: 8, of which 5 were waited for; matrix products, arithmetic and copies ran while one was open for 3% of the time, Pallas kernels for 0%

profile of v2, /device:TPU:3, one launch (start us, length us, event | category | flops | bytes accessed | tf_op | source)
XLA Modules:
  0.0 129.0 jit_solution(6253475319321639065)
XLA Ops:
  0.6 0.7 dynamic_slice.6
  1.4 0.7 dynamic_slice.7
  2.1 0.7 copy.274
  2.8 0.9 convolution_bitcast_fusion.1
  3.8 0.8 multiply_multiply_fusion.1
  4.8 1.1 copy.183
  6.1 4.0 %collective-permute-start = (f32[20,2,8,128]{3,1,2,0:T(2,128)S(1)}, f32[20,2,8,128]{3,1,2,0:T(2,128)S(1)}, u32[]{:S(2)}, u32[]{:S(2)}) collective-permute-start(f32[20,2,8,128]{3,1,2,0:T(2,128)S(1)} %get-tuple-element.34), channel_id=1, source_target_pairs={{0,16},{16,32},{32,48},{48,64},{64,80},{80,96},{96,112},{112,128},... | collective-permute-start | bytes 491528 | tf_op jit(solution)/shard_map/ppermute | solution.py:209
  10.1 8.6 %collective-permute-start.1 = (f32[20,2,8,128]{3,1,2,0:T(2,128)S(1)}, f32[20,2,8,128]{3,1,2,0:T(2,128)S(1)}, u32[]{:S(2)}, u32[]{:S(2)}) collective-permute-start(f32[20,2,8,128]{3,1,2,0:T(2,128)S(1)} %get-tuple-element.35), channel_id=1, source_target_pairs={{16,0},{32,16},{48,32},{64,48},{80,64},{96,80},{112,96},{128,112},... | collective-permute-start | bytes 491528 | tf_op jit(solution)/shard_map/ppermute | solution.py:210
  18.7 0.7 and_convert_fusion
  19.3 0.7 and_convert_fusion.1
  20.0 0.7 collective-permute-done
  20.6 0.9 collective-permute-done.1
  21.6 4.6 %collective-permute-start.2 = (f32[20,8,2,128]{3,1,2,0:T(8,128)S(1)}, f32[20,8,2,128]{3,1,2,0:T(8,128)S(1)}, u32[]{:S(2)}, u32[]{:S(2)}) collective-permute-start(f32[20,8,2,128]{3,1,2,0:T(8,128)S(1)} %get-tuple-element.32), channel_id=1, source_target_pairs={{0,1},{1,2},{2,3},{3,4},{4,5},{5,6},{6,7},{7,8},{8,9},{9,10},{10,1... | collective-permute-start | bytes 491528 | tf_op jit(solution)/shard_map/ppermute | solution.py:209
  26.3 1.9 %collective-permute-start.3 = (f32[20,8,2,128]{3,1,2,0:T(8,128)S(1)}, f32[20,8,2,128]{3,1,2,0:T(8,128)S(1)}, u32[]{:S(2)}, u32[]{:S(2)}) collective-permute-start(f32[20,8,2,128]{3,1,2,0:T(8,128)S(1)} %get-tuple-element.33), channel_id=1, source_target_pairs={{1,0},{2,1},{3,2},{4,3},{5,4},{6,5},{7,6},{8,7},{9,8},{10,9},{11,1... | collective-permute-start | bytes 491528 | tf_op jit(solution)/shard_map/ppermute | solution.py:210
  28.5 4.4 %collective-permute-done.3 = f32[20,8,2,128]{3,1,2,0:T(8,128)S(1)} collective-permute-done((f32[20,8,2,128]{3,1,2,0:T(8,128)S(1)}, f32[20,8,2,128]{3,1,2,0:T(8,128)S(1)}, u32[]{:S(2)}, u32[]{:S(2)}) %collective-permute-start.3) | collective-permute-done | bytes 163872 | tf_op jit(solution)/shard_map/ppermute | solution.py:210
  33.4 0.5 copy.186
  34.0 1.0 copy.205
  36.5 1.1 copy.192
  37.6 7.0 %broadcast_multiply_fusion = (f32[6,24,7,11,128]{4,1,3,2,0:T(8,128)S(1)}, f32[6,24,7,11,128]{4,1,3,2,0:T(8,128)}) fusion(f32[7,11,128]{2,1,0:T(8,128)S(1)} %copy.193, f32[6,24,7,11,128]{4,1,3,2,0:T(8,128)S(1)} %copy.192, f32[24,24,1,1,1]{1,0,4,3,2:T(8,128)S(1)} %copy-done.2), kind=kOutput, calls=%fused_computation.9 | convolution fusion | flops 410167296 | bytes 17072896 | tf_op jit(solution)/shard_map/ij,cjabd->ciabd/dot_general | solution.py:222
  44.6 1.5 %copy.236 = f32[6,24,7,11,128]{4,0,3,2,1:T(8,128)S(1)} copy(f32[6,24,7,11,128]{4,1,3,2,0:T(8,128)S(1)} %get-tuple-element.44) | data formatting | bytes 11354112 | tf_op jit(solution)/shard_map/reshape | solution.py:223
  46.6 0.9 fusion.33
  48.1 1.0 fusion.13
  51.0 3.2 %broadcast_multiply_fusion.1 = (f32[6,24,5,9,128]{4,1,3,2,0:T(8,128)S(1)}, f32[6,24,5,9,128]{4,1,3,2,0:T(8,128)S(1)}) fusion(f32[5,9,128]{2,1,0:T(8,128)S(1)} %copy.207, f32[24,24,1,1,1]{1,0,4,3,2:T(8,128)S(1)} %copy-done.2, f32[6,24,5,9,128]{4,0,3,2,1:T(8,128)S(1)} %bitcast.242), kind=kOutput, calls=%fused_computation.28 | convolution fusion | flops 239708160 | bytes 9978624 | tf_op jit(solution)/shard_map/ij,cjabd->ciabd/dot_general | solution.py:222
  54.3 0.9 copy.247
  55.4 2.6 %fusion.3 = (f32[6]{0:T(128)S(1)}, f32[6,24,4,8,128]{4,1,3,2,0:T(8,128)S(1)}, f32[6,24,4,8,128]{4,1,3,2,0:T(8,128)S(1)}) fusion(f32[6,24,7,11,128]{4,1,3,2,0:T(8,128)S(1)} %copy.192, f32[6,24,7,11,128]{4,1,3,2,0:T(8,128)} %get-tuple-element.45, f32[4,8,128]{2,1,0:T(8,128)S(1)} %get-tuple-element.36, f32[6,24,5,9,128]{4,1,3,2,0:T(8,128)S(1)} %get-tuple-element.47), kind=kLoop, calls=%fused_computation.18 | loop fusion | flops 2949114 | bytes 11812888 | tf_op jit(solution)/shard_map/reduce_sum | solution.py:303
  58.9 2.9 %multiply_reduce_fusion = (f32[6,6]{1,0:T(8,128)S(1)}, f32[6,6]{1,0:T(8,128)S(1)}) fusion(f32[6,24,4,8,128]{4,3,2,1,0:T(8,128)S(1)} %copy.218, f32[6,24,4,8,128]{4,3,2,1,0:T(8,128)S(1)} %copy.216, f32[6,24,4,8,128]{4,3,2,1,0:T(8,128)S(1)} %copy.217), kind=kLoop, calls=%fused_computation | loop fusion | flops 14155704 | bytes 7078176 | tf_op jit(solution)/shard_map/reduce_sum | solution.py:309
  61.8 1.2 fusion.12
  63.3 14.5 %all_to_all.10 = f32[16,1,180]{2,1,0:T(1,128)S(1)} all-to-all(f32[16,1,180]{2,1,0:T(1,128)S(1)} %reshape.145), channel_id=1, replica_groups=mesh['gx'=32,'gy'=16] {'gy'}, dimensions={0} | all-to-all | bytes 23040 | tf_op jit(solution)/shard_map/all_to_all | solution.py:149
  77.8 0.5 broadcast.217
  78.3 0.7 reduce.7
  79.6 16.1 %all_to_all.11 = f32[32,1,180]{2,1,0:T(1,128)S(1)} all-to-all(f32[32,1,180]{2,1,0:T(1,128)S(1)} %reshape.147), channel_id=1, replica_groups=mesh['gx'=32,'gy'=16] {'gx'}, dimensions={0} | all-to-all | bytes 46080 | tf_op jit(solution)/shard_map/all_to_all | solution.py:149
  95.7 0.7 reduce.8
  96.7 0.6 slice_bitcast_fusion.32
  97.4 0.5 cholesky.15
  98.0 0.6 compare_reduce_fusion
  98.6 0.6 fusion.135
  99.9 0.8 fusion.137
  100.8 1.2 convolution_add_fusion
  102.9 5.0 %fusion.4 = f32[4,8,128]{2,1,0:T(8,128)S(1)} fusion(f32[6,24,4,8,128]{4,0,3,2,1:T(8,128)S(1)} %bitcast.250, f32[24,24,1,1,1]{1,0,4,3,2:T(8,128)S(1)} %copy-done.2), kind=kOutput, calls=%fused_computation.21 | convolution fusion | flops 171044864 | bytes 2377984 | tf_op jit(solution)/shard_map/ij,cjabd->ciabd/dot_general | solution.py:137
  108.0 3.3 %collective-permute-start.5 = (f32[4,8,128]{2,1,0:T(8,128)S(1)}, f32[4,8,128]{2,1,0:T(8,128)S(1)}, u32[]{:S(2)}, u32[]{:S(2)}) collective-permute-start(f32[4,8,128]{2,1,0:T(8,128)S(1)} %fusion.148), channel_id=1, source_target_pairs={{16,0},{32,16},{48,32},{64,48},{80,64},{96,80},{112,96},{128,112},... | collective-permute-start | bytes 49160 | tf_op jit(solution)/shard_map/ppermute | solution.py:31
  111.3 2.0 %collective-permute-start.4 = (f32[4,8,128]{2,1,0:T(8,128)S(1)}, f32[4,8,128]{2,1,0:T(8,128)S(1)}, u32[]{:S(2)}, u32[]{:S(2)}) collective-permute-start(f32[4,8,128]{2,1,0:T(8,128)S(1)} %fusion.148), channel_id=1, source_target_pairs={{0,16},{16,32},{32,48},{48,64},{64,80},{80,96},{96,112},{112,128},... | collective-permute-start | bytes 49160 | tf_op jit(solution)/shard_map/ppermute | solution.py:29
  113.3 0.7 convolution_add_fusion.1
  114.0 3.9 %collective-permute-done.4 = f32[4,8,128]{2,1,0:T(8,128)S(1)} collective-permute-done((f32[4,8,128]{2,1,0:T(8,128)S(1)}, f32[4,8,128]{2,1,0:T(8,128)S(1)}, u32[]{:S(2)}, u32[]{:S(2)}) %collective-permute-start.4) | collective-permute-done | bytes 16416 | tf_op jit(solution)/shard_map/ppermute | solution.py:29
  117.9 5.1 %collective-permute-start.6 = (f32[4,4,128]{2,1,0:T(4,128)S(1)}, f32[4,4,128]{2,1,0:T(4,128)S(1)}, u32[]{:S(2)}, u32[]{:S(2)}) collective-permute-start(f32[4,4,128]{2,1,0:T(4,128)S(1)} %get-tuple-element.41), channel_id=1, source_target_pairs={{0,1},{1,2},{2,3},{3,4},{4,5},{5,6},{6,7},{7,8},{8,9},{9,10},{10,1... | collective-permute-start | bytes 24584 | tf_op jit(solution)/shard_map/ppermute | solution.py:29
  123.0 1.9 %collective-permute-start.7 = (f32[4,4,128]{2,1,0:T(4,128)S(1)}, f32[4,4,128]{2,1,0:T(4,128)S(1)}, u32[]{:S(2)}, u32[]{:S(2)}) collective-permute-start(f32[4,4,128]{2,1,0:T(4,128)S(1)} %get-tuple-element.42), channel_id=1, source_target_pairs={{1,0},{2,1},{3,2},{4,3},{5,4},{6,5},{7,6},{8,7},{9,8},{10,9},{11,1... | collective-permute-start | bytes 24584 | tf_op jit(solution)/shard_map/ppermute | solution.py:31
  124.9 0.7 multiply_reduce_fusion.2
  125.6 0.8 copy.229
  128.3 0.7 multiply_minimum_fusion
  (82 shorter events, 9.8 us)
Async XLA Ops:
  6.1 14.6 %collective-permute-start = (f32[20,2,8,128]{3,1,2,0:T(2,128)S(1)}, f32[20,2,8,128]{3,1,2,0:T(2,128)S(1)}, u32[]{:S(2)}, u32[]{:S(2)}) collective-permute-start(f32[20,2,8,128]{3,1,2,0:T(2,128)S(1)} %get-tuple-element.34), channel_id=1, source_target_pairs={{0,16},{16,32},{32,48},{48,64},{64,80},{80,96},{96,112},{112,128},... | collective-permute-start | bytes 491528 | tf_op jit(solution)/shard_map/ppermute | solution.py:209
  10.1 11.4 %collective-permute-start.1 = (f32[20,2,8,128]{3,1,2,0:T(2,128)S(1)}, f32[20,2,8,128]{3,1,2,0:T(2,128)S(1)}, u32[]{:S(2)}, u32[]{:S(2)}) collective-permute-start(f32[20,2,8,128]{3,1,2,0:T(2,128)S(1)} %get-tuple-element.35), channel_id=1, source_target_pairs={{16,0},{32,16},{48,32},{64,48},{80,64},{96,80},{112,96},{128,112},... | collective-permute-start | bytes 491528 | tf_op jit(solution)/shard_map/ppermute | solution.py:210
  21.6 6.9 %collective-permute-start.2 = (f32[20,8,2,128]{3,1,2,0:T(8,128)S(1)}, f32[20,8,2,128]{3,1,2,0:T(8,128)S(1)}, u32[]{:S(2)}, u32[]{:S(2)}) collective-permute-start(f32[20,8,2,128]{3,1,2,0:T(8,128)S(1)} %get-tuple-element.32), channel_id=1, source_target_pairs={{0,1},{1,2},{2,3},{3,4},{4,5},{5,6},{6,7},{7,8},{8,9},{9,10},{10,1... | collective-permute-start | bytes 491528 | tf_op jit(solution)/shard_map/ppermute | solution.py:209
  26.3 6.6 %collective-permute-start.3 = (f32[20,8,2,128]{3,1,2,0:T(8,128)S(1)}, f32[20,8,2,128]{3,1,2,0:T(8,128)S(1)}, u32[]{:S(2)}, u32[]{:S(2)}) collective-permute-start(f32[20,8,2,128]{3,1,2,0:T(8,128)S(1)} %get-tuple-element.33), channel_id=1, source_target_pairs={{1,0},{2,1},{3,2},{4,3},{5,4},{6,5},{7,6},{8,7},{9,8},{10,9},{11,1... | collective-permute-start | bytes 491528 | tf_op jit(solution)/shard_map/ppermute | solution.py:210
  36.5 1.1 copy-start.2
  102.3 5.7 %copy-start.1 = (f32[4,8,128]{2,1,0:T(8,128)S(1)}, f32[4,8,128]{2,1,0:T(8,128)}, u32[]{:S(2)}) copy-start(f32[4,8,128]{2,1,0:T(8,128)} %param.13) | copy-start | bytes 49156
  102.3 5.7 %copy-start.3 = (s32[4,8,128]{2,1,0:T(8,128)S(1)}, s32[4,8,128]{2,1,0:T(8,128)}, u32[]{:S(2)}) copy-start(s32[4,8,128]{2,1,0:T(8,128)} %param.12) | copy-start | bytes 49156
  102.3 11.0 %copy-start = (f32[6,3,4,8,128]{4,3,2,1,0:T(8,128)S(1)}, f32[6,3,4,8,128]{4,3,2,1,0:T(8,128)}, u32[]{:S(2)}) copy-start(f32[6,3,4,8,128]{4,3,2,1,0:T(8,128)} %param.11) | copy-start | bytes 884740
  108.0 6.0 %collective-permute-start.5 = (f32[4,8,128]{2,1,0:T(8,128)S(1)}, f32[4,8,128]{2,1,0:T(8,128)S(1)}, u32[]{:S(2)}, u32[]{:S(2)}) collective-permute-start(f32[4,8,128]{2,1,0:T(8,128)S(1)} %fusion.148), channel_id=1, source_target_pairs={{16,0},{32,16},{48,32},{64,48},{80,64},{96,80},{112,96},{128,112},... | collective-permute-start | bytes 49160 | tf_op jit(solution)/shard_map/ppermute | solution.py:31
  111.3 6.6 %collective-permute-start.4 = (f32[4,8,128]{2,1,0:T(8,128)S(1)}, f32[4,8,128]{2,1,0:T(8,128)S(1)}, u32[]{:S(2)}, u32[]{:S(2)}) collective-permute-start(f32[4,8,128]{2,1,0:T(8,128)S(1)} %fusion.148), channel_id=1, source_target_pairs={{0,16},{16,32},{32,48},{48,64},{64,80},{80,96},{96,112},{112,128},... | collective-permute-start | bytes 49160 | tf_op jit(solution)/shard_map/ppermute | solution.py:29
  117.9 10.4 %collective-permute-start.6 = (f32[4,4,128]{2,1,0:T(4,128)S(1)}, f32[4,4,128]{2,1,0:T(4,128)S(1)}, u32[]{:S(2)}, u32[]{:S(2)}) collective-permute-start(f32[4,4,128]{2,1,0:T(4,128)S(1)} %get-tuple-element.41), channel_id=1, source_target_pairs={{0,1},{1,2},{2,3},{3,4},{4,5},{5,6},{6,7},{7,8},{8,9},{9,10},{10,1... | collective-permute-start | bytes 24584 | tf_op jit(solution)/shard_map/ppermute | solution.py:29
  123.0 5.3 %collective-permute-start.7 = (f32[4,4,128]{2,1,0:T(4,128)S(1)}, f32[4,4,128]{2,1,0:T(4,128)S(1)}, u32[]{:S(2)}, u32[]{:S(2)}) collective-permute-start(f32[4,4,128]{2,1,0:T(4,128)S(1)} %get-tuple-element.42), channel_id=1, source_target_pairs={{1,0},{2,1},{3,2},{4,3},{5,4},{6,5},{7,6},{8,7},{9,8},{10,9},{11,1... | collective-permute-start | bytes 24584 | tf_op jit(solution)/shard_map/ppermute | solution.py:31

commit v3 on v2

--- a/solution.py
+++ b/solution.py
@@ -285,14 +285,13 @@
     for dim, axis in ((0, "gx"), (1, "gy"), (2, None)):
         extent = modulus.shape[dim]
         count = 1 if axis is None else lax.axis_size(axis)
-        places = np.arange(extent * count)
-        kept = np.zeros(extent * count)
+        places = lax.iota(jnp.int32, extent)
+        if axis is not None:
+            places = places + lax.axis_index(axis) * extent
+        kept = jnp.zeros((extent,), jnp.float32)
         for tap_index, weight in enumerate(blur_weights()):
-            inside = (places + 4 - tap_index >= 0) & (places + 4 - tap_index < extent * count)
-            kept = kept + np.where(inside, weight, 0.0)
-        kept = jnp.asarray(kept, jnp.float32)
-        if axis is not None:
-            kept = lax.dynamic_slice_in_dim(kept, lax.axis_index(axis) * extent, extent)
+            shifted = places + 4 - tap_index
+            kept = kept + jnp.where((shifted >= 0) & (shifted < extent * count), weight, 0.0)
         shape = [1, 1, 1]
         shape[dim] = extent
         blur_mass = blur_mass * kept.reshape(shape)
@@ -328,10 +327,13 @@
         + jnp.sum(step_alpha[:, None, :] * grams[3][:, :, None] * step_alpha[None, :, :])
     )
     solution = start_disp + mix_cases(residual, step_alpha)
-    node_field = start_nodes[:, :, 2:-1, 2:-1] + mix_cases(
-        residual_nodes[:, :, 1:, 1:], step_alpha
-    )
-    energy = element_energy(node_field, stiffness)
+    final_elems = start_elems + jnp.sum(
+        residual_elems[:, None] * step_alpha[:, :, None, None, None, None], axis=0
+    )
+    final_loads = start_loads + jnp.sum(
+        residual_loads[:, None] * step_alpha[:, :, None, None, None, None], axis=0
+    )
+    energy = jnp.sum(final_elems * final_loads, axis=(0, 1))
     stimulus = modulus * energy
     smooth = blur_valid(with_halo(stimulus, (("gx", 0),), 4), 0, size_x)
     smooth = blur_valid(with_halo(smooth, (("gy", 1),), 4), 1, size_y)

time: 130 us -> 148 us (1.14)
  blocking collectives: 30.6 us -> 14.6 us
  local copies, waits for them, and re-layouts: 16.8 us -> 31.3 us
  other arithmetic: 15.8 us -> 28.8 us
  starting transfers between devices: 31.4 us -> 39.9 us
  matrix products: 21.3 us -> 15 us
  waiting for transfers between devices: 10 us -> 14.3 us
    all_to_all x2 -> x1, blocking collectives: 30.6 us -> 14.6 us  [tree_sum(): value = jnp.sum(lax.all_to_all(copies, axis, 0, 0, tiled=False), axis=0)]
    all_to_all x0 -> x1, starting transfers between devices: none -> 8.49 us  [tree_sum(): value = jnp.sum(lax.all_to_all(copies, axis, 0, 0, tiled=False), axis=0)]
    unnamed x38 -> x33, local copies, waits for them, and re-layouts: 5.99 us -> 14.1 us
    reduce_sum x1 -> x2, other arithmetic: 2.62 us -> 10.1 us  [the longest x1 5.59 us: on_device(): energy = jnp.sum(final_elems * final_loads, axis=(0, 1))]
    dot_general x1 -> x0, matrix products: 5.04 us -> none  [element_energy(): jnp.einsum('ij,cjabd->ciabd', stiffness, local_disp, precision=highest)]
    all_to_all x0 -> x1, waiting for transfers between devices: none -> 4.24 us  [tree_sum(): value = jnp.sum(lax.all_to_all(copies, axis, 0, 0, tiled=False), axis=0)]
    another operation x3, local copies, waits for them, and re-layouts: 0.69 us -> 4.68 us  [cases_disp(): jnp.stack(corners, axis=1)]
    slice x0 -> x1, other arithmetic: none -> 3.9 us  [on_device(): residual_loads = residual_loads[:, :, 1:, 1:]]
  transfers between devices with their start and end apart: 8 -> 9, of which waited for: 5 -> 6; matrix products, arithmetic and copies ran while one was open for 3% -> 5% of each run, Pallas kernels for 0% -> 0%
where the time goes in v3:
time: 148 us; the launch traced here: 147 us
  starting transfers between devices  39.9 us (27%)
  local copies, waits for them, and re-layouts  31.3 us (21%)
  other arithmetic  28.8 us (19%)
  matrix products  15 us (10%)
  blocking collectives  14.6 us (10%)
  waiting for transfers between devices  14.3 us (10%)
  between operations  3.16 us (2%)
    all_to_all x1, blocking collectives, tree_sum(): value = jnp.sum(lax.all_to_all(copies, axis, 0, 0, tiled=False), axis=0)  14.6 us
    unnamed x33, local copies, waits for them, and re-layouts  14.1 us
    ppermute x2, starting transfers between devices, halo_both(): above = lax.ppermute(head, axis, [(i + 1, i) for i in range(count - 1)])  10.5 us
    dot_general x2, matrix products, node_forces(): jnp.einsum('ij,cjabd->ciabd', stiffness, local_disp, precision=highest)  10.2 us
    ppermute x2, starting transfers between devices, halo_both(): below = lax.ppermute(tail, axis, [(i, i + 1) for i in range(count - 1)])  8.64 us
    all_to_all x1, starting transfers between devices, tree_sum(): value = jnp.sum(lax.all_to_all(copies, axis, 0, 0, tiled=False), axis=0)  8.49 us
    ppermute x2, starting transfers between devices, with_halo(): lax.ppermute(tail, axis, [(i, (i + 1) % count) for i in range(ends)])  7.1 us
    reduce_sum x1, other arithmetic, on_device(): energy = jnp.sum(final_elems * final_loads, axis=(0, 1))  5.59 us
  transfers between devices with their start and end apart: 9, of which 6 were waited for; matrix products, arithmetic and copies ran while one was open for 5% of the time, Pallas kernels for 0%

profile of v3, /device:TPU:3, one launch (start us, length us, event | category | flops | bytes accessed | tf_op | source)
XLA Modules:
  0.0 146.9 jit_solution(15030926787450392570)
XLA Ops:
  1.4 0.9 convolution_bitcast_fusion.1
  2.4 0.8 multiply_multiply_fusion.1
  3.4 1.1 copy.159
  4.7 4.0 %collective-permute-start = (f32[20,2,8,128]{3,1,2,0:T(2,128)S(1)}, f32[20,2,8,128]{3,1,2,0:T(2,128)S(1)}, u32[]{:S(2)}, u32[]{:S(2)}) collective-permute-start(f32[20,2,8,128]{3,1,2,0:T(2,128)S(1)} %get-tuple-element.38), channel_id=1, source_target_pairs={{0,16},{16,32},{32,48},{48,64},{64,80},{80,96},{96,112},{112,128},... | collective-permute-start | bytes 491528 | tf_op jit(solution)/shard_map/ppermute | solution.py:209
  8.7 8.6 %collective-permute-start.1 = (f32[20,2,8,128]{3,1,2,0:T(2,128)S(1)}, f32[20,2,8,128]{3,1,2,0:T(2,128)S(1)}, u32[]{:S(2)}, u32[]{:S(2)}) collective-permute-start(f32[20,2,8,128]{3,1,2,0:T(2,128)S(1)} %get-tuple-element.39), channel_id=1, source_target_pairs={{16,0},{32,16},{48,32},{64,48},{80,64},{96,80},{112,96},{128,112},... | collective-permute-start | bytes 491528 | tf_op jit(solution)/shard_map/ppermute | solution.py:210
  19.2 0.9 collective-permute-done.1
  20.2 4.6 %collective-permute-start.2 = (f32[20,8,2,128]{3,1,2,0:T(8,128)S(1)}, f32[20,8,2,128]{3,1,2,0:T(8,128)S(1)}, u32[]{:S(2)}, u32[]{:S(2)}) collective-permute-start(f32[20,8,2,128]{3,1,2,0:T(8,128)S(1)} %get-tuple-element.36), channel_id=1, source_target_pairs={{0,1},{1,2},{2,3},{3,4},{4,5},{5,6},{6,7},{7,8},{8,9},{9,10},{10,1... | collective-permute-start | bytes 491528 | tf_op jit(solution)/shard_map/ppermute | solution.py:209
  24.8 1.9 %collective-permute-start.3 = (f32[20,8,2,128]{3,1,2,0:T(8,128)S(1)}, f32[20,8,2,128]{3,1,2,0:T(8,128)S(1)}, u32[]{:S(2)}, u32[]{:S(2)}) collective-permute-start(f32[20,8,2,128]{3,1,2,0:T(8,128)S(1)} %get-tuple-element.37), channel_id=1, source_target_pairs={{1,0},{2,1},{3,2},{4,3},{5,4},{6,5},{7,6},{8,7},{9,8},{10,9},{11,1... | collective-permute-start | bytes 491528 | tf_op jit(solution)/shard_map/ppermute | solution.py:210
  27.1 4.4 %collective-permute-done.3 = f32[20,8,2,128]{3,1,2,0:T(8,128)S(1)} collective-permute-done((f32[20,8,2,128]{3,1,2,0:T(8,128)S(1)}, f32[20,8,2,128]{3,1,2,0:T(8,128)S(1)}, u32[]{:S(2)}, u32[]{:S(2)}) %collective-permute-start.3) | collective-permute-done | bytes 163872 | tf_op jit(solution)/shard_map/ppermute | solution.py:210
  31.9 0.9 fusion.20
  33.0 1.0 copy.176
  34.0 1.2 fusion.10
  35.2 1.0 fusion.19
  36.2 1.2 fusion.12
  37.3 1.0 fusion.18
  38.3 1.2 fusion.14
  39.5 1.0 fusion.17
  40.5 1.2 fusion.16
  41.7 3.3 %copy.162 = f32[6,8,3,7,11,128]{5,3,4,2,1,0:T(8,128)S(1)} copy(f32[6,8,3,7,11,128]{5,3,4,2,0,1:T(8,128)} %fusion.16) | data formatting | bytes 11354112 | tf_op jit(solution)/shard_map/stack | solution.py:116
  45.0 1.0 copy.163
  46.0 7.0 %broadcast_multiply_fusion = (f32[6,24,7,11,128]{4,1,3,2,0:T(8,128)S(1)}, f32[6,24,7,11,128]{4,1,3,2,0:T(8,128)}) fusion(f32[7,11,128]{2,1,0:T(8,128)S(1)} %copy.164, f32[6,24,7,11,128]{4,1,3,2,0:T(8,128)S(1)} %copy.163, f32[24,24,1,1,1]{1,0,4,3,2:T(8,128)S(1)} %copy-done.4), kind=kOutput, calls=%fused_computation.6 | convolution fusion | flops 410167296 | bytes 17072896 | tf_op jit(solution)/shard_map/ij,cjabd->ciabd/dot_general | solution.py:222
  53.0 1.5 copy.205
  54.9 0.9 fusion.28
  56.5 1.0 fusion.8
  59.5 3.2 %broadcast_multiply_fusion.1 = (f32[6,24,5,9,128]{4,1,3,2,0:T(8,128)S(1)}, f32[6,24,5,9,128]{4,1,3,2,0:T(8,128)S(1)}) fusion(f32[5,9,128]{2,1,0:T(8,128)S(1)} %copy.178, f32[24,24,1,1,1]{1,0,4,3,2:T(8,128)S(1)} %copy-done.4, f32[6,24,5,9,128]{4,0,3,2,1:T(8,128)S(1)} %bitcast.209), kind=kOutput, calls=%fused_computation.25 | convolution fusion | flops 239708160 | bytes 9978624 | tf_op jit(solution)/shard_map/ij,cjabd->ciabd/dot_general | solution.py:222
  62.7 0.9 copy.214
  63.9 3.9 %fusion.160 = (f32[6,24,4,8,128]{4,1,3,2,0:T(8,128)}, f32[6,24,4,8,128]{4,1,3,2,0:T(8,128)S(1)}, f32[6,24,4,8,128]{4,1,3,2,0:T(8,128)S(1)}, f32[6]{0:T(128)S(1)}) fusion(f32[6,24,5,9,128]{4,1,3,2,0:T(8,128)S(1)} %get-tuple-element.52, f32[4,8,128]{2,1,0:T(8,128)S(1)} %get-tuple-element.40, f32[6,24,7,11,128]{4,1,3,2,0:T(8,128)} %get-tuple-element.50, ...), kind=kLoop, calls=%fused_computation.314 | loop fusion | flops 2949114 | bytes 14172184 | tf_op jit(solution)/shard_map/slice | solution.py:301
  68.6 3.3 %multiply_reduce_fusion.2 = (f32[6,6]{1,0:T(8,128)S(1)}, f32[6,6]{1,0:T(8,128)S(1)}) fusion(f32[6,24,4,8,128]{4,3,2,1,0:T(8,128)S(1)} %copy.189, f32[6,24,4,8,128]{4,3,2,1,0:T(8,128)S(1)} %copy.187, f32[6,24,4,8,128]{4,3,2,1,0:T(8,128)S(1)} %copy.188), kind=kLoop, calls=%fused_computation.2 | loop fusion | flops 14155704 | bytes 7078176 | tf_op jit(solution)/shard_map/reduce_sum | solution.py:308
  71.9 1.2 fusion.7
  73.4 14.6 %all_to_all.10 = f32[16,1,180]{2,1,0:T(1,128)S(1)} all-to-all(f32[16,1,180]{2,1,0:T(1,128)S(1)} %reshape.317), channel_id=1, replica_groups=mesh['gx'=32,'gy'=16] {'gy'}, dimensions={0} | all-to-all | bytes 23040 | tf_op jit(solution)/shard_map/all_to_all | solution.py:149
  89.3 0.9 broadcast_in_dim.179
  90.2 2.0 %reshape.319 = f32[32,1,180]{2,1,0:T(1,128)} reshape(f32[32,5,6,6]{3,2,1,0:T(8,128)} %broadcast_in_dim.179) | data formatting | bytes 46080
  92.2 8.5 %all-to-all-start.1 = ((f32[32,1,180]{2,1,0:T(1,128)}), f32[32,1,180]{2,1,0:T(1,128)S(1)}, u32[]{:S(2)}, u32[]{:S(2)}) async-start(f32[32,1,180]{2,1,0:T(1,128)} %reshape.319), calls=%async_computation.1 | async-start | bytes 65536 | tf_op jit(solution)/shard_map/all_to_all | solution.py:149
  100.7 3.6 %copy.198 = f32[6,24,4,8,128]{4,3,2,1,0:T(8,128)} copy(f32[6,24,4,8,128]{4,1,3,2,0:T(8,128)} %get-tuple-element.34) | data formatting | bytes 4718592 | tf_op jit(solution)/shard_map/slice | solution.py:301
  104.3 4.2 %all-to-all-done.1 = f32[32,1,180]{2,1,0:T(1,128)S(1)} async-done(((f32[32,1,180]{2,1,0:T(1,128)}), f32[32,1,180]{2,1,0:T(1,128)S(1)}, u32[]{:S(2)}, u32[]{:S(2)}) %all-to-all-start.1) | async-done | bytes 23072 | tf_op jit(solution)/shard_map/all_to_all | solution.py:149
  108.5 0.7 reduce.8
  109.2 1.1 reshape.320
  110.3 1.2 reduce_sum.103
  114.7 0.8 fusion.124
  115.5 4.5 %multiply_reduce_fusion.1 = (f32[6,24,4,8,128]{4,3,2,1,0:T(8,128)S(1)}, f32[6,24,4,8,128]{4,3,2,1,0:T(8,128)S(1)}) fusion(f32[6,6]{1,0:T(8,128)S(1)} %get-tuple-element.54, f32[6,24,4,8,128]{4,3,2,1,0:T(8,128)S(1)} %copy.187, f32[6,24,4,8,128]{4,3,2,1,0:T(8,128)} %copy.198), kind=kLoop, calls=%fused_computation.1 | loop fusion | flops 12976128 | bytes 9437328 | tf_op jit(solution)/shard_map/reduce_sum | solution.py:330
  120.0 5.6 %fusion.3 = f32[4,8,128]{2,1,0:T(8,128)S(1)} fusion(f32[6,24,4,8,128]{4,3,2,1,0:T(8,128)S(1)} %get-tuple-element.15, f32[6,24,4,8,128]{4,3,2,1,0:T(8,128)S(1)} %get-tuple-element.14, f32[6,24,7,11,128]{4,1,3,2,0:T(8,128)} %copy-done, f32[6,24,7,11,128]{4,1,3,2,0:T(8,128)} %get-tuple-element.50), kind=kLoop, calls=%fused_computation.14 | loop fusion | flops 2355200 | bytes 9453568 | tf_op jit(solution)/shard_map/reduce_sum | solution.py:336
  125.7 3.3 %collective-permute-start.5 = (f32[4,8,128]{2,1,0:T(8,128)S(1)}, f32[4,8,128]{2,1,0:T(8,128)S(1)}, u32[]{:S(2)}, u32[]{:S(2)}) collective-permute-start(f32[4,8,128]{2,1,0:T(8,128)S(1)} %fusion.158), channel_id=1, source_target_pairs={{16,0},{32,16},{48,32},{64,48},{80,64},{96,80},{112,96},{128,112},... | collective-permute-start | bytes 49160 | tf_op jit(solution)/shard_map/ppermute | solution.py:31
  128.9 2.0 %collective-permute-start.4 = (f32[4,8,128]{2,1,0:T(8,128)S(1)}, f32[4,8,128]{2,1,0:T(8,128)S(1)}, u32[]{:S(2)}, u32[]{:S(2)}) collective-permute-start(f32[4,8,128]{2,1,0:T(8,128)S(1)} %fusion.158), channel_id=1, source_target_pairs={{0,16},{16,32},{32,48},{48,64},{64,80},{80,96},{96,112},{112,128},... | collective-permute-start | bytes 49160 | tf_op jit(solution)/shard_map/ppermute | solution.py:29
  131.7 3.9 %collective-permute-done.4 = f32[4,8,128]{2,1,0:T(8,128)S(1)} collective-permute-done((f32[4,8,128]{2,1,0:T(8,128)S(1)}, f32[4,8,128]{2,1,0:T(8,128)S(1)}, u32[]{:S(2)}, u32[]{:S(2)}) %collective-permute-start.4) | collective-permute-done | bytes 16416 | tf_op jit(solution)/shard_map/ppermute | solution.py:29
  135.6 5.1 %collective-permute-start.6 = (f32[4,4,128]{2,1,0:T(4,128)S(1)}, f32[4,4,128]{2,1,0:T(4,128)S(1)}, u32[]{:S(2)}, u32[]{:S(2)}) collective-permute-start(f32[4,4,128]{2,1,0:T(4,128)S(1)} %get-tuple-element.47), channel_id=1, source_target_pairs={{0,1},{1,2},{2,3},{3,4},{4,5},{5,6},{6,7},{7,8},{8,9},{9,10},{10,1... | collective-permute-start | bytes 24584 | tf_op jit(solution)/shard_map/ppermute | solution.py:29
  140.7 1.9 %collective-permute-start.7 = (f32[4,4,128]{2,1,0:T(4,128)S(1)}, f32[4,4,128]{2,1,0:T(4,128)S(1)}, u32[]{:S(2)}, u32[]{:S(2)}) collective-permute-start(f32[4,4,128]{2,1,0:T(4,128)S(1)} %get-tuple-element.48), channel_id=1, source_target_pairs={{1,0},{2,1},{3,2},{4,3},{5,4},{6,5},{7,6},{8,7},{9,8},{10,9},{11,1... | collective-permute-start | bytes 24584 | tf_op jit(solution)/shard_map/ppermute | solution.py:31
  142.6 0.8 multiply_reduce_fusion.5
  143.3 0.8 copy.200
  (80 shorter events, 14.6 us)
Async XLA Ops:
  4.7 14.6 %collective-permute-start = (f32[20,2,8,128]{3,1,2,0:T(2,128)S(1)}, f32[20,2,8,128]{3,1,2,0:T(2,128)S(1)}, u32[]{:S(2)}, u32[]{:S(2)}) collective-permute-start(f32[20,2,8,128]{3,1,2,0:T(2,128)S(1)} %get-tuple-element.38), channel_id=1, source_target_pairs={{0,16},{16,32},{32,48},{48,64},{64,80},{80,96},{96,112},{112,128},... | collective-permute-start | bytes 491528 | tf_op jit(solution)/shard_map/ppermute | solution.py:209
  8.7 11.4 %collective-permute-start.1 = (f32[20,2,8,128]{3,1,2,0:T(2,128)S(1)}, f32[20,2,8,128]{3,1,2,0:T(2,128)S(1)}, u32[]{:S(2)}, u32[]{:S(2)}) collective-permute-start(f32[20,2,8,128]{3,1,2,0:T(2,128)S(1)} %get-tuple-element.39), channel_id=1, source_target_pairs={{16,0},{32,16},{48,32},{64,48},{80,64},{96,80},{112,96},{128,112},... | collective-permute-start | bytes 491528 | tf_op jit(solution)/shard_map/ppermute | solution.py:210
  20.2 6.9 %collective-permute-start.2 = (f32[20,8,2,128]{3,1,2,0:T(8,128)S(1)}, f32[20,8,2,128]{3,1,2,0:T(8,128)S(1)}, u32[]{:S(2)}, u32[]{:S(2)}) collective-permute-start(f32[20,8,2,128]{3,1,2,0:T(8,128)S(1)} %get-tuple-element.36), channel_id=1, source_target_pairs={{0,1},{1,2},{2,3},{3,4},{4,5},{5,6},{6,7},{7,8},{8,9},{9,10},{10,1... | collective-permute-start | bytes 491528 | tf_op jit(solution)/shard_map/ppermute | solution.py:209
  24.8 6.6 %collective-permute-start.3 = (f32[20,8,2,128]{3,1,2,0:T(8,128)S(1)}, f32[20,8,2,128]{3,1,2,0:T(8,128)S(1)}, u32[]{:S(2)}, u32[]{:S(2)}) collective-permute-start(f32[20,8,2,128]{3,1,2,0:T(8,128)S(1)} %get-tuple-element.37), channel_id=1, source_target_pairs={{1,0},{2,1},{3,2},{4,3},{5,4},{6,5},{7,6},{8,7},{9,8},{10,9},{11,1... | collective-permute-start | bytes 491528 | tf_op jit(solution)/shard_map/ppermute | solution.py:210
  45.0 1.0 copy-start.4
  46.0 17.9 %copy-start = (f32[6,24,7,11,128]{4,1,3,2,0:T(8,128)}, f32[6,24,7,11,128]{4,1,3,2,0:T(8,128)S(1)}, u32[]{:S(2)}) copy-start(f32[6,24,7,11,128]{4,1,3,2,0:T(8,128)S(1)} %copy.163) | copy-start | bytes 17031172
  92.2 16.3 %all-to-all-start.1 = ((f32[32,1,180]{2,1,0:T(1,128)}), f32[32,1,180]{2,1,0:T(1,128)S(1)}, u32[]{:S(2)}, u32[]{:S(2)}) async-start(f32[32,1,180]{2,1,0:T(1,128)} %reshape.319), calls=%async_computation.1 | async-start | bytes 65536 | tf_op jit(solution)/shard_map/all_to_all | solution.py:149
  120.0 5.6 %copy-start.2 = (f32[4,8,128]{2,1,0:T(8,128)S(1)}, f32[4,8,128]{2,1,0:T(8,128)}, u32[]{:S(2)}) copy-start(f32[4,8,128]{2,1,0:T(8,128)} %param.10) | copy-start | bytes 49156
  120.0 5.6 %copy-start.3 = (s32[4,8,128]{2,1,0:T(8,128)S(1)}, s32[4,8,128]{2,1,0:T(8,128)}, u32[]{:S(2)}) copy-start(s32[4,8,128]{2,1,0:T(8,128)} %param.9) | copy-start | bytes 49156
  120.0 10.9 %copy-start.1 = (f32[6,3,4,8,128]{4,3,2,1,0:T(8,128)S(1)}, f32[6,3,4,8,128]{4,3,2,1,0:T(8,128)}, u32[]{:S(2)}) copy-start(f32[6,3,4,8,128]{4,3,2,1,0:T(8,128)} %param.8) | copy-start | bytes 884740
  125.7 6.0 %collective-permute-start.5 = (f32[4,8,128]{2,1,0:T(8,128)S(1)}, f32[4,8,128]{2,1,0:T(8,128)S(1)}, u32[]{:S(2)}, u32[]{:S(2)}) collective-permute-start(f32[4,8,128]{2,1,0:T(8,128)S(1)} %fusion.158), channel_id=1, source_target_pairs={{16,0},{32,16},{48,32},{64,48},{80,64},{96,80},{112,96},{128,112},... | collective-permute-start | bytes 49160 | tf_op jit(solution)/shard_map/ppermute | solution.py:31
  128.9 6.6 %collective-permute-start.4 = (f32[4,8,128]{2,1,0:T(8,128)S(1)}, f32[4,8,128]{2,1,0:T(8,128)S(1)}, u32[]{:S(2)}, u32[]{:S(2)}) collective-permute-start(f32[4,8,128]{2,1,0:T(8,128)S(1)} %fusion.158), channel_id=1, source_target_pairs={{0,16},{16,32},{32,48},{48,64},{64,80},{80,96},{96,112},{112,128},... | collective-permute-start | bytes 49160 | tf_op jit(solution)/shard_map/ppermute | solution.py:29
  135.6 10.5 %collective-permute-start.6 = (f32[4,4,128]{2,1,0:T(4,128)S(1)}, f32[4,4,128]{2,1,0:T(4,128)S(1)}, u32[]{:S(2)}, u32[]{:S(2)}) collective-permute-start(f32[4,4,128]{2,1,0:T(4,128)S(1)} %get-tuple-element.47), channel_id=1, source_target_pairs={{0,1},{1,2},{2,3},{3,4},{4,5},{5,6},{6,7},{7,8},{8,9},{9,10},{10,1... | collective-permute-start | bytes 24584 | tf_op jit(solution)/shard_map/ppermute | solution.py:29
  140.7 5.4 %collective-permute-start.7 = (f32[4,4,128]{2,1,0:T(4,128)S(1)}, f32[4,4,128]{2,1,0:T(4,128)S(1)}, u32[]{:S(2)}, u32[]{:S(2)}) collective-permute-start(f32[4,4,128]{2,1,0:T(4,128)S(1)} %get-tuple-element.48), channel_id=1, source_target_pairs={{1,0},{2,1},{3,2},{4,3},{5,4},{6,5},{7,6},{8,7},{9,8},{10,9},{11,1... | collective-permute-start | bytes 24584 | tf_op jit(solution)/shard_map/ppermute | solution.py:31

commit v4 on v2

--- a/solution.py
+++ b/solution.py
@@ -202,6 +202,60 @@
     return jnp.concatenate([kept[:, :, :1] + to_x, kept[:, :, 1:]], axis=2)
 
 
+def corner_modes(node_field):
+    found = {(): node_field}
+    for dim in (2, 3, 4):
+        grown = {}
+        for key, cells in found.items():
+            low = lax.slice_in_dim(cells, 0, cells.shape[dim] - 1, axis=dim)
+            high = lax.slice_in_dim(cells, 1, cells.shape[dim], axis=dim)
+            grown[key + (0,)] = high + low
+            grown[key + (1,)] = high - low
+        found = grown
+    return [found[(mode // 4, mode // 2 % 2, mode % 2)] for mode in range(8)]
+
+
+def mode_stiffness():
+    step = np.array([[1.0, 1.0], [-1.0, 1.0]])
+    change = np.kron(np.kron(np.kron(step, step), step), np.eye(3))
+    return change @ hex_stiffness() @ change.T / 64.0
+
+
+def mode_loads(modes, table):
+    loads = []
+    for mode in range(8):
+        parts = []
+        for comp in range(3):
+            total = None
+            for other in range(3):
+                source = mode ^ (4 >> comp) ^ (4 >> other)
+                weight = float(table[3 * mode + comp, 3 * source + other])
+                if abs(weight) < 1e-12:
+                    continue
+                term = weight * modes[source][:, other]
+                total = term if total is None else total + term
+            parts.append(jnp.zeros_like(modes[mode][:, comp]) if total is None else total)
+        loads.append(jnp.stack(parts, axis=1))
+    return loads
+
+
+def modes_to_nodes(loads):
+    found = {(mode // 4, mode // 2 % 2, mode % 2): loads[mode] for mode in range(8)}
+    for dim in (4, 3, 2):
+        merged = {}
+        for key in {k[:-1] for k in found}:
+            total = found[key + (0,)]
+            change = found[key + (1,)]
+            widths = [(0, 0)] * total.ndim
+            low = list(widths)
+            low[dim] = (0, 1)
+            high = list(widths)
+            high[dim] = (1, 0)
+            merged[key] = jnp.pad(total - change, low) + jnp.pad(total + change, high)
+        found = merged
+    return found[()]
+
+
 def halo_both(cells, axis, dim, width):
     count = lax.axis_size(axis)
     head = lax.slice_in_dim(cells, 0, width, axis=dim)
@@ -217,22 +271,15 @@
     return ((own >= 0) & (own < total)).astype(jnp.float32)
 
 
-def node_forces(node_field, modulus, stiffness):
-    local_disp = cases_disp(node_field)
-    local_load = jnp.einsum("ij,cjabd->ciabd", stiffness, local_disp, precision=highest)
-    local_force = (local_load * modulus).reshape((node_field.shape[0], 8, 3) + modulus.shape)
-    summed = jnp.zeros_like(node_field)
-    for corner in range(8):
-        off_x, off_y, off_z = (corner // 4, corner // 2 % 2, corner % 2)
-        summed = summed + jnp.pad(
-            local_force[:, corner],
-            ((0, 0), (0, 0), (off_x, 1 - off_x), (off_y, 1 - off_y), (off_z, 1 - off_z)),
-        )
-    return summed[..., :-1], local_disp, local_load
+def node_forces(node_field, modulus, table):
+    modes = corner_modes(node_field)
+    loads = mode_loads(modes, table)
+    summed = modes_to_nodes([part * modulus for part in loads])
+    return summed[..., :-1], jnp.stack(modes, axis=1), jnp.stack(loads, axis=1)
 
 
 def on_device(start_disp, bone_mask, density, load_nodes, load_forces):
-    stiffness = jnp.asarray(hex_stiffness(), jnp.float32)
+    stiffness = mode_stiffness()
     modulus = bone_mask.astype(jnp.float32) * density * density
     case_count = start_disp.shape[0]
     size_x = start_disp.shape[2]
@@ -296,18 +343,18 @@
         shape = [1, 1, 1]
         shape[dim] = extent
         blur_mass = blur_mass * kept.reshape(shape)
-    start_elems = start_elems[:, :, 2:-1, 2:-1]
-    start_loads = start_loads[:, :, 2:-1, 2:-1]
-    residual_elems = residual_elems[:, :, 1:, 1:]
-    residual_loads = residual_loads[:, :, 1:, 1:]
-    start_energy = jnp.sum(start_elems * start_loads * blur_mass, axis=(1, 2, 3, 4))
+    start_elems = start_elems[:, :, :, 2:-1, 2:-1]
+    start_loads = start_loads[:, :, :, 2:-1, 2:-1]
+    residual_elems = residual_elems[:, :, :, 1:, 1:]
+    residual_loads = residual_loads[:, :, :, 1:, 1:]
+    start_energy = jnp.sum(start_elems * start_loads * blur_mass, axis=(1, 2, 3, 4, 5))
     start_weighted = start_loads * blur_mass
     residual_weighted = residual_loads * blur_mass
     cross_energy = jnp.sum(
-        residual_elems[:, None] * start_weighted[None, :], axis=(2, 3, 4, 5)
+        residual_elems[:, None] * start_weighted[None, :], axis=(2, 3, 4, 5, 6)
     )
     residual_energy = jnp.sum(
-        residual_elems[:, None] * residual_weighted[None, :], axis=(2, 3, 4, 5)
+        residual_elems[:, None] * residual_weighted[None, :], axis=(2, 3, 4, 5, 6)
     )
     grams = tree_sum(
         jnp.stack(
@@ -331,7 +378,11 @@
     node_field = start_nodes[:, :, 2:-1, 2:-1] + mix_cases(
         residual_nodes[:, :, 1:, 1:], step_alpha
     )
-    energy = element_energy(node_field, stiffness)
+    final_modes = corner_modes(node_field)
+    final_loads = mode_loads(final_modes, stiffness)
+    energy = sum(
+        jnp.sum(part * load, axis=(0, 1)) for part, load in zip(final_modes, final_loads)
+    )
     stimulus = modulus * energy
     smooth = blur_valid(with_halo(stimulus, (("gx", 0),), 4), 0, size_x)
     smooth = blur_valid(with_halo(smooth, (("gy", 1),), 4), 1, size_y)

time: 130 us -> 133 us (1.023)
  other arithmetic: 15.8 us -> 34.1 us
  matrix products: 21.3 us -> 5.85 us
    dot_general x3 -> x0, matrix products: 15.2 us -> none  [the longest x2 10.2 us: node_forces(): jnp.einsum('ij,cjabd->ciabd', stiffness, local_disp, precision=highest)]
    sub x0 -> x19, other arithmetic: none -> 10.4 us  [the longest x14 8.85 us: modes_to_nodes(): merged[key] = jnp.pad(total - change, low) + jnp.pad(total + change, high)]
    unnamed x38 -> x43, local copies, waits for them, and re-layouts: 5.99 us -> 11.1 us
    unnamed x0 -> x28, other arithmetic: none -> 4.82 us
    reshape x3 -> x0, local copies, waits for them, and re-layouts: 3.41 us -> none  [the longest x2 2.31 us: node_forces(): (local_load * modulus).reshape((node_field.shape[0], 8, 3) + modulus.shape)]
    add x0 -> x15, other arithmetic: none -> 2.72 us  [the longest x9 1.85 us: mode_loads(): total = term if total is None else total + term]
    ppermute x2, waiting for transfers between devices: 5.26 us -> 3.66 us  [halo_both(): above = lax.ppermute(head, axis, [(i + 1, i) for i in range(count - 1)])]
    reduce_sum x1 -> x7, other arithmetic: 2.62 us -> 3.97 us  [the longest x1 3.09 us: on_device(): jnp.sum(start_elems * start_loads * blur_mass, axis=(1, 2, 3, 4, 5))]
  transfers between devices with their start and end apart: 8 -> 8, of which waited for: 5 -> 4; matrix products, arithmetic and copies ran while one was open for 3% -> 3% of each run, Pallas kernels for 0% -> 0%
where the time goes in v4:
time: 133 us; the launch traced here: 132 us
  other arithmetic  34.1 us (26%)
  starting transfers between devices  31.4 us (24%)
  blocking collectives  30.6 us (23%)
  local copies, waits for them, and re-layouts  17.1 us (13%)
  waiting for transfers between devices  9.4 us (7%)
  matrix products  5.85 us (4%)
  between operations  3.49 us (3%)
    all_to_all x2, blocking collectives, tree_sum(): value = jnp.sum(lax.all_to_all(copies, axis, 0, 0, tiled=False), axis=0)  30.6 us
    unnamed x43, local copies, waits for them, and re-layouts  11.1 us
    ppermute x2, starting transfers between devices, halo_both(): above = lax.ppermute(head, axis, [(i + 1, i) for i in range(count - 1)])  10.5 us
    sub x14, other arithmetic, modes_to_nodes(): merged[key] = jnp.pad(total - change, low) + jnp.pad(total + change, high)  8.85 us
    ppermute x2, starting transfers between devices, halo_both(): below = lax.ppermute(tail, axis, [(i, i + 1) for i in range(count - 1)])  8.64 us
    ppermute x2, starting transfers between devices, with_halo(): lax.ppermute(tail, axis, [(i, (i + 1) % count) for i in range(ends)])  7.1 us
    ppermute x2, starting transfers between devices, with_halo(): lax.ppermute(head, axis, [((i + 1) % count, i) for i in range(ends)])  5.19 us
    unnamed x28, other arithmetic  4.82 us
  transfers between devices with their start and end apart: 8, of which 4 were waited for; matrix products, arithmetic and copies ran while one was open for 3% of the time, Pallas kernels for 0%

profile of v4, /device:TPU:3, one launch (start us, length us, event | category | flops | bytes accessed | tf_op | source)
XLA Modules:
  0.0 132.1 jit_solution(10315393323731171162)
XLA Ops:
  0.7 0.7 dynamic_slice.6
  1.4 0.7 dynamic_slice.7
  2.1 0.7 copy.130
  2.8 0.9 convolution_bitcast_fusion
  3.8 0.8 multiply_multiply_fusion.1
  4.8 1.1 copy.87
  6.1 4.0 %collective-permute-start = (f32[20,2,8,128]{3,1,2,0:T(2,128)S(1)}, f32[20,2,8,128]{3,1,2,0:T(2,128)S(1)}, u32[]{:S(2)}, u32[]{:S(2)}) collective-permute-start(f32[20,2,8,128]{3,1,2,0:T(2,128)S(1)} %get-tuple-element.154), channel_id=1, source_target_pairs={{0,16},{16,32},{32,48},{48,64},{64,80},{80,96},{96,112},{112,128},... | collective-permute-start | bytes 491528 | tf_op jit(solution)/shard_map/ppermute | solution.py:263
  10.1 8.6 %collective-permute-start.1 = (f32[20,2,8,128]{3,1,2,0:T(2,128)S(1)}, f32[20,2,8,128]{3,1,2,0:T(2,128)S(1)}, u32[]{:S(2)}, u32[]{:S(2)}) collective-permute-start(f32[20,2,8,128]{3,1,2,0:T(2,128)S(1)} %get-tuple-element.155), channel_id=1, source_target_pairs={{16,0},{32,16},{48,32},{64,48},{80,64},{96,80},{112,96},{128,112},... | collective-permute-start | bytes 491528 | tf_op jit(solution)/shard_map/ppermute | solution.py:264
  18.8 1.9 %collective-permute-done = f32[20,2,8,128]{3,1,2,0:T(2,128)S(1)} collective-permute-done((f32[20,2,8,128]{3,1,2,0:T(2,128)S(1)}, f32[20,2,8,128]{3,1,2,0:T(2,128)S(1)}, u32[]{:S(2)}, u32[]{:S(2)}) %collective-permute-start) | collective-permute-done | bytes 163872 | tf_op jit(solution)/shard_map/ppermute | solution.py:263
  20.7 0.9 collective-permute-done.1
  21.6 4.6 %collective-permute-start.2 = (f32[20,8,2,128]{3,1,2,0:T(8,128)S(1)}, f32[20,8,2,128]{3,1,2,0:T(8,128)S(1)}, u32[]{:S(2)}, u32[]{:S(2)}) collective-permute-start(f32[20,8,2,128]{3,1,2,0:T(8,128)S(1)} %get-tuple-element.144), channel_id=1, source_target_pairs={{0,1},{1,2},{2,3},{3,4},{4,5},{5,6},{6,7},{7,8},{8,9},{9,10},{10,1... | collective-permute-start | bytes 491528 | tf_op jit(solution)/shard_map/ppermute | solution.py:263
  26.3 1.9 %collective-permute-start.3 = (f32[20,8,2,128]{3,1,2,0:T(8,128)S(1)}, f32[20,8,2,128]{3,1,2,0:T(8,128)S(1)}, u32[]{:S(2)}, u32[]{:S(2)}) collective-permute-start(f32[20,8,2,128]{3,1,2,0:T(8,128)S(1)} %get-tuple-element.145), channel_id=1, source_target_pairs={{1,0},{2,1},{3,2},{4,3},{5,4},{6,5},{7,6},{8,7},{9,8},{10,9},{11,1... | collective-permute-start | bytes 491528 | tf_op jit(solution)/shard_map/ppermute | solution.py:264
  28.2 0.9 broadcast_dynamic-update-slice_fusion.1
  29.1 1.0 broadcast_dynamic-update-slice_fusion
  30.1 2.8 %collective-permute-done.3 = f32[20,8,2,128]{3,1,2,0:T(8,128)S(1)} collective-permute-done((f32[20,8,2,128]{3,1,2,0:T(8,128)S(1)}, f32[20,8,2,128]{3,1,2,0:T(8,128)S(1)}, u32[]{:S(2)}, u32[]{:S(2)}) %collective-permute-start.3) | collective-permute-done | bytes 163872 | tf_op jit(solution)/shard_map/ppermute | solution.py:264
  34.0 1.0 copy.95
  40.1 1.1 fusion.7
  41.4 1.1 fusion.5
  42.5 0.7 fusion.17
  44.0 1.0 fusion.9
  49.0 0.7 slice-done
  50.2 1.2 multiply_subtract_fusion.5
  51.5 1.1 multiply_subtract_fusion.7
  52.7 1.1 multiply_subtract_fusion.4
  55.0 3.0 %copy-done = f32[6,8,3,7,11,128]{5,0,4,3,2,1:T(8,128)} copy-done((f32[6,8,3,7,11,128]{5,0,4,3,2,1:T(8,128)}, f32[6,8,3,7,11,128]{5,0,4,3,2,1:T(8,128)S(1)}, u32[]{:S(2)}) %copy-start) | copy-done | bytes 5677080
  58.0 3.1 %fusion.1 = (f32[6]{0:T(128)S(1)}, f32[6,8,3,4,8,128]{5,0,4,3,2,1:T(8,128)S(1)}, f32[6,8,3,4,8,128]{5,0,4,3,2,1:T(8,128)S(1)}) fusion(f32[6,8,3,7,11,128]{5,0,4,3,2,1:T(8,128)S(1)} %get-tuple-element.17, f32[6,8,3,7,11,128]{5,0,4,3,2,1:T(8,128)} %copy-done, f32[4,8,128]{2,1,0:T(8,128)S(1)} %get-tuple-element.160, ...), kind=kLoop, calls=%fused_computation.7 | loop fusion | flops 2949114 | bytes 11812888 | tf_op jit(solution)/shard_map/reduce_sum | solution.py:350
  62.8 0.6 fusion.13
  64.3 0.7 fusion.15
  65.4 1.0 fusion.8
  66.4 3.0 %multiply_reduce_fusion = (f32[6,6]{1,0:T(8,128)S(1)}, f32[6,6]{1,0:T(8,128)S(1)}) fusion(f32[6,8,3,4,8,128]{5,4,3,2,1,0:T(8,128)S(1)} %copy.100, f32[6,8,3,4,8,128]{5,4,3,2,1,0:T(8,128)S(1)} %copy.98, f32[6,8,3,4,8,128]{5,4,3,2,1,0:T(8,128)S(1)} %copy.99), kind=kLoop, calls=%fused_computation | loop fusion | flops 14155704 | bytes 7078176 | tf_op jit(solution)/shard_map/reduce_sum | solution.py:356
  69.7 14.6 %all_to_all.10 = f32[16,1,180]{2,1,0:T(1,128)S(1)} all-to-all(f32[16,1,180]{2,1,0:T(1,128)S(1)} %reshape.127), channel_id=1, replica_groups=mesh['gx'=32,'gy'=16] {'gy'}, dimensions={0} | all-to-all | bytes 23040 | tf_op jit(solution)/shard_map/all_to_all | solution.py:149
  84.8 0.7 reduce.7
  86.0 16.1 %all_to_all.11 = f32[32,1,180]{2,1,0:T(1,128)S(1)} all-to-all(f32[32,1,180]{2,1,0:T(1,128)S(1)} %reshape.129), channel_id=1, replica_groups=mesh['gx'=32,'gy'=16] {'gx'}, dimensions={0} | all-to-all | bytes 46080 | tf_op jit(solution)/shard_map/all_to_all | solution.py:149
  102.1 0.7 reduce.8
  103.1 0.6 slice_bitcast_fusion
  104.4 0.6 compare_reduce_fusion
  105.0 0.6 fusion.106
  106.4 0.8 fusion.108
  107.2 1.3 convolution_add_fusion
  110.9 3.3 %collective-permute-start.5 = (f32[4,8,128]{2,1,0:T(8,128)S(1)}, f32[4,8,128]{2,1,0:T(8,128)S(1)}, u32[]{:S(2)}, u32[]{:S(2)}) collective-permute-start(f32[4,8,128]{2,1,0:T(8,128)S(1)} %add_multiply_fusion), channel_id=1, source_target_pairs={{16,0},{32,16},{48,32},{64,48},{80,64},{96,80},{112,96},{128,112},... | collective-permute-start | bytes 49160 | tf_op jit(solution)/shard_map/ppermute | solution.py:31
  114.2 2.0 %collective-permute-start.4 = (f32[4,8,128]{2,1,0:T(8,128)S(1)}, f32[4,8,128]{2,1,0:T(8,128)S(1)}, u32[]{:S(2)}, u32[]{:S(2)}) collective-permute-start(f32[4,8,128]{2,1,0:T(8,128)S(1)} %add_multiply_fusion), channel_id=1, source_target_pairs={{0,16},{16,32},{32,48},{48,64},{64,80},{80,96},{96,112},{112,128},... | collective-permute-start | bytes 49160 | tf_op jit(solution)/shard_map/ppermute | solution.py:29
  116.2 0.7 convolution_add_fusion.1
  116.9 3.9 %collective-permute-done.4 = f32[4,8,128]{2,1,0:T(8,128)S(1)} collective-permute-done((f32[4,8,128]{2,1,0:T(8,128)S(1)}, f32[4,8,128]{2,1,0:T(8,128)S(1)}, u32[]{:S(2)}, u32[]{:S(2)}) %collective-permute-start.4) | collective-permute-done | bytes 16416 | tf_op jit(solution)/shard_map/ppermute | solution.py:29
  120.8 5.1 %collective-permute-start.6 = (f32[4,4,128]{2,1,0:T(4,128)S(1)}, f32[4,4,128]{2,1,0:T(4,128)S(1)}, u32[]{:S(2)}, u32[]{:S(2)}) collective-permute-start(f32[4,4,128]{2,1,0:T(4,128)S(1)} %get-tuple-element.165), channel_id=1, source_target_pairs={{0,1},{1,2},{2,3},{3,4},{4,5},{5,6},{6,7},{7,8},{8,9},{9,10},{10,1... | collective-permute-start | bytes 24584 | tf_op jit(solution)/shard_map/ppermute | solution.py:29
  125.9 1.9 %collective-permute-start.7 = (f32[4,4,128]{2,1,0:T(4,128)S(1)}, f32[4,4,128]{2,1,0:T(4,128)S(1)}, u32[]{:S(2)}, u32[]{:S(2)}) collective-permute-start(f32[4,4,128]{2,1,0:T(4,128)S(1)} %get-tuple-element.166), channel_id=1, source_target_pairs={{1,0},{2,1},{3,2},{4,3},{5,4},{6,5},{7,6},{8,7},{9,8},{10,9},{11,1... | collective-permute-start | bytes 24584 | tf_op jit(solution)/shard_map/ppermute | solution.py:31
  127.8 0.7 multiply_reduce_fusion.3
  128.5 0.8 copy.108
  131.3 0.7 multiply_minimum_fusion
  (153 shorter events, 21.7 us)
Async XLA Ops:
  0.6 18.1 %copy-start.11 = (s32[10]{0:T(128)S(1)}, s32[10]{0:T(128)}, u32[]{:S(2)}) copy-start(s32[10]{0:T(128)} %constant.141.clone) | copy-start | bytes 124
  0.6 18.1 %copy-start.10 = (s32[6]{0:T(128)S(1)}, s32[6]{0:T(128)}, u32[]{:S(2)}) copy-start(s32[6]{0:T(128)} %constant.140.clone) | copy-start | bytes 76
  6.1 14.6 %collective-permute-start = (f32[20,2,8,128]{3,1,2,0:T(2,128)S(1)}, f32[20,2,8,128]{3,1,2,0:T(2,128)S(1)}, u32[]{:S(2)}, u32[]{:S(2)}) collective-permute-start(f32[20,2,8,128]{3,1,2,0:T(2,128)S(1)} %get-tuple-element.154), channel_id=1, source_target_pairs={{0,16},{16,32},{32,48},{48,64},{64,80},{80,96},{96,112},{112,128},... | collective-permute-start | bytes 491528 | tf_op jit(solution)/shard_map/ppermute | solution.py:263
  10.1 11.4 %collective-permute-start.1 = (f32[20,2,8,128]{3,1,2,0:T(2,128)S(1)}, f32[20,2,8,128]{3,1,2,0:T(2,128)S(1)}, u32[]{:S(2)}, u32[]{:S(2)}) collective-permute-start(f32[20,2,8,128]{3,1,2,0:T(2,128)S(1)} %get-tuple-element.155), channel_id=1, source_target_pairs={{16,0},{32,16},{48,32},{64,48},{80,64},{96,80},{112,96},{128,112},... | collective-permute-start | bytes 491528 | tf_op jit(solution)/shard_map/ppermute | solution.py:264
  21.6 8.5 %collective-permute-start.2 = (f32[20,8,2,128]{3,1,2,0:T(8,128)S(1)}, f32[20,8,2,128]{3,1,2,0:T(8,128)S(1)}, u32[]{:S(2)}, u32[]{:S(2)}) collective-permute-start(f32[20,8,2,128]{3,1,2,0:T(8,128)S(1)} %get-tuple-element.144), channel_id=1, source_target_pairs={{0,1},{1,2},{2,3},{3,4},{4,5},{5,6},{6,7},{7,8},{8,9},{9,10},{10,1... | collective-permute-start | bytes 491528 | tf_op jit(solution)/shard_map/ppermute | solution.py:263
  26.3 6.6 %collective-permute-start.3 = (f32[20,8,2,128]{3,1,2,0:T(8,128)S(1)}, f32[20,8,2,128]{3,1,2,0:T(8,128)S(1)}, u32[]{:S(2)}, u32[]{:S(2)}) collective-permute-start(f32[20,8,2,128]{3,1,2,0:T(8,128)S(1)} %get-tuple-element.145), channel_id=1, source_target_pairs={{1,0},{2,1},{3,2},{4,3},{5,4},{6,5},{7,6},{8,7},{9,8},{10,9},{11,1... | collective-permute-start | bytes 491528 | tf_op jit(solution)/shard_map/ppermute | solution.py:264
  47.5 2.2 %slice-start = ((s8[4423680]{0:T(1024)(128)(4,1)}), s8[4194304]{0:T(1024)(128)(4,1)S(1)}, s32[]{:S(2)}) async-start(s8[4423680]{0:T(1024)(128)(4,1)} %bitcast.147), calls=%async_computation.2 | async-start | bytes 8388608
  48.0 1.9 %slice-start.1 = ((s8[4423680]{0:T(1024)(128)(4,1)}), s8[229376]{0:T(1024)(128)(4,1)S(1)}, s32[]{:S(2)}) async-start(s8[4423680]{0:T(1024)(128)(4,1)} %bitcast.147), calls=%async_computation.3 | async-start | bytes 458752
  49.9 4.0 %slice-start.2 = ((s8[7569408]{0:T(1024)(128)(4,1)}), s8[4194304]{0:T(1024)(128)(4,1)S(1)}, s32[]{:S(2)}) async-start(s8[7569408]{0:T(1024)(128)(4,1)} %bitcast.149), calls=%async_computation.4 | async-start | bytes 8388608
  51.5 2.8 %slice-start.3 = ((s8[7569408]{0:T(1024)(128)(4,1)}), s8[3375104]{0:T(1024)(128)(4,1)S(1)}, s32[]{:S(2)}) async-start(s8[7569408]{0:T(1024)(128)(4,1)} %bitcast.149), calls=%async_computation.5 | async-start | bytes 6750208
  55.0 3.0 %copy-start = (f32[6,8,3,7,11,128]{5,0,4,3,2,1:T(8,128)}, f32[6,8,3,7,11,128]{5,0,4,3,2,1:T(8,128)S(1)}, u32[]{:S(2)}) copy-start(f32[6,8,3,7,11,128]{5,0,4,3,2,1:T(8,128)S(1)} %bitcast_dynamic-update-slice_fusion.8) | copy-start | bytes 17031172
  61.5 1.1 copy-start.3
  61.6 1.2 copy-start.4
  62.8 1.1 copy-start.1
  62.8 1.2 copy-start.2
  62.8 1.4 %copy-start.5 = (f32[6,3,5,9,128]{4,0,3,2,1:T(8,128)S(1)}, f32[6,3,5,9,128]{4,0,3,2,1:T(8,128)}, u32[]{:S(2)}) copy-start(f32[6,3,5,9,128]{4,0,3,2,1:T(8,128)} %get-tuple-element.101) | copy-start | bytes 1244164
  62.8 1.5 %copy-start.6 = (f32[6,3,5,9,128]{4,0,3,2,1:T(8,128)S(1)}, f32[6,3,5,9,128]{4,0,3,2,1:T(8,128)}, u32[]{:S(2)}) copy-start(f32[6,3,5,9,128]{4,0,3,2,1:T(8,128)} %get-tuple-element.102) | copy-start | bytes 1244164
  110.2 0.7 copy-start.8
  110.2 0.7 copy-start.9
  110.3 5.9 %copy-start.7 = (f32[6,3,4,8,128]{4,3,2,1,0:T(8,128)S(1)}, f32[6,3,4,8,128]{4,3,2,1,0:T(8,128)}, u32[]{:S(2)}) copy-start(f32[6,3,4,8,128]{4,3,2,1,0:T(8,128)} %param.10) | copy-start | bytes 884740
  110.9 6.0 %collective-permute-start.5 = (f32[4,8,128]{2,1,0:T(8,128)S(1)}, f32[4,8,128]{2,1,0:T(8,128)S(1)}, u32[]{:S(2)}, u32[]{:S(2)}) collective-permute-start(f32[4,8,128]{2,1,0:T(8,128)S(1)} %add_multiply_fusion), channel_id=1, source_target_pairs={{16,0},{32,16},{48,32},{64,48},{80,64},{96,80},{112,96},{128,112},... | collective-permute-start | bytes 49160 | tf_op jit(solution)/shard_map/ppermute | solution.py:31
  114.2 6.6 %collective-permute-start.4 = (f32[4,8,128]{2,1,0:T(8,128)S(1)}, f32[4,8,128]{2,1,0:T(8,128)S(1)}, u32[]{:S(2)}, u32[]{:S(2)}) collective-permute-start(f32[4,8,128]{2,1,0:T(8,128)S(1)} %add_multiply_fusion), channel_id=1, source_target_pairs={{0,16},{16,32},{32,48},{48,64},{64,80},{80,96},{96,112},{112,128},... | collective-permute-start | bytes 49160 | tf_op jit(solution)/shard_map/ppermute | solution.py:29
  120.8 10.5 %collective-permute-start.6 = (f32[4,4,128]{2,1,0:T(4,128)S(1)}, f32[4,4,128]{2,1,0:T(4,128)S(1)}, u32[]{:S(2)}, u32[]{:S(2)}) collective-permute-start(f32[4,4,128]{2,1,0:T(4,128)S(1)} %get-tuple-element.165), channel_id=1, source_target_pairs={{0,1},{1,2},{2,3},{3,4},{4,5},{5,6},{6,7},{7,8},{8,9},{9,10},{10,1... | collective-permute-start | bytes 24584 | tf_op jit(solution)/shard_map/ppermute | solution.py:29
  125.9 5.4 %collective-permute-start.7 = (f32[4,4,128]{2,1,0:T(4,128)S(1)}, f32[4,4,128]{2,1,0:T(4,128)S(1)}, u32[]{:S(2)}, u32[]{:S(2)}) collective-permute-start(f32[4,4,128]{2,1,0:T(4,128)S(1)} %get-tuple-element.166), channel_id=1, source_target_pairs={{1,0},{2,1},{3,2},{4,3},{5,4},{6,5},{7,6},{8,7},{9,8},{10,9},{11,1... | collective-permute-start | bytes 24584 | tf_op jit(solution)/shard_map/ppermute | solution.py:31

commit v5 on v3

--- a/solution.py
+++ b/solution.py
@@ -202,6 +202,43 @@
     return jnp.concatenate([kept[:, :, :1] + to_x, kept[:, :, 1:]], axis=2)
 
 
+def corner_modes(node_field):
+    found = {(): node_field}
+    for dim in (2, 3, 4):
+        grown = {}
+        for key, cells in found.items():
+            low = lax.slice_in_dim(cells, 0, cells.shape[dim] - 1, axis=dim)
+            high = lax.slice_in_dim(cells, 1, cells.shape[dim], axis=dim)
+            grown[key + (0,)] = high + low
+            grown[key + (1,)] = high - low
+        found = grown
+    return [found[(mode // 4, mode // 2 % 2, mode % 2)] for mode in range(8)]
+
+
+def mode_stiffness():
+    step = np.array([[1.0, 1.0], [-1.0, 1.0]])
+    change = np.kron(np.kron(np.kron(step, step), step), np.eye(3))
+    return change @ hex_stiffness() @ change.T / 64.0
+
+
+def mode_loads(modes, table):
+    loads = []
+    for mode in range(8):
+        parts = []
+        for comp in range(3):
+            total = None
+            for other in range(3):
+                source = mode ^ (4 >> comp) ^ (4 >> other)
+                weight = float(table[3 * mode + comp, 3 * source + other])
+                if abs(weight) < 1e-12:
+                    continue
+                term = weight * modes[source][:, other]
+                total = term if total is None else total + term
+            parts.append(jnp.zeros_like(modes[mode][:, comp]) if total is None else total)
+        loads.append(jnp.stack(parts, axis=1))
+    return loads
+
+
 def halo_both(cells, axis, dim, width):
     count = lax.axis_size(axis)
     head = lax.slice_in_dim(cells, 0, width, axis=dim)
@@ -327,13 +364,14 @@
         + jnp.sum(step_alpha[:, None, :] * grams[3][:, :, None] * step_alpha[None, :, :])
     )
     solution = start_disp + mix_cases(residual, step_alpha)
-    final_elems = start_elems + jnp.sum(
-        residual_elems[:, None] * step_alpha[:, :, None, None, None, None], axis=0
-    )
-    final_loads = start_loads + jnp.sum(
-        residual_loads[:, None] * step_alpha[:, :, None, None, None, None], axis=0
-    )
-    energy = jnp.sum(final_elems * final_loads, axis=(0, 1))
+    node_field = start_nodes[:, :, 2:-1, 2:-1] + mix_cases(
+        residual_nodes[:, :, 1:, 1:], step_alpha
+    )
+    final_modes = corner_modes(node_field)
+    final_loads = mode_loads(final_modes, mode_stiffness())
+    energy = sum(
+        jnp.sum(part * load, axis=(0, 1)) for part, load in zip(final_modes, final_loads)
+    )
     stimulus = modulus * energy
     smooth = blur_valid(with_halo(stimulus, (("gx", 0),), 4), 0, size_x)
     smooth = blur_valid(with_halo(smooth, (("gy", 1),), 4), 1, size_y)

time: 148 us -> 125 us (0.84)
  local copies, waits for them, and re-layouts: 31.3 us -> 14.5 us
  blocking collectives: 14.6 us -> 30.6 us
  other arithmetic: 28.8 us -> 18.3 us
  starting transfers between devices: 39.9 us -> 31.4 us
  waiting for transfers between devices: 14.3 us -> 10 us
    all_to_all x1 -> x2, blocking collectives: 14.6 us -> 30.6 us  [tree_sum(): value = jnp.sum(lax.all_to_all(copies, axis, 0, 0, tiled=False), axis=0)]
    unnamed x33 -> x31, local copies, waits for them, and re-layouts: 14.1 us -> 5.35 us
    all_to_all x1 -> x0, starting transfers between devices: 8.49 us -> none  [tree_sum(): value = jnp.sum(lax.all_to_all(copies, axis, 0, 0, tiled=False), axis=0)]
    reduce_sum x2 -> x7, other arithmetic: 10.1 us -> 3.49 us  [the longest x1 2.62 us: on_device(): jnp.sum(start_elems * start_loads * blur_mass, axis=(1, 2, 3, 4))]
    all_to_all x1 -> x0, waiting for transfers between devices: 4.24 us -> none  [tree_sum(): value = jnp.sum(lax.all_to_all(copies, axis, 0, 0, tiled=False), axis=0)]
    another operation x3 -> x2, local copies, waits for them, and re-layouts: 4.68 us -> 0.52 us  [cases_disp(): jnp.stack(corners, axis=1)]
    slice x1 -> x0, other arithmetic: 3.9 us -> none  [on_device(): residual_loads = residual_loads[:, :, 1:, 1:]]
    slice x2 -> x0, local copies, waits for them, and re-layouts: 3.63 us -> none  [the longest x1 3.56 us: on_device(): residual_loads = residual_loads[:, :, 1:, 1:]]
  transfers between devices with their start and end apart: 9 -> 8, of which waited for: 6 -> 5; matrix products, arithmetic and copies ran while one was open for 5% -> 3% of each run, Pallas kernels for 0% -> 0%
where the time goes in v5:
time: 125 us; the launch traced here: 124 us
  starting transfers between devices  31.4 us (25%)
  blocking collectives  30.6 us (24%)
  other arithmetic  18.3 us (15%)
  matrix products  16.3 us (13%)
  local copies, waits for them, and re-layouts  14.5 us (12%)
  waiting for transfers between devices  10 us (8%)
  between operations  3.23 us (3%)
    all_to_all x2, blocking collectives, tree_sum(): value = jnp.sum(lax.all_to_all(copies, axis, 0, 0, tiled=False), axis=0)  30.6 us
    ppermute x2, starting transfers between devices, halo_both(): above = lax.ppermute(head, axis, [(i + 1, i) for i in range(count - 1)])  10.5 us
    dot_general x2, matrix products, node_forces(): jnp.einsum('ij,cjabd->ciabd', stiffness, local_disp, precision=highest)  10.2 us
    ppermute x2, starting transfers between devices, halo_both(): below = lax.ppermute(tail, axis, [(i, i + 1) for i in range(count - 1)])  8.64 us
    ppermute x2, starting transfers between devices, with_halo(): lax.ppermute(tail, axis, [(i, (i + 1) % count) for i in range(ends)])  7.1 us
    unnamed x31, local copies, waits for them, and re-layouts  5.35 us
    ppermute x2, waiting for transfers between devices, halo_both(): above = lax.ppermute(head, axis, [(i + 1, i) for i in range(count - 1)])  5.26 us
    ppermute x2, starting transfers between devices, with_halo(): lax.ppermute(head, axis, [((i + 1) % count, i) for i in range(ends)])  5.19 us
  transfers between devices with their start and end apart: 8, of which 5 were waited for; matrix products, arithmetic and copies ran while one was open for 3% of the time, Pallas kernels for 0%

profile of v5, /device:TPU:3, one launch (start us, length us, event | category | flops | bytes accessed | tf_op | source)
XLA Modules:
  0.0 124.3 jit_solution(2675180617326569660)
XLA Ops:
  0.7 0.7 copy.256
  1.4 0.9 convolution_bitcast_fusion.1
  2.4 0.8 multiply_multiply_fusion.1
  3.4 1.1 copy.172
  4.7 4.0 %collective-permute-start = (f32[20,2,8,128]{3,1,2,0:T(2,128)S(1)}, f32[20,2,8,128]{3,1,2,0:T(2,128)S(1)}, u32[]{:S(2)}, u32[]{:S(2)}) collective-permute-start(f32[20,2,8,128]{3,1,2,0:T(2,128)S(1)} %get-tuple-element.68), channel_id=1, source_target_pairs={{0,16},{16,32},{32,48},{48,64},{64,80},{80,96},{96,112},{112,128},... | collective-permute-start | bytes 491528 | tf_op jit(solution)/shard_map/ppermute | solution.py:246
  8.7 8.6 %collective-permute-start.1 = (f32[20,2,8,128]{3,1,2,0:T(2,128)S(1)}, f32[20,2,8,128]{3,1,2,0:T(2,128)S(1)}, u32[]{:S(2)}, u32[]{:S(2)}) collective-permute-start(f32[20,2,8,128]{3,1,2,0:T(2,128)S(1)} %get-tuple-element.69), channel_id=1, source_target_pairs={{16,0},{32,16},{48,32},{64,48},{80,64},{96,80},{112,96},{128,112},... | collective-permute-start | bytes 491528 | tf_op jit(solution)/shard_map/ppermute | solution.py:247
  17.2 0.7 and_convert_fusion.1
  17.9 0.7 and_convert_fusion
  18.6 0.7 collective-permute-done
  19.2 0.9 collective-permute-done.1
  20.2 4.6 %collective-permute-start.2 = (f32[20,8,2,128]{3,1,2,0:T(8,128)S(1)}, f32[20,8,2,128]{3,1,2,0:T(8,128)S(1)}, u32[]{:S(2)}, u32[]{:S(2)}) collective-permute-start(f32[20,8,2,128]{3,1,2,0:T(8,128)S(1)} %get-tuple-element.63), channel_id=1, source_target_pairs={{0,1},{1,2},{2,3},{3,4},{4,5},{5,6},{6,7},{7,8},{8,9},{9,10},{10,1... | collective-permute-start | bytes 491528 | tf_op jit(solution)/shard_map/ppermute | solution.py:246
  24.8 1.9 %collective-permute-start.3 = (f32[20,8,2,128]{3,1,2,0:T(8,128)S(1)}, f32[20,8,2,128]{3,1,2,0:T(8,128)S(1)}, u32[]{:S(2)}, u32[]{:S(2)}) collective-permute-start(f32[20,8,2,128]{3,1,2,0:T(8,128)S(1)} %get-tuple-element.64), channel_id=1, source_target_pairs={{1,0},{2,1},{3,2},{4,3},{5,4},{6,5},{7,6},{8,7},{9,8},{10,9},{11,1... | collective-permute-start | bytes 491528 | tf_op jit(solution)/shard_map/ppermute | solution.py:247
  27.1 4.4 %collective-permute-done.3 = f32[20,8,2,128]{3,1,2,0:T(8,128)S(1)} collective-permute-done((f32[20,8,2,128]{3,1,2,0:T(8,128)S(1)}, f32[20,8,2,128]{3,1,2,0:T(8,128)S(1)}, u32[]{:S(2)}, u32[]{:S(2)}) %collective-permute-start.3) | collective-permute-done | bytes 163872 | tf_op jit(solution)/shard_map/ppermute | solution.py:247
  32.0 0.5 copy.175
  32.5 1.0 copy.194
  35.1 1.1 copy.181
  36.2 7.0 %broadcast_multiply_fusion = (f32[6,24,7,11,128]{4,1,3,2,0:T(8,128)S(1)}, f32[6,24,7,11,128]{4,1,3,2,0:T(8,128)}) fusion(f32[7,11,128]{2,1,0:T(8,128)S(1)} %copy.182, f32[6,24,7,11,128]{4,1,3,2,0:T(8,128)S(1)} %copy.181, f32[24,24,1,1,1]{1,0,4,3,2:T(8,128)S(1)} %copy-done.3), kind=kOutput, calls=%fused_computation.9 | convolution fusion | flops 410167296 | bytes 17072896 | tf_op jit(solution)/shard_map/ij,cjabd->ciabd/dot_general | solution.py:259
  43.2 1.5 %copy.223 = f32[6,24,7,11,128]{4,0,3,2,1:T(8,128)S(1)} copy(f32[6,24,7,11,128]{4,1,3,2,0:T(8,128)S(1)} %get-tuple-element.78) | data formatting | bytes 11354112 | tf_op jit(solution)/shard_map/reshape | solution.py:260
  44.6 0.5 slice_bitcast_fusion.5
  45.1 0.9 fusion.28
  46.7 1.0 fusion.8
  49.2 0.5 copy.205
  49.6 3.2 %broadcast_multiply_fusion.1 = (f32[6,24,5,9,128]{4,1,3,2,0:T(8,128)S(1)}, f32[6,24,5,9,128]{4,1,3,2,0:T(8,128)S(1)}) fusion(f32[5,9,128]{2,1,0:T(8,128)S(1)} %copy.196, f32[24,24,1,1,1]{1,0,4,3,2:T(8,128)S(1)} %copy-done.3, f32[6,24,5,9,128]{4,0,3,2,1:T(8,128)S(1)} %bitcast.204), kind=kOutput, calls=%fused_computation.24 | convolution fusion | flops 239708160 | bytes 9978624 | tf_op jit(solution)/shard_map/ij,cjabd->ciabd/dot_general | solution.py:259
  52.8 0.9 copy.234
  54.0 2.6 %fusion.3 = (f32[6]{0:T(128)S(1)}, f32[6,24,4,8,128]{4,1,3,2,0:T(8,128)S(1)}, f32[6,24,4,8,128]{4,1,3,2,0:T(8,128)S(1)}) fusion(f32[6,24,7,11,128]{4,1,3,2,0:T(8,128)S(1)} %copy.181, f32[6,24,7,11,128]{4,1,3,2,0:T(8,128)} %get-tuple-element.79, f32[4,8,128]{2,1,0:T(8,128)S(1)} %get-tuple-element.70, f32[6,24,5,9,128]{4,1,3,2,0:T(8,128)S(1)} %get-tuple-element.81), kind=kLoop, calls=%fused_computation.18 | loop fusion | flops 2949114 | bytes 11812888 | tf_op jit(solution)/shard_map/reduce_sum | solution.py:339
  57.5 2.9 %multiply_reduce_fusion = (f32[6,6]{1,0:T(8,128)S(1)}, f32[6,6]{1,0:T(8,128)S(1)}) fusion(f32[6,24,4,8,128]{4,3,2,1,0:T(8,128)S(1)} %copy.207, f32[6,24,4,8,128]{4,3,2,1,0:T(8,128)S(1)} %copy.205, f32[6,24,4,8,128]{4,3,2,1,0:T(8,128)S(1)} %copy.206), kind=kLoop, calls=%fused_computation | loop fusion | flops 14155704 | bytes 7078176 | tf_op jit(solution)/shard_map/reduce_sum | solution.py:345
  60.4 1.2 fusion.7
  61.9 14.6 %all_to_all.10 = f32[16,1,180]{2,1,0:T(1,128)S(1)} all-to-all(f32[16,1,180]{2,1,0:T(1,128)S(1)} %reshape.317), channel_id=1, replica_groups=mesh['gx'=32,'gy'=16] {'gy'}, dimensions={0} | all-to-all | bytes 23040 | tf_op jit(solution)/shard_map/all_to_all | solution.py:149
  76.4 0.5 broadcast.970
  76.9 0.7 reduce.7
  78.2 16.1 %all_to_all.11 = f32[32,1,180]{2,1,0:T(1,128)S(1)} all-to-all(f32[32,1,180]{2,1,0:T(1,128)S(1)} %reshape.319), channel_id=1, replica_groups=mesh['gx'=32,'gy'=16] {'gx'}, dimensions={0} | all-to-all | bytes 46080 | tf_op jit(solution)/shard_map/all_to_all | solution.py:149
  94.3 0.7 reduce.8
  95.3 0.6 slice_bitcast_fusion.24
  96.0 0.5 cholesky.15
  96.5 0.6 compare_reduce_fusion
  97.2 0.6 fusion.132
  97.8 0.5 custom-call.8
  98.5 0.8 fusion.134
  99.3 1.3 %convolution_add_fusion = f32[6,3,5,9,129]{4,0,3,2,1:T(8,128)S(1)} fusion(f32[6,3,6,10,128]{4,0,3,2,1:T(8,128)S(1)} %maximum_multiply_fusion, f32[6,3,8,12,128]{4,0,3,2,1:T(8,128)S(1)} %copy.175, f32[6,6]{1,0:T(8,128)S(1)} %get-tuple-element.83), kind=kOutput, calls=%fused_computation.27 | convolution fusion | flops 7627770 | bytes 1855800 | tf_op jit(solution)/shard_map/kabcd,kj->jabcd/dot_general | solution.py:154
  103.2 3.3 %collective-permute-start.5 = (f32[4,8,128]{2,1,0:T(8,128)S(1)}, f32[4,8,128]{2,1,0:T(8,128)S(1)}, u32[]{:S(2)}, u32[]{:S(2)}) collective-permute-start(f32[4,8,128]{2,1,0:T(8,128)S(1)} %add_multiply_fusion), channel_id=1, source_target_pairs={{16,0},{32,16},{48,32},{64,48},{80,64},{96,80},{112,96},{128,112},... | collective-permute-start | bytes 49160 | tf_op jit(solution)/shard_map/ppermute | solution.py:31
  106.5 2.0 %collective-permute-start.4 = (f32[4,8,128]{2,1,0:T(8,128)S(1)}, f32[4,8,128]{2,1,0:T(8,128)S(1)}, u32[]{:S(2)}, u32[]{:S(2)}) collective-permute-start(f32[4,8,128]{2,1,0:T(8,128)S(1)} %add_multiply_fusion), channel_id=1, source_target_pairs={{0,16},{16,32},{32,48},{48,64},{64,80},{80,96},{96,112},{112,128},... | collective-permute-start | bytes 49160 | tf_op jit(solution)/shard_map/ppermute | solution.py:29
  108.5 0.7 convolution_add_fusion.1
  109.3 3.9 %collective-permute-done.4 = f32[4,8,128]{2,1,0:T(8,128)S(1)} collective-permute-done((f32[4,8,128]{2,1,0:T(8,128)S(1)}, f32[4,8,128]{2,1,0:T(8,128)S(1)}, u32[]{:S(2)}, u32[]{:S(2)}) %collective-permute-start.4) | collective-permute-done | bytes 16416 | tf_op jit(solution)/shard_map/ppermute | solution.py:29
  113.1 5.1 %collective-permute-start.6 = (f32[4,4,128]{2,1,0:T(4,128)S(1)}, f32[4,4,128]{2,1,0:T(4,128)S(1)}, u32[]{:S(2)}, u32[]{:S(2)}) collective-permute-start(f32[4,4,128]{2,1,0:T(4,128)S(1)} %get-tuple-element.75), channel_id=1, source_target_pairs={{0,1},{1,2},{2,3},{3,4},{4,5},{5,6},{6,7},{7,8},{8,9},{9,10},{10,1... | collective-permute-start | bytes 24584 | tf_op jit(solution)/shard_map/ppermute | solution.py:29
  118.2 1.9 %collective-permute-start.7 = (f32[4,4,128]{2,1,0:T(4,128)S(1)}, f32[4,4,128]{2,1,0:T(4,128)S(1)}, u32[]{:S(2)}, u32[]{:S(2)}) collective-permute-start(f32[4,4,128]{2,1,0:T(4,128)S(1)} %get-tuple-element.76), channel_id=1, source_target_pairs={{1,0},{2,1},{3,2},{4,3},{5,4},{6,5},{7,6},{8,7},{9,8},{10,9},{11,1... | collective-permute-start | bytes 24584 | tf_op jit(solution)/shard_map/ppermute | solution.py:31
  120.2 0.7 multiply_reduce_fusion.3
  120.8 0.8 copy.216
  123.6 0.7 multiply_minimum_fusion
  (89 shorter events, 10.1 us)
Async XLA Ops:
  4.7 14.6 %collective-permute-start = (f32[20,2,8,128]{3,1,2,0:T(2,128)S(1)}, f32[20,2,8,128]{3,1,2,0:T(2,128)S(1)}, u32[]{:S(2)}, u32[]{:S(2)}) collective-permute-start(f32[20,2,8,128]{3,1,2,0:T(2,128)S(1)} %get-tuple-element.68), channel_id=1, source_target_pairs={{0,16},{16,32},{32,48},{48,64},{64,80},{80,96},{96,112},{112,128},... | collective-permute-start | bytes 491528 | tf_op jit(solution)/shard_map/ppermute | solution.py:246
  8.7 11.4 %collective-permute-start.1 = (f32[20,2,8,128]{3,1,2,0:T(2,128)S(1)}, f32[20,2,8,128]{3,1,2,0:T(2,128)S(1)}, u32[]{:S(2)}, u32[]{:S(2)}) collective-permute-start(f32[20,2,8,128]{3,1,2,0:T(2,128)S(1)} %get-tuple-element.69), channel_id=1, source_target_pairs={{16,0},{32,16},{48,32},{64,48},{80,64},{96,80},{112,96},{128,112},... | collective-permute-start | bytes 491528 | tf_op jit(solution)/shard_map/ppermute | solution.py:247
  20.2 6.9 %collective-permute-start.2 = (f32[20,8,2,128]{3,1,2,0:T(8,128)S(1)}, f32[20,8,2,128]{3,1,2,0:T(8,128)S(1)}, u32[]{:S(2)}, u32[]{:S(2)}) collective-permute-start(f32[20,8,2,128]{3,1,2,0:T(8,128)S(1)} %get-tuple-element.63), channel_id=1, source_target_pairs={{0,1},{1,2},{2,3},{3,4},{4,5},{5,6},{6,7},{7,8},{8,9},{9,10},{10,1... | collective-permute-start | bytes 491528 | tf_op jit(solution)/shard_map/ppermute | solution.py:246
  24.8 6.6 %collective-permute-start.3 = (f32[20,8,2,128]{3,1,2,0:T(8,128)S(1)}, f32[20,8,2,128]{3,1,2,0:T(8,128)S(1)}, u32[]{:S(2)}, u32[]{:S(2)}) collective-permute-start(f32[20,8,2,128]{3,1,2,0:T(8,128)S(1)} %get-tuple-element.64), channel_id=1, source_target_pairs={{1,0},{2,1},{3,2},{4,3},{5,4},{6,5},{7,6},{8,7},{9,8},{10,9},{11,1... | collective-permute-start | bytes 491528 | tf_op jit(solution)/shard_map/ppermute | solution.py:247
  35.1 1.1 copy-start.3
  102.1 1.1 copy-start.1
  102.1 1.1 copy-start.2
  102.1 6.5 %copy-start = (f32[6,3,4,8,128]{4,3,2,1,0:T(8,128)S(1)}, f32[6,3,4,8,128]{4,3,2,1,0:T(8,128)}, u32[]{:S(2)}) copy-start(f32[6,3,4,8,128]{4,3,2,1,0:T(8,128)} %param.8) | copy-start | bytes 884740
  103.2 6.0 %collective-permute-start.5 = (f32[4,8,128]{2,1,0:T(8,128)S(1)}, f32[4,8,128]{2,1,0:T(8,128)S(1)}, u32[]{:S(2)}, u32[]{:S(2)}) collective-permute-start(f32[4,8,128]{2,1,0:T(8,128)S(1)} %add_multiply_fusion), channel_id=1, source_target_pairs={{16,0},{32,16},{48,32},{64,48},{80,64},{96,80},{112,96},{128,112},... | collective-permute-start | bytes 49160 | tf_op jit(solution)/shard_map/ppermute | solution.py:31
  106.5 6.6 %collective-permute-start.4 = (f32[4,8,128]{2,1,0:T(8,128)S(1)}, f32[4,8,128]{2,1,0:T(8,128)S(1)}, u32[]{:S(2)}, u32[]{:S(2)}) collective-permute-start(f32[4,8,128]{2,1,0:T(8,128)S(1)} %add_multiply_fusion), channel_id=1, source_target_pairs={{0,16},{16,32},{32,48},{48,64},{64,80},{80,96},{96,112},{112,128},... | collective-permute-start | bytes 49160 | tf_op jit(solution)/shard_map/ppermute | solution.py:29
  113.1 10.4 %collective-permute-start.6 = (f32[4,4,128]{2,1,0:T(4,128)S(1)}, f32[4,4,128]{2,1,0:T(4,128)S(1)}, u32[]{:S(2)}, u32[]{:S(2)}) collective-permute-start(f32[4,4,128]{2,1,0:T(4,128)S(1)} %get-tuple-element.75), channel_id=1, source_target_pairs={{0,1},{1,2},{2,3},{3,4},{4,5},{5,6},{6,7},{7,8},{8,9},{9,10},{10,1... | collective-permute-start | bytes 24584 | tf_op jit(solution)/shard_map/ppermute | solution.py:29
  118.2 5.3 %collective-permute-start.7 = (f32[4,4,128]{2,1,0:T(4,128)S(1)}, f32[4,4,128]{2,1,0:T(4,128)S(1)}, u32[]{:S(2)}, u32[]{:S(2)}) collective-permute-start(f32[4,4,128]{2,1,0:T(4,128)S(1)} %get-tuple-element.76), channel_id=1, source_target_pairs={{1,0},{2,1},{3,2},{4,3},{5,4},{6,5},{7,6},{8,7},{9,8},{10,9},{11,1... | collective-permute-start | bytes 24584 | tf_op jit(solution)/shard_map/ppermute | solution.py:31

commit v6 on v5

--- a/solution.py
+++ b/solution.py
@@ -143,7 +143,7 @@
 
 
 def tree_sum(value):
-    for axis in ("gy", "gx"):
+    for axis in ("gx", "gy"):
         count = lax.axis_size(axis)
         copies = jnp.broadcast_to(value[None], (count,) + value.shape)
         value = jnp.sum(lax.all_to_all(copies, axis, 0, 0, tiled=False), axis=0)

time: 125 us -> 125 us (level)
  no operation moved by 1% of the time
where the time goes in v6:
time: 125 us; the launch traced here: 124 us
  blocking collectives  31.6 us (25%)
  starting transfers between devices  30.2 us (24%)
  other arithmetic  18.3 us (15%)
  matrix products  16.3 us (13%)
  local copies, waits for them, and re-layouts  14.5 us (12%)
  waiting for transfers between devices  9.78 us (8%)
  between operations  3.22 us (3%)
    all_to_all x2, blocking collectives, tree_sum(): value = jnp.sum(lax.all_to_all(copies, axis, 0, 0, tiled=False), axis=0)  31.6 us
    ppermute x2, starting transfers between devices, halo_both(): above = lax.ppermute(head, axis, [(i + 1, i) for i in range(count - 1)])  10.5 us
    dot_general x2, matrix products, node_forces(): jnp.einsum('ij,cjabd->ciabd', stiffness, local_disp, precision=highest)  10.2 us
    ppermute x2, starting transfers between devices, halo_both(): below = lax.ppermute(tail, axis, [(i, i + 1) for i in range(count - 1)])  8.64 us
    ppermute x2, starting transfers between devices, with_halo(): lax.ppermute(tail, axis, [(i, (i + 1) % count) for i in range(ends)])  6.15 us
    unnamed x31, local copies, waits for them, and re-layouts  5.35 us
    ppermute x2, waiting for transfers between devices, halo_both(): above = lax.ppermute(head, axis, [(i + 1, i) for i in range(count - 1)])  5.26 us
    ppermute x2, starting transfers between devices, with_halo(): lax.ppermute(head, axis, [((i + 1) % count, i) for i in range(ends)])  4.95 us
  transfers between devices with their start and end apart: 8, of which 5 were waited for; matrix products, arithmetic and copies ran while one was open for 3% of the time, Pallas kernels for 0%

profile of v6, /device:TPU:3, one launch (start us, length us, event | category | flops | bytes accessed | tf_op | source)
XLA Modules:
  0.0 123.8 jit_solution(10960715056447856885)
XLA Ops:
  0.7 0.7 copy.256
  1.4 0.9 convolution_bitcast_fusion.1
  2.4 0.8 multiply_multiply_fusion.1
  3.4 1.1 copy.172
  4.7 4.0 %collective-permute-start = (f32[20,2,8,128]{3,1,2,0:T(2,128)S(1)}, f32[20,2,8,128]{3,1,2,0:T(2,128)S(1)}, u32[]{:S(2)}, u32[]{:S(2)}) collective-permute-start(f32[20,2,8,128]{3,1,2,0:T(2,128)S(1)} %get-tuple-element.68), channel_id=1, source_target_pairs={{0,16},{16,32},{32,48},{48,64},{64,80},{80,96},{96,112},{112,128},... | collective-permute-start | bytes 491528 | tf_op jit(solution)/shard_map/ppermute | solution.py:246
  8.7 8.6 %collective-permute-start.1 = (f32[20,2,8,128]{3,1,2,0:T(2,128)S(1)}, f32[20,2,8,128]{3,1,2,0:T(2,128)S(1)}, u32[]{:S(2)}, u32[]{:S(2)}) collective-permute-start(f32[20,2,8,128]{3,1,2,0:T(2,128)S(1)} %get-tuple-element.69), channel_id=1, source_target_pairs={{16,0},{32,16},{48,32},{64,48},{80,64},{96,80},{112,96},{128,112},... | collective-permute-start | bytes 491528 | tf_op jit(solution)/shard_map/ppermute | solution.py:247
  17.2 0.7 and_convert_fusion.1
  17.9 0.7 and_convert_fusion
  18.6 0.7 collective-permute-done
  19.2 0.9 collective-permute-done.1
  20.2 4.6 %collective-permute-start.2 = (f32[20,8,2,128]{3,1,2,0:T(8,128)S(1)}, f32[20,8,2,128]{3,1,2,0:T(8,128)S(1)}, u32[]{:S(2)}, u32[]{:S(2)}) collective-permute-start(f32[20,8,2,128]{3,1,2,0:T(8,128)S(1)} %get-tuple-element.63), channel_id=1, source_target_pairs={{0,1},{1,2},{2,3},{3,4},{4,5},{5,6},{6,7},{7,8},{8,9},{9,10},{10,1... | collective-permute-start | bytes 491528 | tf_op jit(solution)/shard_map/ppermute | solution.py:246
  24.8 1.9 %collective-permute-start.3 = (f32[20,8,2,128]{3,1,2,0:T(8,128)S(1)}, f32[20,8,2,128]{3,1,2,0:T(8,128)S(1)}, u32[]{:S(2)}, u32[]{:S(2)}) collective-permute-start(f32[20,8,2,128]{3,1,2,0:T(8,128)S(1)} %get-tuple-element.64), channel_id=1, source_target_pairs={{1,0},{2,1},{3,2},{4,3},{5,4},{6,5},{7,6},{8,7},{9,8},{10,9},{11,1... | collective-permute-start | bytes 491528 | tf_op jit(solution)/shard_map/ppermute | solution.py:247
  27.1 4.4 %collective-permute-done.3 = f32[20,8,2,128]{3,1,2,0:T(8,128)S(1)} collective-permute-done((f32[20,8,2,128]{3,1,2,0:T(8,128)S(1)}, f32[20,8,2,128]{3,1,2,0:T(8,128)S(1)}, u32[]{:S(2)}, u32[]{:S(2)}) %collective-permute-start.3) | collective-permute-done | bytes 163872 | tf_op jit(solution)/shard_map/ppermute | solution.py:247
  32.0 0.5 copy.175
  32.5 1.0 copy.194
  35.1 1.1 copy.181
  36.2 7.0 %broadcast_multiply_fusion = (f32[6,24,7,11,128]{4,1,3,2,0:T(8,128)S(1)}, f32[6,24,7,11,128]{4,1,3,2,0:T(8,128)}) fusion(f32[7,11,128]{2,1,0:T(8,128)S(1)} %copy.182, f32[6,24,7,11,128]{4,1,3,2,0:T(8,128)S(1)} %copy.181, f32[24,24,1,1,1]{1,0,4,3,2:T(8,128)S(1)} %copy-done.3), kind=kOutput, calls=%fused_computation.9 | convolution fusion | flops 410167296 | bytes 17072896 | tf_op jit(solution)/shard_map/ij,cjabd->ciabd/dot_general | solution.py:259
  43.2 1.5 %copy.223 = f32[6,24,7,11,128]{4,0,3,2,1:T(8,128)S(1)} copy(f32[6,24,7,11,128]{4,1,3,2,0:T(8,128)S(1)} %get-tuple-element.78) | data formatting | bytes 11354112 | tf_op jit(solution)/shard_map/reshape | solution.py:260
  44.6 0.5 slice_bitcast_fusion.5
  45.1 0.9 fusion.28
  46.7 1.0 fusion.8
  49.2 0.5 copy.205
  49.6 3.2 %broadcast_multiply_fusion.1 = (f32[6,24,5,9,128]{4,1,3,2,0:T(8,128)S(1)}, f32[6,24,5,9,128]{4,1,3,2,0:T(8,128)S(1)}) fusion(f32[5,9,128]{2,1,0:T(8,128)S(1)} %copy.196, f32[24,24,1,1,1]{1,0,4,3,2:T(8,128)S(1)} %copy-done.3, f32[6,24,5,9,128]{4,0,3,2,1:T(8,128)S(1)} %bitcast.204), kind=kOutput, calls=%fused_computation.24 | convolution fusion | flops 239708160 | bytes 9978624 | tf_op jit(solution)/shard_map/ij,cjabd->ciabd/dot_general | solution.py:259
  52.8 0.9 copy.234
  54.0 2.6 %fusion.3 = (f32[6]{0:T(128)S(1)}, f32[6,24,4,8,128]{4,1,3,2,0:T(8,128)S(1)}, f32[6,24,4,8,128]{4,1,3,2,0:T(8,128)S(1)}) fusion(f32[6,24,7,11,128]{4,1,3,2,0:T(8,128)S(1)} %copy.181, f32[6,24,7,11,128]{4,1,3,2,0:T(8,128)} %get-tuple-element.79, f32[4,8,128]{2,1,0:T(8,128)S(1)} %get-tuple-element.70, f32[6,24,5,9,128]{4,1,3,2,0:T(8,128)S(1)} %get-tuple-element.81), kind=kLoop, calls=%fused_computation.18 | loop fusion | flops 2949114 | bytes 11812888 | tf_op jit(solution)/shard_map/reduce_sum | solution.py:339
  57.5 2.9 %multiply_reduce_fusion = (f32[6,6]{1,0:T(8,128)S(1)}, f32[6,6]{1,0:T(8,128)S(1)}) fusion(f32[6,24,4,8,128]{4,3,2,1,0:T(8,128)S(1)} %copy.207, f32[6,24,4,8,128]{4,3,2,1,0:T(8,128)S(1)} %copy.205, f32[6,24,4,8,128]{4,3,2,1,0:T(8,128)S(1)} %copy.206), kind=kLoop, calls=%fused_computation | loop fusion | flops 14155704 | bytes 7078176 | tf_op jit(solution)/shard_map/reduce_sum | solution.py:345
  60.4 1.2 fusion.7
  62.0 16.1 %all_to_all.10 = f32[32,1,180]{2,1,0:T(1,128)S(1)} all-to-all(f32[32,1,180]{2,1,0:T(1,128)S(1)} %reshape.317), channel_id=1, replica_groups=mesh['gx'=32,'gy'=16] {'gx'}, dimensions={0} | all-to-all | bytes 46080 | tf_op jit(solution)/shard_map/all_to_all | solution.py:149
  78.1 0.5 broadcast.970
  78.6 0.7 reduce.7
  79.8 15.5 %all_to_all.11 = f32[16,1,180]{2,1,0:T(1,128)S(1)} all-to-all(f32[16,1,180]{2,1,0:T(1,128)S(1)} %reshape.319), channel_id=1, replica_groups=mesh['gx'=32,'gy'=16] {'gy'}, dimensions={0} | all-to-all | bytes 23040 | tf_op jit(solution)/shard_map/all_to_all | solution.py:149
  95.4 0.7 reduce.8
  96.3 0.6 slice_bitcast_fusion.24
  97.0 0.5 cholesky.15
  97.5 0.6 compare_reduce_fusion
  98.2 0.6 fusion.132
  98.8 0.5 custom-call.8
  99.5 0.8 fusion.134
  100.3 1.3 %convolution_add_fusion = f32[6,3,5,9,129]{4,0,3,2,1:T(8,128)S(1)} fusion(f32[6,3,6,10,128]{4,0,3,2,1:T(8,128)S(1)} %maximum_multiply_fusion, f32[6,3,8,12,128]{4,0,3,2,1:T(8,128)S(1)} %copy.175, f32[6,6]{1,0:T(8,128)S(1)} %get-tuple-element.83), kind=kOutput, calls=%fused_computation.27 | convolution fusion | flops 7627770 | bytes 1855800 | tf_op jit(solution)/shard_map/kabcd,kj->jabcd/dot_general | solution.py:154
  104.2 3.0 %collective-permute-start.5 = (f32[4,8,128]{2,1,0:T(8,128)S(1)}, f32[4,8,128]{2,1,0:T(8,128)S(1)}, u32[]{:S(2)}, u32[]{:S(2)}) collective-permute-start(f32[4,8,128]{2,1,0:T(8,128)S(1)} %add_multiply_fusion), channel_id=1, source_target_pairs={{16,0},{32,16},{48,32},{64,48},{80,64},{96,80},{112,96},{128,112},... | collective-permute-start | bytes 49160 | tf_op jit(solution)/shard_map/ppermute | solution.py:31
  107.3 2.3 %collective-permute-start.4 = (f32[4,8,128]{2,1,0:T(8,128)S(1)}, f32[4,8,128]{2,1,0:T(8,128)S(1)}, u32[]{:S(2)}, u32[]{:S(2)}) collective-permute-start(f32[4,8,128]{2,1,0:T(8,128)S(1)} %add_multiply_fusion), channel_id=1, source_target_pairs={{0,16},{16,32},{32,48},{48,64},{64,80},{80,96},{96,112},{112,128},... | collective-permute-start | bytes 49160 | tf_op jit(solution)/shard_map/ppermute | solution.py:29
  109.5 0.7 convolution_add_fusion.1
  110.2 3.6 %collective-permute-done.4 = f32[4,8,128]{2,1,0:T(8,128)S(1)} collective-permute-done((f32[4,8,128]{2,1,0:T(8,128)S(1)}, f32[4,8,128]{2,1,0:T(8,128)S(1)}, u32[]{:S(2)}, u32[]{:S(2)}) %collective-permute-start.4) | collective-permute-done | bytes 16416 | tf_op jit(solution)/shard_map/ppermute | solution.py:29
  113.9 3.9 %collective-permute-start.6 = (f32[4,4,128]{2,1,0:T(4,128)S(1)}, f32[4,4,128]{2,1,0:T(4,128)S(1)}, u32[]{:S(2)}, u32[]{:S(2)}) collective-permute-start(f32[4,4,128]{2,1,0:T(4,128)S(1)} %get-tuple-element.75), channel_id=1, source_target_pairs={{0,1},{1,2},{2,3},{3,4},{4,5},{5,6},{6,7},{7,8},{8,9},{9,10},{10,1... | collective-permute-start | bytes 24584 | tf_op jit(solution)/shard_map/ppermute | solution.py:29
  117.8 1.9 %collective-permute-start.7 = (f32[4,4,128]{2,1,0:T(4,128)S(1)}, f32[4,4,128]{2,1,0:T(4,128)S(1)}, u32[]{:S(2)}, u32[]{:S(2)}) collective-permute-start(f32[4,4,128]{2,1,0:T(4,128)S(1)} %get-tuple-element.76), channel_id=1, source_target_pairs={{1,0},{2,1},{3,2},{4,3},{5,4},{6,5},{7,6},{8,7},{9,8},{10,9},{11,1... | collective-permute-start | bytes 24584 | tf_op jit(solution)/shard_map/ppermute | solution.py:31
  119.7 0.7 multiply_reduce_fusion.3
  120.4 0.8 copy.216
  123.1 0.7 multiply_minimum_fusion
  (89 shorter events, 10.1 us)
Async XLA Ops:
  4.7 14.6 %collective-permute-start = (f32[20,2,8,128]{3,1,2,0:T(2,128)S(1)}, f32[20,2,8,128]{3,1,2,0:T(2,128)S(1)}, u32[]{:S(2)}, u32[]{:S(2)}) collective-permute-start(f32[20,2,8,128]{3,1,2,0:T(2,128)S(1)} %get-tuple-element.68), channel_id=1, source_target_pairs={{0,16},{16,32},{32,48},{48,64},{64,80},{80,96},{96,112},{112,128},... | collective-permute-start | bytes 491528 | tf_op jit(solution)/shard_map/ppermute | solution.py:246
  8.7 11.4 %collective-permute-start.1 = (f32[20,2,8,128]{3,1,2,0:T(2,128)S(1)}, f32[20,2,8,128]{3,1,2,0:T(2,128)S(1)}, u32[]{:S(2)}, u32[]{:S(2)}) collective-permute-start(f32[20,2,8,128]{3,1,2,0:T(2,128)S(1)} %get-tuple-element.69), channel_id=1, source_target_pairs={{16,0},{32,16},{48,32},{64,48},{80,64},{96,80},{112,96},{128,112},... | collective-permute-start | bytes 491528 | tf_op jit(solution)/shard_map/ppermute | solution.py:247
  20.2 6.9 %collective-permute-start.2 = (f32[20,8,2,128]{3,1,2,0:T(8,128)S(1)}, f32[20,8,2,128]{3,1,2,0:T(8,128)S(1)}, u32[]{:S(2)}, u32[]{:S(2)}) collective-permute-start(f32[20,8,2,128]{3,1,2,0:T(8,128)S(1)} %get-tuple-element.63), channel_id=1, source_target_pairs={{0,1},{1,2},{2,3},{3,4},{4,5},{5,6},{6,7},{7,8},{8,9},{9,10},{10,1... | collective-permute-start | bytes 491528 | tf_op jit(solution)/shard_map/ppermute | solution.py:246
  24.8 6.6 %collective-permute-start.3 = (f32[20,8,2,128]{3,1,2,0:T(8,128)S(1)}, f32[20,8,2,128]{3,1,2,0:T(8,128)S(1)}, u32[]{:S(2)}, u32[]{:S(2)}) collective-permute-start(f32[20,8,2,128]{3,1,2,0:T(8,128)S(1)} %get-tuple-element.64), channel_id=1, source_target_pairs={{1,0},{2,1},{3,2},{4,3},{5,4},{6,5},{7,6},{8,7},{9,8},{10,9},{11,1... | collective-permute-start | bytes 491528 | tf_op jit(solution)/shard_map/ppermute | solution.py:247
  35.1 1.1 copy-start.3
  103.0 1.1 copy-start.1
  103.0 1.1 copy-start.2
  103.1 6.5 %copy-start = (f32[6,3,4,8,128]{4,3,2,1,0:T(8,128)S(1)}, f32[6,3,4,8,128]{4,3,2,1,0:T(8,128)}, u32[]{:S(2)}) copy-start(f32[6,3,4,8,128]{4,3,2,1,0:T(8,128)} %param.8) | copy-start | bytes 884740
  104.2 6.0 %collective-permute-start.5 = (f32[4,8,128]{2,1,0:T(8,128)S(1)}, f32[4,8,128]{2,1,0:T(8,128)S(1)}, u32[]{:S(2)}, u32[]{:S(2)}) collective-permute-start(f32[4,8,128]{2,1,0:T(8,128)S(1)} %add_multiply_fusion), channel_id=1, source_target_pairs={{16,0},{32,16},{48,32},{64,48},{80,64},{96,80},{112,96},{128,112},... | collective-permute-start | bytes 49160 | tf_op jit(solution)/shard_map/ppermute | solution.py:31
  107.3 6.6 %collective-permute-start.4 = (f32[4,8,128]{2,1,0:T(8,128)S(1)}, f32[4,8,128]{2,1,0:T(8,128)S(1)}, u32[]{:S(2)}, u32[]{:S(2)}) collective-permute-start(f32[4,8,128]{2,1,0:T(8,128)S(1)} %add_multiply_fusion), channel_id=1, source_target_pairs={{0,16},{16,32},{32,48},{48,64},{64,80},{80,96},{96,112},{112,128},... | collective-permute-start | bytes 49160 | tf_op jit(solution)/shard_map/ppermute | solution.py:29
  113.9 9.2 %collective-permute-start.6 = (f32[4,4,128]{2,1,0:T(4,128)S(1)}, f32[4,4,128]{2,1,0:T(4,128)S(1)}, u32[]{:S(2)}, u32[]{:S(2)}) collective-permute-start(f32[4,4,128]{2,1,0:T(4,128)S(1)} %get-tuple-element.75), channel_id=1, source_target_pairs={{0,1},{1,2},{2,3},{3,4},{4,5},{5,6},{6,7},{7,8},{8,9},{9,10},{10,1... | collective-permute-start | bytes 24584 | tf_op jit(solution)/shard_map/ppermute | solution.py:29
  117.8 5.3 %collective-permute-start.7 = (f32[4,4,128]{2,1,0:T(4,128)S(1)}, f32[4,4,128]{2,1,0:T(4,128)S(1)}, u32[]{:S(2)}, u32[]{:S(2)}) collective-permute-start(f32[4,4,128]{2,1,0:T(4,128)S(1)} %get-tuple-element.76), channel_id=1, source_target_pairs={{1,0},{2,1},{3,2},{4,3},{5,4},{6,5},{7,6},{8,7},{9,8},{10,9},{11,1... | collective-permute-start | bytes 24584 | tf_op jit(solution)/shard_map/ppermute | solution.py:31

commit v7 on v3

--- a/solution.py
+++ b/solution.py
@@ -143,7 +143,7 @@
 
 
 def tree_sum(value):
-    for axis in ("gy", "gx"):
+    for axis in ("gx", "gy"):
         count = lax.axis_size(axis)
         copies = jnp.broadcast_to(value[None], (count,) + value.shape)
         value = jnp.sum(lax.all_to_all(copies, axis, 0, 0, tiled=False), axis=0)
@@ -202,6 +202,59 @@
     return jnp.concatenate([kept[:, :, :1] + to_x, kept[:, :, 1:]], axis=2)
 
 
+def corner_modes(node_field):
+    cells = node_field
+    for step, dim in enumerate((2, 3, 4)):
+        dim = dim + step
+        low = lax.slice_in_dim(cells, 0, cells.shape[dim] - 1, axis=dim)
+        high = lax.slice_in_dim(cells, 1, cells.shape[dim], axis=dim)
+        cells = jnp.stack([high + low, high - low], axis=step)
+    return cells
+
+
+def mode_stiffness():
+    step = np.array([[1.0, 1.0], [-1.0, 1.0]])
+    change = np.kron(np.kron(np.kron(step, step), step), np.eye(3))
+    return change @ hex_stiffness() @ change.T / 64.0
+
+
+def mode_loads(modes, table):
+    loads = []
+    for comp in range(3):
+        total = None
+        for other in range(3):
+            weights = np.zeros((8,))
+            for mode in range(8):
+                source = mode ^ (4 >> comp) ^ (4 >> other)
+                weights[mode] = table[3 * mode + comp, 3 * source + other]
+            weights[np.abs(weights) < 1e-12] = 0.0
+            if not weights.any():
+                continue
+            part = modes[:, :, :, :, other]
+            flips = tuple(sorted({comp, other})) if comp != other else ()
+            if flips:
+                part = jnp.flip(part, axis=flips)
+            term = jnp.asarray(weights.reshape(2, 2, 2, 1, 1, 1, 1), jnp.float32) * part
+            total = term if total is None else total + term
+        loads.append(total)
+    return jnp.stack(loads, axis=4)
+
+
+def modes_to_nodes(loads):
+    cells = loads
+    for mode_axis in (2, 1, 0):
+        dim = cells.ndim - (3 - mode_axis)
+        total = lax.index_in_dim(cells, 0, axis=mode_axis, keepdims=False)
+        change = lax.index_in_dim(cells, 1, axis=mode_axis, keepdims=False)
+        dim = dim - 1
+        low = [(0, 0)] * total.ndim
+        low[dim] = (0, 1)
+        high = [(0, 0)] * total.ndim
+        high[dim] = (1, 0)
+        cells = jnp.pad(total - change, low) + jnp.pad(total + change, high)
+    return cells
+
+
 def halo_both(cells, axis, dim, width):
     count = lax.axis_size(axis)
     head = lax.slice_in_dim(cells, 0, width, axis=dim)
@@ -217,22 +270,15 @@
     return ((own >= 0) & (own < total)).astype(jnp.float32)
 
 
-def node_forces(node_field, modulus, stiffness):
-    local_disp = cases_disp(node_field)
-    local_load = jnp.einsum("ij,cjabd->ciabd", stiffness, local_disp, precision=highest)
-    local_force = (local_load * modulus).reshape((node_field.shape[0], 8, 3) + modulus.shape)
-    summed = jnp.zeros_like(node_field)
-    for corner in range(8):
-        off_x, off_y, off_z = (corner // 4, corner // 2 % 2, corner % 2)
-        summed = summed + jnp.pad(
-            local_force[:, corner],
-            ((0, 0), (0, 0), (off_x, 1 - off_x), (off_y, 1 - off_y), (off_z, 1 - off_z)),
-        )
-    return summed[..., :-1], local_disp, local_load
+def node_forces(node_field, modulus, table):
+    modes = corner_modes(node_field)
+    loads = mode_loads(modes, table)
+    summed = modes_to_nodes(loads * modulus)
+    return summed[..., :-1], modes, loads
 
 
 def on_device(start_disp, bone_mask, density, load_nodes, load_forces):
-    stiffness = jnp.asarray(hex_stiffness(), jnp.float32)
+    stiffness = mode_stiffness()
     modulus = bone_mask.astype(jnp.float32) * density * density
     case_count = start_disp.shape[0]
     size_x = start_disp.shape[2]
@@ -295,18 +341,20 @@
         shape = [1, 1, 1]
         shape[dim] = extent
         blur_mass = blur_mass * kept.reshape(shape)
-    start_elems = start_elems[:, :, 2:-1, 2:-1]
-    start_loads = start_loads[:, :, 2:-1, 2:-1]
-    residual_elems = residual_elems[:, :, 1:, 1:]
-    residual_loads = residual_loads[:, :, 1:, 1:]
-    start_energy = jnp.sum(start_elems * start_loads * blur_mass, axis=(1, 2, 3, 4))
+    start_elems = start_elems[..., 2:-1, 2:-1, :]
+    start_loads = start_loads[..., 2:-1, 2:-1, :]
+    residual_elems = residual_elems[..., 1:, 1:, :]
+    residual_loads = residual_loads[..., 1:, 1:, :]
     start_weighted = start_loads * blur_mass
     residual_weighted = residual_loads * blur_mass
+    start_energy = jnp.sum(start_elems * start_weighted, axis=(0, 1, 2, 4, 5, 6, 7))
     cross_energy = jnp.sum(
-        residual_elems[:, None] * start_weighted[None, :], axis=(2, 3, 4, 5)
+        residual_elems[:, :, :, :, None] * start_weighted[:, :, :, None, :],
+        axis=(0, 1, 2, 5, 6, 7, 8),
     )
     residual_energy = jnp.sum(
-        residual_elems[:, None] * residual_weighted[None, :], axis=(2, 3, 4, 5)
+        residual_elems[:, :, :, :, None] * residual_weighted[:, :, :, None, :],
+        axis=(0, 1, 2, 5, 6, 7, 8),
     )
     grams = tree_sum(
         jnp.stack(
@@ -327,13 +375,12 @@
         + jnp.sum(step_alpha[:, None, :] * grams[3][:, :, None] * step_alpha[None, :, :])
     )
     solution = start_disp + mix_cases(residual, step_alpha)
-    final_elems = start_elems + jnp.sum(
-        residual_elems[:, None] * step_alpha[:, :, None, None, None, None], axis=0
-    )
-    final_loads = start_loads + jnp.sum(
-        residual_loads[:, None] * step_alpha[:, :, None, None, None, None], axis=0
-    )
-    energy = jnp.sum(final_elems * final_loads, axis=(0, 1))
+    node_field = start_nodes[:, :, 2:-1, 2:-1] + mix_cases(
+        residual_nodes[:, :, 1:, 1:], step_alpha
+    )
+    final_modes = corner_modes(node_field)
+    final_loads = mode_loads(final_modes, stiffness)
+    energy = jnp.sum(final_modes * final_loads, axis=(0, 1, 2, 3, 4))
     stimulus = modulus * energy
     smooth = blur_valid(with_halo(stimulus, (("gx", 0),), 4), 0, size_x)
     smooth = blur_valid(with_halo(smooth, (("gy", 1),), 4), 1, size_y)

time: 148 us -> 142 us (0.959)
  the two profiles are of different devices: /device:TPU:3 before, /device:TPU:1 now
where the time goes in v7:
time: 142 us; the launch traced here: 141 us
  other arithmetic  43.2 us (30%)
  blocking collectives  36.4 us (26%)
  starting transfers between devices  23 us (16%)
  local copies, waits for them, and re-layouts  17.3 us (12%)
  waiting for transfers between devices  11.9 us (8%)
  matrix products  5.84 us (4%)
  between operations  3.34 us (2%)
    all_to_all x2, blocking collectives, tree_sum(): value = jnp.sum(lax.all_to_all(copies, axis, 0, 0, tiled=False), axis=0)  36.4 us
    ppermute x2, starting transfers between devices, halo_both(): below = lax.ppermute(tail, axis, [(i, i + 1) for i in range(count - 1)])  10.4 us
    unnamed x53, local copies, waits for them, and re-layouts  10.1 us
    ppermute x2, waiting for transfers between devices, halo_both(): above = lax.ppermute(head, axis, [(i + 1, i) for i in range(count - 1)])  8.5 us
    another operation x10, other arithmetic, corner_modes(): cells = jnp.stack([high + low, high - low], axis=step)  7.84 us
    another operation x8, other arithmetic, mode_loads(): return jnp.stack(loads, axis=4)  7.56 us
    ppermute x2, starting transfers between devices, with_halo(): lax.ppermute(tail, axis, [(i, (i + 1) % count) for i in range(ends)])  6.22 us
    sub x6, other arithmetic, modes_to_nodes(): cells = jnp.pad(total - change, low) + jnp.pad(total + change, high)  5.55 us
  transfers between devices with their start and end apart: 8, of which 4 were waited for; matrix products, arithmetic and copies ran while one was open for 2% of the time, Pallas kernels for 0%

profile of v7, /device:TPU:1, one launch (start us, length us, event | category | flops | bytes accessed | tf_op | source)
XLA Modules:
  0.0 140.9 jit_solution(15255833709330621030)
XLA Ops:
  0.7 0.8 multiply_multiply_fusion.1
  1.5 0.7 copy.268
  2.2 0.9 convolution_bitcast_fusion
  3.4 1.1 copy.193
  4.7 4.8 %collective-permute-start = (f32[20,2,8,128]{3,1,2,0:T(2,128)S(1)}, f32[20,2,8,128]{3,1,2,0:T(2,128)S(1)}, u32[]{:S(2)}, u32[]{:S(2)}) collective-permute-start(f32[20,2,8,128]{3,1,2,0:T(2,128)S(1)} %get-tuple-element.66), channel_id=1, source_target_pairs={{0,16},{16,32},{32,48},{48,64},{64,80},{80,96},{96,112},{112,128},... | collective-permute-start | bytes 491528 | tf_op jit(solution)/shard_map/ppermute | solution.py:262
  9.5 1.3 collective-permute-start.1
  10.9 0.9 collective-permute-done
  11.8 4.5 %collective-permute-done.1 = f32[20,2,8,128]{3,1,2,0:T(2,128)S(1)} collective-permute-done((f32[20,2,8,128]{3,1,2,0:T(2,128)S(1)}, f32[20,2,8,128]{3,1,2,0:T(2,128)S(1)}, u32[]{:S(2)}, u32[]{:S(2)}) %collective-permute-start.1) | collective-permute-done | bytes 163872 | tf_op jit(solution)/shard_map/ppermute | solution.py:263
  16.3 5.5 %collective-permute-start.2 = (f32[20,8,2,128]{3,1,2,0:T(8,128)S(1)}, f32[20,8,2,128]{3,1,2,0:T(8,128)S(1)}, u32[]{:S(2)}, u32[]{:S(2)}) collective-permute-start(f32[20,8,2,128]{3,1,2,0:T(8,128)S(1)} %get-tuple-element.64), channel_id=1, source_target_pairs={{0,1},{1,2},{2,3},{3,4},{4,5},{5,6},{6,7},{7,8},{8,9},{9,10},{10,1... | collective-permute-start | bytes 491528 | tf_op jit(solution)/shard_map/ppermute | solution.py:262
  21.9 1.9 %collective-permute-start.3 = (f32[20,8,2,128]{3,1,2,0:T(8,128)S(1)}, f32[20,8,2,128]{3,1,2,0:T(8,128)S(1)}, u32[]{:S(2)}, u32[]{:S(2)}) collective-permute-start(f32[20,8,2,128]{3,1,2,0:T(8,128)S(1)} %get-tuple-element.65), channel_id=1, source_target_pairs={{1,0},{2,1},{3,2},{4,3},{5,4},{6,5},{7,6},{8,7},{9,8},{10,9},{11,1... | collective-permute-start | bytes 491528 | tf_op jit(solution)/shard_map/ppermute | solution.py:263
  24.5 4.0 %collective-permute-done.3 = f32[20,8,2,128]{3,1,2,0:T(8,128)S(1)} collective-permute-done((f32[20,8,2,128]{3,1,2,0:T(8,128)S(1)}, f32[20,8,2,128]{3,1,2,0:T(8,128)S(1)}, u32[]{:S(2)}, u32[]{:S(2)}) %collective-permute-start.3) | collective-permute-done | bytes 163872 | tf_op jit(solution)/shard_map/ppermute | solution.py:263
  29.9 1.0 add_bitcast_fusion.3
  30.9 2.6 %subtract_bitcast_fusion = (f32[2,2,1,6,3,7,11,128]{7,3,6,5,4,0,1,2:T(8,128)S(1)}, f32[2,2,1,6,3,7,11,128]{7,3,6,5,4,0,1,2:T(8,128)S(1)}) fusion(f32[2,1,6,3,7,11,129]{6,2,5,4,3,0,1:T(8,128)S(1)} %get-tuple-element.47, f32[2,1,6,3,7,11,129]{6,2,5,4,3,0,1:T(8,128)S(1)} %get-tuple-element.46), kind=kLoop, calls=%fused_computation.48 | loop fusion | flops 3548160 | bytes 8537760 | tf_op jit(solution)/shard_map/stack | solution.py:211
  34.1 1.3 copy-done
  35.5 1.1 copy-done.2
  37.4 1.0 add_bitcast_fusion.5
  38.4 3.5 %pad_maximum_fusion = (f32[2,2,2,6,3,7,11,128]{7,3,6,5,0,1,2,4:T(8,128)}, f32[2,2,2,6,3,7,11,128]{7,3,6,5,0,1,2,4:T(8,128)S(1)}) fusion(f32[2,2,2,6,1,7,11,128]{7,3,6,5,0,1,2,4:T(8,128)S(1)} %get-tuple-element.29, f32[2,2,2,6,1,7,11,128]{7,3,6,5,0,1,2,4:T(8,128)S(1)} %get-tuple-element.28, f32[2,2,2,6,1,7,11,128]{7,3,6,5,0,1,2,4:T(8,128)S(1)} %get-tuple-element.24, ...), kind=kLoop, calls=%fused_computation.10 | loop fusion | flops 4257792 | bytes 17070592 | tf_op jit(solution)/shard_map/stack | solution.py:240
  42.8 2.0 %fusion.3 = f32[2,6,3,7,11,129]{5,1,4,3,0,2:T(8,128)S(1)} fusion(f32[2,2,6,3,7,11,128]{6,2,5,4,0,1,3:T(8,128)S(1)} %add_bitcast_fusion.1, f32[2,2,6,3,7,11,128]{6,2,5,4,0,1,3:T(8,128)S(1)} %fusion.4), kind=kLoop, calls=%fused_computation.42 | loop fusion | flops 1072764 | bytes 7107408 | tf_op jit(solution)/shard_map/sub | solution.py:254
  44.8 2.0 %add_bitcast_fusion = f32[2,6,3,7,11,129]{5,1,4,3,0,2:T(8,128)S(1)} fusion(f32[2,2,6,3,7,11,128]{6,2,5,4,0,1,3:T(8,128)S(1)} %add_bitcast_fusion.1, f32[2,2,6,3,7,11,128]{6,2,5,4,0,1,3:T(8,128)S(1)} %fusion.4), kind=kLoop, calls=%fused_computation.45 | loop fusion | flops 1072764 | bytes 7107408 | tf_op jit(solution)/shard_map/add | solution.py:254
  46.8 0.7 fusion.19
  48.4 1.0 copy.211
  49.6 1.0 maximum_multiply_fusion
  51.3 1.2 subtract_bitcast_fusion.4
  53.3 1.0 fusion.30
  54.3 1.8 %copy.218 = f32[2,2,2,6,3,4,8,128]{7,6,5,4,3,2,1,0:T(8,128)} copy(f32[2,2,2,6,3,4,8,128]{7,3,6,5,4,0,1,2:T(8,128)S(1)} %pad_maximum_fusion.6) | data formatting | bytes 4718592 | tf_op jit(solution)/shard_map/slice | solution.py:346
  57.8 1.5 %copy-done.1 = f32[2,2,1,6,3,7,11,128]{7,3,6,5,4,0,1,2:T(8,128)S(1)} copy-done((f32[2,2,1,6,3,7,11,128]{7,3,6,5,4,0,1,2:T(8,128)S(1)}, f32[2,2,1,6,3,7,11,128]{7,3,6,5,4,0,1,2:T(8,128)}, u32[]{:S(2)}) %copy-start.1) | copy-done | bytes 2838552
  59.2 1.2 copy-done.3
  60.4 5.0 %fusion.8 = (f32[6]{0:T(128)S(1)}, f32[2,2,2,6,3,4,8,128]{7,3,6,5,4,0,1,2:T(8,128)}, f32[2,2,2,6,3,4,8,128]{7,3,6,5,4,0,1,2:T(8,128)S(1)}) fusion(f32[2,2,1,6,3,7,11,128]{7,3,6,5,4,0,1,2:T(8,128)S(1)} %copy-done.1, f32[2,2,1,6,3,7,11,128]{7,3,6,5,4,0,1,2:T(8,128)S(1)} %copy-done.3, f32[4,8,128]{2,1,0:T(8,128)S(1)} %get-tuple-element.68, ...), kind=kLoop, calls=%fused_computation.59 | loop fusion | flops 2949114 | bytes 15917080 | tf_op jit(solution)/shard_map/reduce_sum | solution.py:350
  65.4 2.3 %copy.220 = f32[2,2,2,6,3,4,8,128]{7,6,5,4,3,2,1,0:T(8,128)S(1)} copy(f32[2,2,2,6,3,4,8,128]{7,3,6,5,4,0,1,2:T(8,128)} %get-tuple-element.17) | data formatting | bytes 4718592 | tf_op jit(solution)/shard_map/mul | solution.py:348
  68.4 1.8 %subtract_bitcast_fusion.2 = (f32[2,6,3,5,9,129]{5,1,4,3,2,0:T(8,128)S(1)}, f32[2,6,3,5,9,129]{5,1,4,3,2,0:T(8,128)S(1)}) fusion(f32[2,2,6,3,5,9,128]{6,2,5,4,3,0,1:T(8,128)S(1)} %get-tuple-element.39, f32[2,2,6,3,5,9,128]{6,2,5,4,3,0,1:T(8,128)S(1)} %get-tuple-element.38), kind=kLoop, calls=%fused_computation.85 | loop fusion | flops 1044900 | bytes 4989600 | tf_op jit(solution)/shard_map/sub | solution.py:254
  70.8 1.4 %copy-done.4 = f32[2,2,2,6,3,4,8,128]{7,6,5,4,3,2,1,0:T(8,128)S(1)} copy-done((f32[2,2,2,6,3,4,8,128]{7,6,5,4,3,2,1,0:T(8,128)S(1)}, f32[2,2,2,6,3,4,8,128]{7,6,5,4,3,2,1,0:T(8,128)}, u32[]{:S(2)}) %copy-start.4) | copy-done | bytes 2359320
  72.2 2.7 %multiply_reduce_fusion = (f32[6,6]{1,0:T(8,128)S(1)}, f32[6,6]{1,0:T(8,128)S(1)}) fusion(f32[2,2,2,6,3,4,8,128]{7,6,5,4,3,2,1,0:T(8,128)S(1)} %copy.221, f32[2,2,2,6,3,4,8,128]{7,6,5,4,3,2,1,0:T(8,128)S(1)} %copy-done.4, f32[2,2,2,6,3,4,8,128]{7,6,5,4,3,2,1,0:T(8,128)S(1)} %copy.220), kind=kLoop, calls=%fused_computation | loop fusion | flops 14155704 | bytes 7078176 | tf_op jit(solution)/shard_map/reduce_sum | solution.py:355
  74.9 1.0 fusion.29
  76.3 20.8 %all_to_all.10 = f32[32,1,180]{2,1,0:T(1,128)S(1)} all-to-all(f32[32,1,180]{2,1,0:T(1,128)S(1)} %reshape.311), channel_id=1, replica_groups=mesh['gx'=32,'gy'=16] {'gx'}, dimensions={0} | all-to-all | bytes 46080 | tf_op jit(solution)/shard_map/all_to_all | solution.py:149
  97.7 0.7 reduce.7
  98.9 15.5 %all_to_all.11 = f32[16,1,180]{2,1,0:T(1,128)S(1)} all-to-all(f32[16,1,180]{2,1,0:T(1,128)S(1)} %reshape.313), channel_id=1, replica_groups=mesh['gx'=32,'gy'=16] {'gy'}, dimensions={0} | all-to-all | bytes 23040 | tf_op jit(solution)/shard_map/all_to_all | solution.py:149
  118.6 0.8 fusion.109
  119.4 1.3 convolution_add_fusion
  121.2 0.9 add_bitcast_fusion.13
  123.3 0.8 fusion.6
  124.1 2.3 %collective-permute-start.4 = (f32[4,8,128]{2,1,0:T(8,128)S(1)}, f32[4,8,128]{2,1,0:T(8,128)S(1)}, u32[]{:S(2)}, u32[]{:S(2)}) collective-permute-start(f32[4,8,128]{2,1,0:T(8,128)S(1)} %fusion.145), channel_id=1, source_target_pairs={{0,16},{16,32},{32,48},{48,64},{64,80},{80,96},{96,112},{112,128},... | collective-permute-start | bytes 49160 | tf_op jit(solution)/shard_map/ppermute | solution.py:29
  126.4 1.3 collective-permute-start.5
  128.4 2.5 %collective-permute-done.5 = f32[4,8,128]{2,1,0:T(8,128)S(1)} collective-permute-done((f32[4,8,128]{2,1,0:T(8,128)S(1)}, f32[4,8,128]{2,1,0:T(8,128)S(1)}, u32[]{:S(2)}, u32[]{:S(2)}) %collective-permute-start.5) | collective-permute-done | bytes 16416 | tf_op jit(solution)/shard_map/ppermute | solution.py:31
  131.0 3.9 %collective-permute-start.6 = (f32[4,4,128]{2,1,0:T(4,128)S(1)}, f32[4,4,128]{2,1,0:T(4,128)S(1)}, u32[]{:S(2)}, u32[]{:S(2)}) collective-permute-start(f32[4,4,128]{2,1,0:T(4,128)S(1)} %get-tuple-element.73), channel_id=1, source_target_pairs={{0,1},{1,2},{2,3},{3,4},{4,5},{5,6},{6,7},{7,8},{8,9},{9,10},{10,1... | collective-permute-start | bytes 24584 | tf_op jit(solution)/shard_map/ppermute | solution.py:29
  134.9 1.9 %collective-permute-start.7 = (f32[4,4,128]{2,1,0:T(4,128)S(1)}, f32[4,4,128]{2,1,0:T(4,128)S(1)}, u32[]{:S(2)}, u32[]{:S(2)}) collective-permute-start(f32[4,4,128]{2,1,0:T(4,128)S(1)} %get-tuple-element.74), channel_id=1, source_target_pairs={{1,0},{2,1},{3,2},{4,3},{5,4},{6,5},{7,6},{8,7},{9,8},{10,9},{11,1... | collective-permute-start | bytes 24584 | tf_op jit(solution)/shard_map/ppermute | solution.py:31
  136.8 0.7 multiply_reduce_fusion.2
  137.5 0.8 copy.234
  140.2 0.7 multiply_minimum_fusion
  (118 shorter events, 18.2 us)
Async XLA Ops:
  0.6 10.2 %copy-start.21 = (s32[6]{0:T(128)S(1)}, s32[6]{0:T(128)}, u32[]{:S(2)}) copy-start(s32[6]{0:T(128)} %constant.214.clone) | copy-start | bytes 76
  0.6 10.2 %copy-start.20 = (s32[10]{0:T(128)S(1)}, s32[10]{0:T(128)}, u32[]{:S(2)}) copy-start(s32[10]{0:T(128)} %constant.215.clone) | copy-start | bytes 124
  4.7 7.1 %collective-permute-start = (f32[20,2,8,128]{3,1,2,0:T(2,128)S(1)}, f32[20,2,8,128]{3,1,2,0:T(2,128)S(1)}, u32[]{:S(2)}, u32[]{:S(2)}) collective-permute-start(f32[20,2,8,128]{3,1,2,0:T(2,128)S(1)} %get-tuple-element.66), channel_id=1, source_target_pairs={{0,16},{16,32},{32,48},{48,64},{64,80},{80,96},{96,112},{112,128},... | collective-permute-start | bytes 491528 | tf_op jit(solution)/shard_map/ppermute | solution.py:262
  9.5 6.7 %collective-permute-start.1 = (f32[20,2,8,128]{3,1,2,0:T(2,128)S(1)}, f32[20,2,8,128]{3,1,2,0:T(2,128)S(1)}, u32[]{:S(2)}, u32[]{:S(2)}) collective-permute-start(f32[20,2,8,128]{3,1,2,0:T(2,128)S(1)} %get-tuple-element.67), channel_id=1, source_target_pairs={{16,0},{32,16},{48,32},{64,48},{80,64},{96,80},{112,96},{128,112},... | collective-permute-start | bytes 491528 | tf_op jit(solution)/shard_map/ppermute | solution.py:263
  16.3 8.1 %collective-permute-start.2 = (f32[20,8,2,128]{3,1,2,0:T(8,128)S(1)}, f32[20,8,2,128]{3,1,2,0:T(8,128)S(1)}, u32[]{:S(2)}, u32[]{:S(2)}) collective-permute-start(f32[20,8,2,128]{3,1,2,0:T(8,128)S(1)} %get-tuple-element.64), channel_id=1, source_target_pairs={{0,1},{1,2},{2,3},{3,4},{4,5},{5,6},{6,7},{7,8},{8,9},{9,10},{10,1... | collective-permute-start | bytes 491528 | tf_op jit(solution)/shard_map/ppermute | solution.py:262
  21.9 6.6 %collective-permute-start.3 = (f32[20,8,2,128]{3,1,2,0:T(8,128)S(1)}, f32[20,8,2,128]{3,1,2,0:T(8,128)S(1)}, u32[]{:S(2)}, u32[]{:S(2)}) collective-permute-start(f32[20,8,2,128]{3,1,2,0:T(8,128)S(1)} %get-tuple-element.65), channel_id=1, source_target_pairs={{1,0},{2,1},{3,2},{4,3},{5,4},{6,5},{7,6},{8,7},{9,8},{10,9},{11,1... | collective-permute-start | bytes 491528 | tf_op jit(solution)/shard_map/ppermute | solution.py:263
  33.5 1.9 %copy-start = (f32[2,2,1,6,3,7,11,128]{7,3,6,5,4,0,1,2:T(8,128)}, f32[2,2,1,6,3,7,11,128]{7,3,6,5,4,0,1,2:T(8,128)S(1)}, u32[]{:S(2)}) copy-start(f32[2,2,1,6,3,7,11,128]{7,3,6,5,4,0,1,2:T(8,128)S(1)} %get-tuple-element.32) | copy-start | bytes 8515588
  33.6 3.1 %copy-start.2 = (f32[2,2,1,6,3,7,11,128]{7,3,6,5,4,0,1,2:T(8,128)}, f32[2,2,1,6,3,7,11,128]{7,3,6,5,4,0,1,2:T(8,128)S(1)}, u32[]{:S(2)}) copy-start(f32[2,2,1,6,3,7,11,128]{7,3,6,5,4,0,1,2:T(8,128)S(1)} %get-tuple-element.33) | copy-start | bytes 8515588
  33.6 3.1 %copy-start.14 = (f32[2,2,2]{0,1,2:T(2,128)S(1)}, f32[2,2,2]{0,1,2:T(2,128)}, u32[]{:S(2)}) copy-start(f32[2,2,2]{0,1,2:T(2,128)} %constant.253) | copy-start | bytes 100
  33.6 3.0 %copy-start.16 = (f32[2,2,2]{0,1,2:T(2,128)S(1)}, f32[2,2,2]{0,1,2:T(2,128)}, u32[]{:S(2)}) copy-start(f32[2,2,2]{0,1,2:T(2,128)} %constant.254) | copy-start | bytes 100
  33.6 3.0 %copy-start.18 = (f32[2,2,2]{0,1,2:T(2,128)S(1)}, f32[2,2,2]{0,1,2:T(2,128)}, u32[]{:S(2)}) copy-start(f32[2,2,2]{0,1,2:T(2,128)} %constant.255) | copy-start | bytes 100
  36.6 0.7 copy-start.8
  36.6 0.7 copy-start.9
  36.7 0.7 copy-start.10
  36.7 0.7 copy-start.11
  36.7 0.7 copy-start.12
  36.7 0.7 copy-start.13
  54.3 1.8 %copy-start.15 = (f32[2,2,2]{0,1,2:T(2,128)S(1)}, f32[2,2,2]{0,1,2:T(2,128)}, u32[]{:S(2)}) copy-start(f32[2,2,2]{0,1,2:T(2,128)} %constant.253) | copy-start | bytes 100
  54.3 1.8 %copy-start.17 = (f32[2,2,2]{0,1,2:T(2,128)S(1)}, f32[2,2,2]{0,1,2:T(2,128)}, u32[]{:S(2)}) copy-start(f32[2,2,2]{0,1,2:T(2,128)} %constant.254) | copy-start | bytes 100
  54.3 1.8 %copy-start.19 = (f32[2,2,2]{0,1,2:T(2,128)S(1)}, f32[2,2,2]{0,1,2:T(2,128)}, u32[]{:S(2)}) copy-start(f32[2,2,2]{0,1,2:T(2,128)} %constant.255) | copy-start | bytes 100
  57.1 2.1 %copy-start.1 = (f32[2,2,1,6,3,7,11,128]{7,3,6,5,4,0,1,2:T(8,128)S(1)}, f32[2,2,1,6,3,7,11,128]{7,3,6,5,4,0,1,2:T(8,128)}, u32[]{:S(2)}) copy-start(f32[2,2,1,6,3,7,11,128]{7,3,6,5,4,0,1,2:T(8,128)} %copy-done) | copy-start | bytes 8515588
  57.2 3.2 %copy-start.3 = (f32[2,2,1,6,3,7,11,128]{7,3,6,5,4,0,1,2:T(8,128)S(1)}, f32[2,2,1,6,3,7,11,128]{7,3,6,5,4,0,1,2:T(8,128)}, u32[]{:S(2)}) copy-start(f32[2,2,1,6,3,7,11,128]{7,3,6,5,4,0,1,2:T(8,128)} %copy-done.2) | copy-start | bytes 8515588
  70.5 1.7 %copy-start.4 = (f32[2,2,2,6,3,4,8,128]{7,6,5,4,3,2,1,0:T(8,128)S(1)}, f32[2,2,2,6,3,4,8,128]{7,6,5,4,3,2,1,0:T(8,128)}, u32[]{:S(2)}) copy-start(f32[2,2,2,6,3,4,8,128]{7,6,5,4,3,2,1,0:T(8,128)} %copy.218) | copy-start | bytes 7077892
  123.2 0.8 copy-start.6
  123.2 0.8 copy-start.7
  123.3 4.5 %copy-start.5 = (f32[6,3,4,8,128]{4,3,2,1,0:T(8,128)S(1)}, f32[6,3,4,8,128]{4,3,2,1,0:T(8,128)}, u32[]{:S(2)}) copy-start(f32[6,3,4,8,128]{4,3,2,1,0:T(8,128)} %param.34) | copy-start | bytes 884740
  124.1 4.3 %collective-permute-start.4 = (f32[4,8,128]{2,1,0:T(8,128)S(1)}, f32[4,8,128]{2,1,0:T(8,128)S(1)}, u32[]{:S(2)}, u32[]{:S(2)}) collective-permute-start(f32[4,8,128]{2,1,0:T(8,128)S(1)} %fusion.145), channel_id=1, source_target_pairs={{0,16},{16,32},{32,48},{48,64},{64,80},{80,96},{96,112},{112,128},... | collective-permute-start | bytes 49160 | tf_op jit(solution)/shard_map/ppermute | solution.py:29
  126.4 4.5 %collective-permute-start.5 = (f32[4,8,128]{2,1,0:T(8,128)S(1)}, f32[4,8,128]{2,1,0:T(8,128)S(1)}, u32[]{:S(2)}, u32[]{:S(2)}) collective-permute-start(f32[4,8,128]{2,1,0:T(8,128)S(1)} %fusion.145), channel_id=1, source_target_pairs={{16,0},{32,16},{48,32},{64,48},{80,64},{96,80},{112,96},{128,112},... | collective-permute-start | bytes 49160 | tf_op jit(solution)/shard_map/ppermute | solution.py:31
  131.0 9.2 %collective-permute-start.6 = (f32[4,4,128]{2,1,0:T(4,128)S(1)}, f32[4,4,128]{2,1,0:T(4,128)S(1)}, u32[]{:S(2)}, u32[]{:S(2)}) collective-permute-start(f32[4,4,128]{2,1,0:T(4,128)S(1)} %get-tuple-element.73), channel_id=1, source_target_pairs={{0,1},{1,2},{2,3},{3,4},{4,5},{5,6},{6,7},{7,8},{8,9},{9,10},{10,1... | collective-permute-start | bytes 24584 | tf_op jit(solution)/shard_map/ppermute | solution.py:29
  134.9 5.3 %collective-permute-start.7 = (f32[4,4,128]{2,1,0:T(4,128)S(1)}, f32[4,4,128]{2,1,0:T(4,128)S(1)}, u32[]{:S(2)}, u32[]{:S(2)}) collective-permute-start(f32[4,4,128]{2,1,0:T(4,128)S(1)} %get-tuple-element.74), channel_id=1, source_target_pairs={{1,0},{2,1},{3,2},{4,3},{5,4},{6,5},{7,6},{8,7},{9,8},{10,9},{11,1... | collective-permute-start | bytes 24584 | tf_op jit(solution)/shard_map/ppermute | solution.py:31

commit v8 on v6

--- a/solution.py
+++ b/solution.py
@@ -151,7 +151,7 @@
 
 
 def mix_cases(field, coeffs):
-    return jnp.einsum("kabcd,kj->jabcd", field, coeffs, precision=highest)
+    return jnp.sum(field[:, None] * coeffs[:, :, None, None, None, None], axis=0)
 
 
 def solve_spd(matrix, rhs_matrix):
@@ -280,16 +280,21 @@
     fields = case_count * 3
 
     slot_ids = jnp.arange(size_x * size_y, dtype=jnp.int32)
-    matches = (load_nodes[0, 0][:, :, None] == slot_ids).astype(jnp.float32)
-    top_plane = jnp.einsum("cls,ckl->cks", matches, load_forces[0, 0], precision=highest).reshape(
-        fields, size_x, size_y
-    )
+    matches = load_nodes[0, 0][:, None, :, None] == slot_ids
+    top_plane = jnp.sum(
+        jnp.where(matches, load_forces[0, 0][:, :, :, None], 0.0), axis=2
+    ).reshape(fields, size_x, size_y)
     packed_loads = jnp.pad(top_plane.transpose(1, 2, 0), ((0, 0), (0, 0), (0, size_z - fields)))
+    parts = [start_disp.reshape(fields, size_x, size_y, size_z), modulus[None], packed_loads[None]]
+    count = lax.axis_size("gx")
+    head = jnp.concatenate([part[:, :2] for part in parts], axis=0)
+    tail = jnp.concatenate([part[:, -2:] for part in parts], axis=0)
+    below = lax.ppermute(tail, "gx", [(i, i + 1) for i in range(count - 1)])
+    above = lax.ppermute(head, "gx", [(i + 1, i) for i in range(count - 1)])
     packed = jnp.concatenate(
-        [start_disp.reshape(fields, size_x, size_y, size_z), modulus[None], packed_loads[None]],
-        axis=0,
-    )
-    packed = halo_both(halo_both(packed, "gx", 1, 2), "gy", 2, 2)
+        [below, jnp.concatenate(parts, axis=0), above], axis=1
+    )
+    packed = halo_both(packed, "gy", 2, 2)
     wide_start = packed[:fields].reshape(case_count, 3, size_x + 4, size_y + 4, size_z)
     wide_modulus = packed[fields]
     wide_loads = packed[fields + 1, 1:-1, 1:-1, :fields].transpose(2, 0, 1)

time: 125 us -> 126 us (level)
  blocking collectives: 31.6 us -> 12.1 us
  waiting for transfers between devices: 9.78 us -> 20.9 us
  starting transfers between devices: 30.2 us -> 38.9 us
  matrix products: 16.3 us -> 13.4 us
  other arithmetic: 18.3 us -> 20.6 us
  local copies, waits for them, and re-layouts: 14.5 us -> 15.8 us
    all_to_all x2 -> x1, blocking collectives: 31.6 us -> 12.1 us  [tree_sum(): value = jnp.sum(lax.all_to_all(copies, axis, 0, 0, tiled=False), axis=0)]
    ppermute x0 -> x2, starting transfers between devices: none -> 12.6 us  [the longest x1 10.6 us: on_device(): above = lax.ppermute(head, 'gx', [(i + 1, i) for i in range(count - 1)])]
    ppermute x2 -> x1, starting transfers between devices: 10.5 us -> 1.92 us  [halo_both(): above = lax.ppermute(head, axis, [(i + 1, i) for i in range(count - 1)])]
    all_to_all x0 -> x1, starting transfers between devices: none -> 8.41 us  [tree_sum(): value = jnp.sum(lax.all_to_all(copies, axis, 0, 0, tiled=False), axis=0)]
    all_to_all x0 -> x1, waiting for transfers between devices: none -> 6.81 us  [tree_sum(): value = jnp.sum(lax.all_to_all(copies, axis, 0, 0, tiled=False), axis=0)]
    ppermute x0 -> x2, waiting for transfers between devices: none -> 5.37 us  [the longest x1 5.37 us: on_device(): below = lax.ppermute(tail, 'gx', [(i, i + 1) for i in range(count - 1)])]
    ppermute x2 -> x1, starting transfers between devices: 8.64 us -> 4.96 us  [halo_both(): below = lax.ppermute(tail, axis, [(i, i + 1) for i in range(count - 1)])]
    dot_general x3 -> x0, matrix products: 2.87 us -> none  [the longest x2 1.94 us: mix_cases(): return jnp.einsum('kabcd,kj->jabcd', field, coeffs, precision=highest)]
  transfers between devices with their start and end apart: 8 -> 9, of which waited for: 5 -> 5; matrix products, arithmetic and copies ran while one was open for 3% -> 3% of each run, Pallas kernels for 0% -> 0%
where the time goes in v8:
time: 126 us; the launch traced here: 125 us
  starting transfers between devices  38.9 us (31%)
  waiting for transfers between devices  20.9 us (17%)
  other arithmetic  20.6 us (16%)
  local copies, waits for them, and re-layouts  15.8 us (13%)
  matrix products  13.4 us (11%)
  blocking collectives  12.1 us (10%)
  between operations  3.29 us (3%)
    all_to_all x1, blocking collectives, tree_sum(): value = jnp.sum(lax.all_to_all(copies, axis, 0, 0, tiled=False), axis=0)  12.1 us
    ppermute x1, starting transfers between devices, on_device(): above = lax.ppermute(head, 'gx', [(i + 1, i) for i in range(count - 1)])  10.6 us
    dot_general x2, matrix products, node_forces(): jnp.einsum('ij,cjabd->ciabd', stiffness, local_disp, precision=highest)  10.2 us
    all_to_all x1, starting transfers between devices, tree_sum(): value = jnp.sum(lax.all_to_all(copies, axis, 0, 0, tiled=False), axis=0)  8.41 us
    all_to_all x1, waiting for transfers between devices, tree_sum(): value = jnp.sum(lax.all_to_all(copies, axis, 0, 0, tiled=False), axis=0)  6.81 us
    ppermute x2, starting transfers between devices, with_halo(): lax.ppermute(tail, axis, [(i, (i + 1) % count) for i in range(ends)])  6.15 us
    unnamed x31, local copies, waits for them, and re-layouts  5.88 us
    ppermute x1, waiting for transfers between devices, on_device(): below = lax.ppermute(tail, 'gx', [(i, i + 1) for i in range(count - 1)])  5.37 us
  transfers between devices with their start and end apart: 9, of which 5 were waited for; matrix products, arithmetic and copies ran while one was open for 3% of the time, Pallas kernels for 0%

profile of v8, /device:TPU:3, one launch (start us, length us, event | category | flops | bytes accessed | tf_op | source)
XLA Modules:
  0.0 125.0 jit_solution(7758179582909455070)
XLA Ops:
  0.7 0.7 copy.205
  1.4 0.7 copy.204
  2.5 0.8 multiply_multiply_fusion.1
  3.5 1.1 copy.126
  4.8 10.6 %collective-permute-start.1 = (f32[20,2,8,128]{3,1,2,0:T(2,128)S(1)}, f32[20,2,8,128]{3,1,2,0:T(2,128)S(1)}, u32[]{:S(2)}, u32[]{:S(2)}) collective-permute-start(f32[20,2,8,128]{3,1,2,0:T(2,128)S(1)} %pad_maximum_fusion.7), channel_id=1, source_target_pairs={{16,0},{32,16},{48,32},{64,48},{80,64},{96,80},{112,96},{128,112},... | collective-permute-start | bytes 491528 | tf_op jit(solution)/shard_map/ppermute | solution.py:293
  15.6 1.9 %collective-permute-start = (f32[20,2,8,128]{3,1,2,0:T(2,128)S(1)}, f32[20,2,8,128]{3,1,2,0:T(2,128)S(1)}, u32[]{:S(2)}, u32[]{:S(2)}) collective-permute-start(f32[20,2,8,128]{3,1,2,0:T(2,128)S(1)} %pad_maximum_fusion.6), channel_id=1, source_target_pairs={{0,16},{16,32},{32,48},{48,64},{64,80},{80,96},{96,112},{112,128},... | collective-permute-start | bytes 491528 | tf_op jit(solution)/shard_map/ppermute | solution.py:292
  17.6 0.7 and_convert_fusion.1
  18.3 0.7 and_convert_fusion
  19.0 5.4 %collective-permute-done = f32[20,2,8,128]{3,1,2,0:T(2,128)S(1)} collective-permute-done((f32[20,2,8,128]{3,1,2,0:T(2,128)S(1)}, f32[20,2,8,128]{3,1,2,0:T(2,128)S(1)}, u32[]{:S(2)}, u32[]{:S(2)}) %collective-permute-start) | collective-permute-done | bytes 163872 | tf_op jit(solution)/shard_map/ppermute | solution.py:292
  24.4 5.0 %collective-permute-start.2 = (f32[20,8,2,128]{3,1,2,0:T(8,128)S(1)}, f32[20,8,2,128]{3,1,2,0:T(8,128)S(1)}, u32[]{:S(2)}, u32[]{:S(2)}) collective-permute-start(f32[20,8,2,128]{3,1,2,0:T(8,128)S(1)} %get-tuple-element.57), channel_id=1, source_target_pairs={{0,1},{1,2},{2,3},{3,4},{4,5},{5,6},{6,7},{7,8},{8,9},{9,10},{10,1... | collective-permute-start | bytes 491528 | tf_op jit(solution)/shard_map/ppermute | solution.py:246
  29.4 1.9 %collective-permute-start.3 = (f32[20,8,2,128]{3,1,2,0:T(8,128)S(1)}, f32[20,8,2,128]{3,1,2,0:T(8,128)S(1)}, u32[]{:S(2)}, u32[]{:S(2)}) collective-permute-start(f32[20,8,2,128]{3,1,2,0:T(8,128)S(1)} %get-tuple-element.58), channel_id=1, source_target_pairs={{1,0},{2,1},{3,2},{4,3},{5,4},{6,5},{7,6},{8,7},{9,8},{10,9},{11,1... | collective-permute-start | bytes 491528 | tf_op jit(solution)/shard_map/ppermute | solution.py:247
  31.7 4.4 %collective-permute-done.3 = f32[20,8,2,128]{3,1,2,0:T(8,128)S(1)} collective-permute-done((f32[20,8,2,128]{3,1,2,0:T(8,128)S(1)}, f32[20,8,2,128]{3,1,2,0:T(8,128)S(1)}, u32[]{:S(2)}, u32[]{:S(2)}) %collective-permute-start.3) | collective-permute-done | bytes 163872 | tf_op jit(solution)/shard_map/ppermute | solution.py:247
  36.6 0.5 copy.133
  37.1 1.0 copy.152
  39.6 1.1 copy.139
  40.7 7.0 %broadcast_multiply_fusion = (f32[6,24,7,11,128]{4,1,3,2,0:T(8,128)S(1)}, f32[6,24,7,11,128]{4,1,3,2,0:T(8,128)}) fusion(f32[7,11,128]{2,1,0:T(8,128)S(1)} %copy.140, f32[6,24,7,11,128]{4,1,3,2,0:T(8,128)S(1)} %copy.139, f32[24,24,1,1,1]{1,0,4,3,2:T(8,128)S(1)} %copy-done.3), kind=kOutput, calls=%fused_computation.10 | convolution fusion | flops 410167296 | bytes 17072896 | tf_op jit(solution)/shard_map/ij,cjabd->ciabd/dot_general | solution.py:259
  47.7 1.5 %copy.177 = f32[6,24,7,11,128]{4,0,3,2,1:T(8,128)S(1)} copy(f32[6,24,7,11,128]{4,1,3,2,0:T(8,128)S(1)} %get-tuple-element.76) | data formatting | bytes 11354112 | tf_op jit(solution)/shard_map/reshape | solution.py:260
  49.2 0.5 slice_bitcast_fusion.5
  49.7 0.9 fusion.29
  51.3 1.0 fusion.8
  53.7 0.5 copy.164
  54.2 3.2 %broadcast_multiply_fusion.1 = (f32[6,24,5,9,128]{4,1,3,2,0:T(8,128)S(1)}, f32[6,24,5,9,128]{4,1,3,2,0:T(8,128)S(1)}) fusion(f32[5,9,128]{2,1,0:T(8,128)S(1)} %copy.155, f32[24,24,1,1,1]{1,0,4,3,2:T(8,128)S(1)} %copy-done.3, f32[6,24,5,9,128]{4,0,3,2,1:T(8,128)S(1)} %bitcast.196), kind=kOutput, calls=%fused_computation.26 | convolution fusion | flops 239708160 | bytes 9978624 | tf_op jit(solution)/shard_map/ij,cjabd->ciabd/dot_general | solution.py:259
  57.4 0.9 copy.186
  58.6 2.6 %fusion.3 = (f32[6]{0:T(128)S(1)}, f32[6,24,4,8,128]{4,1,3,2,0:T(8,128)S(1)}, f32[6,24,4,8,128]{4,1,3,2,0:T(8,128)S(1)}) fusion(f32[6,24,7,11,128]{4,1,3,2,0:T(8,128)S(1)} %copy.139, f32[6,24,7,11,128]{4,1,3,2,0:T(8,128)} %get-tuple-element.77, f32[4,8,128]{2,1,0:T(8,128)S(1)} %get-tuple-element.66, f32[6,24,5,9,128]{4,1,3,2,0:T(8,128)S(1)} %get-tuple-element.79), kind=kLoop, calls=%fused_computation.19 | loop fusion | flops 2949114 | bytes 11812888 | tf_op jit(solution)/shard_map/reduce_sum | solution.py:344
  62.0 2.9 %multiply_reduce_fusion = (f32[6,6]{1,0:T(8,128)S(1)}, f32[6,6]{1,0:T(8,128)S(1)}) fusion(f32[6,24,4,8,128]{4,3,2,1,0:T(8,128)S(1)} %copy.166, f32[6,24,4,8,128]{4,3,2,1,0:T(8,128)S(1)} %copy.164, f32[6,24,4,8,128]{4,3,2,1,0:T(8,128)S(1)} %copy.165), kind=kLoop, calls=%fused_computation | loop fusion | flops 14155704 | bytes 7078176 | tf_op jit(solution)/shard_map/reduce_sum | solution.py:350
  64.9 1.2 fusion.7
  66.6 12.1 %all_to_all.10 = f32[32,1,180]{2,1,0:T(1,128)S(1)} all-to-all(f32[32,1,180]{2,1,0:T(1,128)S(1)} %reshape.326), channel_id=1, replica_groups=mesh['gx'=32,'gy'=16] {'gx'}, dimensions={0} | all-to-all | bytes 46080 | tf_op jit(solution)/shard_map/all_to_all | solution.py:149
  78.6 0.5 broadcast.986
  79.2 0.7 reduce.7
  80.2 0.8 reshape.328
  81.0 8.4 %all-to-all-start.1 = ((f32[16,1,180]{2,1,0:T(1,128)}), f32[16,1,180]{2,1,0:T(1,128)S(1)}, u32[]{:S(2)}, u32[]{:S(2)}) async-start(f32[16,1,180]{2,1,0:T(1,128)} %reshape.328), calls=%async_computation.1 | async-start | bytes 32768 | tf_op jit(solution)/shard_map/all_to_all | solution.py:149
  89.9 6.8 %all-to-all-done.1 = f32[16,1,180]{2,1,0:T(1,128)S(1)} async-done(((f32[16,1,180]{2,1,0:T(1,128)}), f32[16,1,180]{2,1,0:T(1,128)S(1)}, u32[]{:S(2)}, u32[]{:S(2)}) %all-to-all-start.1) | async-done | bytes 11552 | tf_op jit(solution)/shard_map/all_to_all | solution.py:149
  96.7 0.7 reduce.8
  97.6 0.6 slice_bitcast_fusion.24
  98.3 0.5 cholesky.15
  98.9 0.6 compare_reduce_fusion
  99.5 0.6 fusion.127
  100.2 0.5 custom-call.8
  100.8 0.8 fusion.129
  101.7 0.9 multiply_reduce_fusion.2
  105.3 3.0 %collective-permute-start.5 = (f32[4,8,128]{2,1,0:T(8,128)S(1)}, f32[4,8,128]{2,1,0:T(8,128)S(1)}, u32[]{:S(2)}, u32[]{:S(2)}) collective-permute-start(f32[4,8,128]{2,1,0:T(8,128)S(1)} %add_multiply_fusion), channel_id=1, source_target_pairs={{16,0},{32,16},{48,32},{64,48},{80,64},{96,80},{112,96},{128,112},... | collective-permute-start | bytes 49160 | tf_op jit(solution)/shard_map/ppermute | solution.py:31
  108.4 2.3 %collective-permute-start.4 = (f32[4,8,128]{2,1,0:T(8,128)S(1)}, f32[4,8,128]{2,1,0:T(8,128)S(1)}, u32[]{:S(2)}, u32[]{:S(2)}) collective-permute-start(f32[4,8,128]{2,1,0:T(8,128)S(1)} %add_multiply_fusion), channel_id=1, source_target_pairs={{0,16},{16,32},{32,48},{48,64},{64,80},{80,96},{96,112},{112,128},... | collective-permute-start | bytes 49160 | tf_op jit(solution)/shard_map/ppermute | solution.py:29
  110.9 4.1 %collective-permute-done.4 = f32[4,8,128]{2,1,0:T(8,128)S(1)} collective-permute-done((f32[4,8,128]{2,1,0:T(8,128)S(1)}, f32[4,8,128]{2,1,0:T(8,128)S(1)}, u32[]{:S(2)}, u32[]{:S(2)}) %collective-permute-start.4) | collective-permute-done | bytes 16416 | tf_op jit(solution)/shard_map/ppermute | solution.py:29
  115.0 3.9 %collective-permute-start.6 = (f32[4,4,128]{2,1,0:T(4,128)S(1)}, f32[4,4,128]{2,1,0:T(4,128)S(1)}, u32[]{:S(2)}, u32[]{:S(2)}) collective-permute-start(f32[4,4,128]{2,1,0:T(4,128)S(1)} %get-tuple-element.71), channel_id=1, source_target_pairs={{0,1},{1,2},{2,3},{3,4},{4,5},{5,6},{6,7},{7,8},{8,9},{9,10},{10,1... | collective-permute-start | bytes 24584 | tf_op jit(solution)/shard_map/ppermute | solution.py:29
  118.9 1.9 %collective-permute-start.7 = (f32[4,4,128]{2,1,0:T(4,128)S(1)}, f32[4,4,128]{2,1,0:T(4,128)S(1)}, u32[]{:S(2)}, u32[]{:S(2)}) collective-permute-start(f32[4,4,128]{2,1,0:T(4,128)S(1)} %get-tuple-element.72), channel_id=1, source_target_pairs={{1,0},{2,1},{3,2},{4,3},{5,4},{6,5},{7,6},{8,7},{9,8},{10,9},{11,1... | collective-permute-start | bytes 24584 | tf_op jit(solution)/shard_map/ppermute | solution.py:31
  120.8 0.7 multiply_reduce_fusion.5
  121.5 0.8 add.785
  124.2 0.7 multiply_minimum_fusion
  (104 shorter events, 11.3 us)
Async XLA Ops:
  4.8 14.2 %collective-permute-start.1 = (f32[20,2,8,128]{3,1,2,0:T(2,128)S(1)}, f32[20,2,8,128]{3,1,2,0:T(2,128)S(1)}, u32[]{:S(2)}, u32[]{:S(2)}) collective-permute-start(f32[20,2,8,128]{3,1,2,0:T(2,128)S(1)} %pad_maximum_fusion.7), channel_id=1, source_target_pairs={{16,0},{32,16},{48,32},{64,48},{80,64},{96,80},{112,96},{128,112},... | collective-permute-start | bytes 491528 | tf_op jit(solution)/shard_map/ppermute | solution.py:293
  15.6 8.8 %collective-permute-start = (f32[20,2,8,128]{3,1,2,0:T(2,128)S(1)}, f32[20,2,8,128]{3,1,2,0:T(2,128)S(1)}, u32[]{:S(2)}, u32[]{:S(2)}) collective-permute-start(f32[20,2,8,128]{3,1,2,0:T(2,128)S(1)} %pad_maximum_fusion.6), channel_id=1, source_target_pairs={{0,16},{16,32},{32,48},{48,64},{64,80},{80,96},{96,112},{112,128},... | collective-permute-start | bytes 491528 | tf_op jit(solution)/shard_map/ppermute | solution.py:292
  24.4 7.2 %collective-permute-start.2 = (f32[20,8,2,128]{3,1,2,0:T(8,128)S(1)}, f32[20,8,2,128]{3,1,2,0:T(8,128)S(1)}, u32[]{:S(2)}, u32[]{:S(2)}) collective-permute-start(f32[20,8,2,128]{3,1,2,0:T(8,128)S(1)} %get-tuple-element.57), channel_id=1, source_target_pairs={{0,1},{1,2},{2,3},{3,4},{4,5},{5,6},{6,7},{7,8},{8,9},{9,10},{10,1... | collective-permute-start | bytes 491528 | tf_op jit(solution)/shard_map/ppermute | solution.py:246
  29.4 6.6 %collective-permute-start.3 = (f32[20,8,2,128]{3,1,2,0:T(8,128)S(1)}, f32[20,8,2,128]{3,1,2,0:T(8,128)S(1)}, u32[]{:S(2)}, u32[]{:S(2)}) collective-permute-start(f32[20,8,2,128]{3,1,2,0:T(8,128)S(1)} %get-tuple-element.58), channel_id=1, source_target_pairs={{1,0},{2,1},{3,2},{4,3},{5,4},{6,5},{7,6},{8,7},{9,8},{10,9},{11,1... | collective-permute-start | bytes 491528 | tf_op jit(solution)/shard_map/ppermute | solution.py:247
  39.6 1.1 copy-start.3
  81.0 15.7 %all-to-all-start.1 = ((f32[16,1,180]{2,1,0:T(1,128)}), f32[16,1,180]{2,1,0:T(1,128)S(1)}, u32[]{:S(2)}, u32[]{:S(2)}) async-start(f32[16,1,180]{2,1,0:T(1,128)} %reshape.328), calls=%async_computation.1 | async-start | bytes 32768 | tf_op jit(solution)/shard_map/all_to_all | solution.py:149
  104.2 1.1 copy-start.1
  104.2 1.1 copy-start.2
  104.4 17.1 %copy-start = (f32[6,3,4,8,128]{4,3,2,1,0:T(8,128)S(1)}, f32[6,3,4,8,128]{4,3,2,1,0:T(8,128)}, u32[]{:S(2)}) copy-start(f32[6,3,4,8,128]{4,3,2,1,0:T(8,128)} %param.8) | copy-start | bytes 884740
  105.3 5.5 %collective-permute-start.5 = (f32[4,8,128]{2,1,0:T(8,128)S(1)}, f32[4,8,128]{2,1,0:T(8,128)S(1)}, u32[]{:S(2)}, u32[]{:S(2)}) collective-permute-start(f32[4,8,128]{2,1,0:T(8,128)S(1)} %add_multiply_fusion), channel_id=1, source_target_pairs={{16,0},{32,16},{48,32},{64,48},{80,64},{96,80},{112,96},{128,112},... | collective-permute-start | bytes 49160 | tf_op jit(solution)/shard_map/ppermute | solution.py:31
  108.4 6.6 %collective-permute-start.4 = (f32[4,8,128]{2,1,0:T(8,128)S(1)}, f32[4,8,128]{2,1,0:T(8,128)S(1)}, u32[]{:S(2)}, u32[]{:S(2)}) collective-permute-start(f32[4,8,128]{2,1,0:T(8,128)S(1)} %add_multiply_fusion), channel_id=1, source_target_pairs={{0,16},{16,32},{32,48},{48,64},{64,80},{80,96},{96,112},{112,128},... | collective-permute-start | bytes 49160 | tf_op jit(solution)/shard_map/ppermute | solution.py:29
  115.0 9.2 %collective-permute-start.6 = (f32[4,4,128]{2,1,0:T(4,128)S(1)}, f32[4,4,128]{2,1,0:T(4,128)S(1)}, u32[]{:S(2)}, u32[]{:S(2)}) collective-permute-start(f32[4,4,128]{2,1,0:T(4,128)S(1)} %get-tuple-element.71), channel_id=1, source_target_pairs={{0,1},{1,2},{2,3},{3,4},{4,5},{5,6},{6,7},{7,8},{8,9},{9,10},{10,1... | collective-permute-start | bytes 24584 | tf_op jit(solution)/shard_map/ppermute | solution.py:29
  118.9 5.3 %collective-permute-start.7 = (f32[4,4,128]{2,1,0:T(4,128)S(1)}, f32[4,4,128]{2,1,0:T(4,128)S(1)}, u32[]{:S(2)}, u32[]{:S(2)}) collective-permute-start(f32[4,4,128]{2,1,0:T(4,128)S(1)} %get-tuple-element.72), channel_id=1, source_target_pairs={{1,0},{2,1},{3,2},{4,3},{5,4},{6,5},{7,6},{8,7},{9,8},{10,9},{11,1... | collective-permute-start | bytes 24584 | tf_op jit(solution)/shard_map/ppermute | solution.py:31

commit v9 on v6

--- a/solution.py
+++ b/solution.py
@@ -337,13 +337,12 @@
     residual_elems = residual_elems[:, :, 1:, 1:]
     residual_loads = residual_loads[:, :, 1:, 1:]
     start_energy = jnp.sum(start_elems * start_loads * blur_mass, axis=(1, 2, 3, 4))
-    start_weighted = start_loads * blur_mass
-    residual_weighted = residual_loads * blur_mass
+    residual_scaled = residual_elems * blur_mass
     cross_energy = jnp.sum(
-        residual_elems[:, None] * start_weighted[None, :], axis=(2, 3, 4, 5)
+        residual_scaled[:, None] * start_loads[None, :], axis=(2, 3, 4, 5)
     )
     residual_energy = jnp.sum(
-        residual_elems[:, None] * residual_weighted[None, :], axis=(2, 3, 4, 5)
+        residual_scaled[:, None] * residual_loads[None, :], axis=(2, 3, 4, 5)
     )
     grams = tree_sum(
         jnp.stack(

time: 125 us -> 125 us (level)
  no operation moved by 1% of the time
where the time goes in v9:
time: 125 us; the launch traced here: 124 us
  blocking collectives  31.6 us (25%)
  starting transfers between devices  30.2 us (24%)
  other arithmetic  18.1 us (14%)
  matrix products  16 us (13%)
  local copies, waits for them, and re-layouts  14.9 us (12%)
  waiting for transfers between devices  9.78 us (8%)
  between operations  3.23 us (3%)
    all_to_all x2, blocking collectives, tree_sum(): value = jnp.sum(lax.all_to_all(copies, axis, 0, 0, tiled=False), axis=0)  31.6 us
    ppermute x2, starting transfers between devices, halo_both(): above = lax.ppermute(head, axis, [(i + 1, i) for i in range(count - 1)])  10.5 us
    dot_general x2, matrix products, node_forces(): jnp.einsum('ij,cjabd->ciabd', stiffness, local_disp, precision=highest)  9.98 us
    ppermute x2, starting transfers between devices, halo_both(): below = lax.ppermute(tail, axis, [(i, i + 1) for i in range(count - 1)])  8.64 us
    ppermute x2, starting transfers between devices, with_halo(): lax.ppermute(tail, axis, [(i, (i + 1) % count) for i in range(ends)])  6.15 us
    unnamed x31, local copies, waits for them, and re-layouts  5.35 us
    ppermute x2, waiting for transfers between devices, halo_both(): above = lax.ppermute(head, axis, [(i + 1, i) for i in range(count - 1)])  5.26 us
    ppermute x2, starting transfers between devices, with_halo(): lax.ppermute(head, axis, [((i + 1) % count, i) for i in range(ends)])  4.95 us
  transfers between devices with their start and end apart: 8, of which 5 were waited for; matrix products, arithmetic and copies ran while one was open for 3% of the time, Pallas kernels for 0%

profile of v9, /device:TPU:3, one launch (start us, length us, event | category | flops | bytes accessed | tf_op | source)
XLA Modules:
  0.0 123.9 jit_solution(9170998352288393089)
XLA Ops:
  0.7 0.7 copy.215
  1.4 0.9 convolution_bitcast_fusion.2
  2.4 0.8 multiply_multiply_fusion.1
  3.4 1.1 copy.144
  4.7 4.0 %collective-permute-start = (f32[20,2,8,128]{3,1,2,0:T(2,128)S(1)}, f32[20,2,8,128]{3,1,2,0:T(2,128)S(1)}, u32[]{:S(2)}, u32[]{:S(2)}) collective-permute-start(f32[20,2,8,128]{3,1,2,0:T(2,128)S(1)} %get-tuple-element.68), channel_id=1, source_target_pairs={{0,16},{16,32},{32,48},{48,64},{64,80},{80,96},{96,112},{112,128},... | collective-permute-start | bytes 491528 | tf_op jit(solution)/shard_map/ppermute | solution.py:246
  8.7 8.6 %collective-permute-start.1 = (f32[20,2,8,128]{3,1,2,0:T(2,128)S(1)}, f32[20,2,8,128]{3,1,2,0:T(2,128)S(1)}, u32[]{:S(2)}, u32[]{:S(2)}) collective-permute-start(f32[20,2,8,128]{3,1,2,0:T(2,128)S(1)} %get-tuple-element.69), channel_id=1, source_target_pairs={{16,0},{32,16},{48,32},{64,48},{80,64},{96,80},{112,96},{128,112},... | collective-permute-start | bytes 491528 | tf_op jit(solution)/shard_map/ppermute | solution.py:247
  17.2 0.7 and_convert_fusion.1
  17.9 0.7 and_convert_fusion
  18.6 0.7 collective-permute-done
  19.2 0.9 collective-permute-done.1
  20.2 4.6 %collective-permute-start.2 = (f32[20,8,2,128]{3,1,2,0:T(8,128)S(1)}, f32[20,8,2,128]{3,1,2,0:T(8,128)S(1)}, u32[]{:S(2)}, u32[]{:S(2)}) collective-permute-start(f32[20,8,2,128]{3,1,2,0:T(8,128)S(1)} %get-tuple-element.63), channel_id=1, source_target_pairs={{0,1},{1,2},{2,3},{3,4},{4,5},{5,6},{6,7},{7,8},{8,9},{9,10},{10,1... | collective-permute-start | bytes 491528 | tf_op jit(solution)/shard_map/ppermute | solution.py:246
  24.8 1.9 %collective-permute-start.3 = (f32[20,8,2,128]{3,1,2,0:T(8,128)S(1)}, f32[20,8,2,128]{3,1,2,0:T(8,128)S(1)}, u32[]{:S(2)}, u32[]{:S(2)}) collective-permute-start(f32[20,8,2,128]{3,1,2,0:T(8,128)S(1)} %get-tuple-element.64), channel_id=1, source_target_pairs={{1,0},{2,1},{3,2},{4,3},{5,4},{6,5},{7,6},{8,7},{9,8},{10,9},{11,1... | collective-permute-start | bytes 491528 | tf_op jit(solution)/shard_map/ppermute | solution.py:247
  27.1 4.4 %collective-permute-done.3 = f32[20,8,2,128]{3,1,2,0:T(8,128)S(1)} collective-permute-done((f32[20,8,2,128]{3,1,2,0:T(8,128)S(1)}, f32[20,8,2,128]{3,1,2,0:T(8,128)S(1)}, u32[]{:S(2)}, u32[]{:S(2)}) %collective-permute-start.3) | collective-permute-done | bytes 163872 | tf_op jit(solution)/shard_map/ppermute | solution.py:247
  32.0 0.5 copy.147
  32.5 1.0 copy.166
  35.1 1.1 copy.153
  36.2 7.0 %broadcast_multiply_fusion = (f32[6,24,7,11,128]{4,1,3,2,0:T(8,128)S(1)}, f32[6,24,7,11,128]{4,1,3,2,0:T(8,128)}) fusion(f32[7,11,128]{2,1,0:T(8,128)S(1)} %copy.154, f32[6,24,7,11,128]{4,1,3,2,0:T(8,128)S(1)} %copy.153, f32[24,24,1,1,1]{1,0,4,3,2:T(8,128)S(1)} %copy-done.3), kind=kOutput, calls=%fused_computation.7 | convolution fusion | flops 410167296 | bytes 17072896 | tf_op jit(solution)/shard_map/ij,cjabd->ciabd/dot_general | solution.py:259
  43.2 1.5 %copy.188 = f32[6,24,7,11,128]{4,0,3,2,1:T(8,128)S(1)} copy(f32[6,24,7,11,128]{4,1,3,2,0:T(8,128)S(1)} %get-tuple-element.78) | data formatting | bytes 11354112 | tf_op jit(solution)/shard_map/reshape | solution.py:260
  44.6 0.5 slice_bitcast_fusion.5
  45.1 0.9 fusion.23
  46.7 1.0 fusion.3
  48.7 0.6 copy.196
  49.4 2.5 %fusion.1 = (f32[6]{0:T(128)S(1)}, f32[6,24,4,8,128]{4,1,3,2,0:T(8,128)S(1)}, f32[6,24,4,8,128]{4,1,3,2,0:T(8,128)S(1)}) fusion(f32[6,24,7,11,128]{4,1,3,2,0:T(8,128)S(1)} %copy.153, f32[4,8,128]{2,1,0:T(8,128)S(1)} %get-tuple-element.70, f32[6,24,7,11,128]{4,1,3,2,0:T(8,128)} %get-tuple-element.79, f32[6,24,5,9,128]{4,1,3,2,0:T(8,128)S(1)} %copy.196), kind=kLoop, calls=%fused_computation.16 | loop fusion | flops 2359290 | bytes 11812888 | tf_op jit(solution)/shard_map/reduce_sum | solution.py:339
  52.7 3.0 %broadcast_multiply_fusion.1 = (f32[6,24,5,9,128]{4,1,3,2,0:T(8,128)S(1)}, f32[6,24,5,9,128]{4,1,3,2,0:T(8,128)S(1)}) fusion(f32[5,9,128]{2,1,0:T(8,128)S(1)} %copy.168, f32[6,24,5,9,128]{4,1,3,2,0:T(8,128)S(1)} %copy.196, f32[24,24,1,1,1]{1,0,4,3,2:T(8,128)S(1)} %copy-done.3), kind=kOutput, calls=%fused_computation.21 | convolution fusion | flops 239708160 | bytes 9978624 | tf_op jit(solution)/shard_map/ij,cjabd->ciabd/dot_general | solution.py:259
  55.7 0.9 copy.169
  57.5 2.9 %multiply_reduce_fusion = (f32[6,6]{1,0:T(8,128)S(1)}, f32[6,6]{1,0:T(8,128)S(1)}) fusion(f32[6,24,4,8,128]{4,3,2,1,0:T(8,128)S(1)} %copy.172, f32[6,24,4,8,128]{4,3,2,1,0:T(8,128)S(1)} %copy.170, f32[6,24,4,8,128]{4,3,2,1,0:T(8,128)S(1)} %copy.171), kind=kLoop, calls=%fused_computation | loop fusion | flops 14155704 | bytes 7078176 | tf_op jit(solution)/shard_map/reduce_sum | solution.py:344
  60.4 1.2 fusion.2
  62.1 16.1 %all_to_all.10 = f32[32,1,180]{2,1,0:T(1,128)S(1)} all-to-all(f32[32,1,180]{2,1,0:T(1,128)S(1)} %reshape.317), channel_id=1, replica_groups=mesh['gx'=32,'gy'=16] {'gx'}, dimensions={0} | all-to-all | bytes 46080 | tf_op jit(solution)/shard_map/all_to_all | solution.py:149
  78.2 0.5 broadcast.970
  78.7 0.7 reduce.7
  79.9 15.5 %all_to_all.11 = f32[16,1,180]{2,1,0:T(1,128)S(1)} all-to-all(f32[16,1,180]{2,1,0:T(1,128)S(1)} %reshape.319), channel_id=1, replica_groups=mesh['gx'=32,'gy'=16] {'gy'}, dimensions={0} | all-to-all | bytes 23040 | tf_op jit(solution)/shard_map/all_to_all | solution.py:149
  95.5 0.7 reduce.8
  96.3 0.6 slice_bitcast_fusion.24
  97.0 0.5 cholesky.15
  97.6 0.6 compare_reduce_fusion
  98.2 0.6 fusion.127
  98.9 0.5 custom-call.8
  99.6 0.8 fusion.129
  100.4 1.3 %convolution_add_fusion = f32[6,3,5,9,129]{4,0,3,2,1:T(8,128)S(1)} fusion(f32[6,3,6,10,128]{4,0,3,2,1:T(8,128)S(1)} %maximum_multiply_fusion, f32[6,3,8,12,128]{4,0,3,2,1:T(8,128)S(1)} %copy.147, f32[6,6]{1,0:T(8,128)S(1)} %get-tuple-element.83), kind=kOutput, calls=%fused_computation.24 | convolution fusion | flops 7627770 | bytes 1855800 | tf_op jit(solution)/shard_map/kabcd,kj->jabcd/dot_general | solution.py:154
  104.3 3.0 %collective-permute-start.5 = (f32[4,8,128]{2,1,0:T(8,128)S(1)}, f32[4,8,128]{2,1,0:T(8,128)S(1)}, u32[]{:S(2)}, u32[]{:S(2)}) collective-permute-start(f32[4,8,128]{2,1,0:T(8,128)S(1)} %add_multiply_fusion), channel_id=1, source_target_pairs={{16,0},{32,16},{48,32},{64,48},{80,64},{96,80},{112,96},{128,112},... | collective-permute-start | bytes 49160 | tf_op jit(solution)/shard_map/ppermute | solution.py:31
  107.3 2.3 %collective-permute-start.4 = (f32[4,8,128]{2,1,0:T(8,128)S(1)}, f32[4,8,128]{2,1,0:T(8,128)S(1)}, u32[]{:S(2)}, u32[]{:S(2)}) collective-permute-start(f32[4,8,128]{2,1,0:T(8,128)S(1)} %add_multiply_fusion), channel_id=1, source_target_pairs={{0,16},{16,32},{32,48},{48,64},{64,80},{80,96},{96,112},{112,128},... | collective-permute-start | bytes 49160 | tf_op jit(solution)/shard_map/ppermute | solution.py:29
  109.6 0.7 convolution_add_fusion.1
  110.3 3.6 %collective-permute-done.4 = f32[4,8,128]{2,1,0:T(8,128)S(1)} collective-permute-done((f32[4,8,128]{2,1,0:T(8,128)S(1)}, f32[4,8,128]{2,1,0:T(8,128)S(1)}, u32[]{:S(2)}, u32[]{:S(2)}) %collective-permute-start.4) | collective-permute-done | bytes 16416 | tf_op jit(solution)/shard_map/ppermute | solution.py:29
  114.0 3.9 %collective-permute-start.6 = (f32[4,4,128]{2,1,0:T(4,128)S(1)}, f32[4,4,128]{2,1,0:T(4,128)S(1)}, u32[]{:S(2)}, u32[]{:S(2)}) collective-permute-start(f32[4,4,128]{2,1,0:T(4,128)S(1)} %get-tuple-element.75), channel_id=1, source_target_pairs={{0,1},{1,2},{2,3},{3,4},{4,5},{5,6},{6,7},{7,8},{8,9},{9,10},{10,1... | collective-permute-start | bytes 24584 | tf_op jit(solution)/shard_map/ppermute | solution.py:29
  117.9 1.9 %collective-permute-start.7 = (f32[4,4,128]{2,1,0:T(4,128)S(1)}, f32[4,4,128]{2,1,0:T(4,128)S(1)}, u32[]{:S(2)}, u32[]{:S(2)}) collective-permute-start(f32[4,4,128]{2,1,0:T(4,128)S(1)} %get-tuple-element.76), channel_id=1, source_target_pairs={{1,0},{2,1},{3,2},{4,3},{5,4},{6,5},{7,6},{8,7},{9,8},{10,9},{11,1... | collective-permute-start | bytes 24584 | tf_op jit(solution)/shard_map/ppermute | solution.py:31
  119.8 0.7 multiply_reduce_fusion.3
  120.5 0.8 copy.181
  123.2 0.7 multiply_minimum_fusion
  (90 shorter events, 10.3 us)
Async XLA Ops:
  4.7 14.6 %collective-permute-start = (f32[20,2,8,128]{3,1,2,0:T(2,128)S(1)}, f32[20,2,8,128]{3,1,2,0:T(2,128)S(1)}, u32[]{:S(2)}, u32[]{:S(2)}) collective-permute-start(f32[20,2,8,128]{3,1,2,0:T(2,128)S(1)} %get-tuple-element.68), channel_id=1, source_target_pairs={{0,16},{16,32},{32,48},{48,64},{64,80},{80,96},{96,112},{112,128},... | collective-permute-start | bytes 491528 | tf_op jit(solution)/shard_map/ppermute | solution.py:246
  8.7 11.4 %collective-permute-start.1 = (f32[20,2,8,128]{3,1,2,0:T(2,128)S(1)}, f32[20,2,8,128]{3,1,2,0:T(2,128)S(1)}, u32[]{:S(2)}, u32[]{:S(2)}) collective-permute-start(f32[20,2,8,128]{3,1,2,0:T(2,128)S(1)} %get-tuple-element.69), channel_id=1, source_target_pairs={{16,0},{32,16},{48,32},{64,48},{80,64},{96,80},{112,96},{128,112},... | collective-permute-start | bytes 491528 | tf_op jit(solution)/shard_map/ppermute | solution.py:247
  20.2 6.9 %collective-permute-start.2 = (f32[20,8,2,128]{3,1,2,0:T(8,128)S(1)}, f32[20,8,2,128]{3,1,2,0:T(8,128)S(1)}, u32[]{:S(2)}, u32[]{:S(2)}) collective-permute-start(f32[20,8,2,128]{3,1,2,0:T(8,128)S(1)} %get-tuple-element.63), channel_id=1, source_target_pairs={{0,1},{1,2},{2,3},{3,4},{4,5},{5,6},{6,7},{7,8},{8,9},{9,10},{10,1... | collective-permute-start | bytes 491528 | tf_op jit(solution)/shard_map/ppermute | solution.py:246
  24.8 6.6 %collective-permute-start.3 = (f32[20,8,2,128]{3,1,2,0:T(8,128)S(1)}, f32[20,8,2,128]{3,1,2,0:T(8,128)S(1)}, u32[]{:S(2)}, u32[]{:S(2)}) collective-permute-start(f32[20,8,2,128]{3,1,2,0:T(8,128)S(1)} %get-tuple-element.64), channel_id=1, source_target_pairs={{1,0},{2,1},{3,2},{4,3},{5,4},{6,5},{7,6},{8,7},{9,8},{10,9},{11,1... | collective-permute-start | bytes 491528 | tf_op jit(solution)/shard_map/ppermute | solution.py:247
  35.1 1.1 copy-start.3
  103.1 1.1 copy-start.1
  103.1 1.1 copy-start.2
  103.1 6.5 %copy-start = (f32[6,3,4,8,128]{4,3,2,1,0:T(8,128)S(1)}, f32[6,3,4,8,128]{4,3,2,1,0:T(8,128)}, u32[]{:S(2)}) copy-start(f32[6,3,4,8,128]{4,3,2,1,0:T(8,128)} %param.8) | copy-start | bytes 884740
  104.3 6.0 %collective-permute-start.5 = (f32[4,8,128]{2,1,0:T(8,128)S(1)}, f32[4,8,128]{2,1,0:T(8,128)S(1)}, u32[]{:S(2)}, u32[]{:S(2)}) collective-permute-start(f32[4,8,128]{2,1,0:T(8,128)S(1)} %add_multiply_fusion), channel_id=1, source_target_pairs={{16,0},{32,16},{48,32},{64,48},{80,64},{96,80},{112,96},{128,112},... | collective-permute-start | bytes 49160 | tf_op jit(solution)/shard_map/ppermute | solution.py:31
  107.3 6.6 %collective-permute-start.4 = (f32[4,8,128]{2,1,0:T(8,128)S(1)}, f32[4,8,128]{2,1,0:T(8,128)S(1)}, u32[]{:S(2)}, u32[]{:S(2)}) collective-permute-start(f32[4,8,128]{2,1,0:T(8,128)S(1)} %add_multiply_fusion), channel_id=1, source_target_pairs={{0,16},{16,32},{32,48},{48,64},{64,80},{80,96},{96,112},{112,128},... | collective-permute-start | bytes 49160 | tf_op jit(solution)/shard_map/ppermute | solution.py:29
  114.0 9.2 %collective-permute-start.6 = (f32[4,4,128]{2,1,0:T(4,128)S(1)}, f32[4,4,128]{2,1,0:T(4,128)S(1)}, u32[]{:S(2)}, u32[]{:S(2)}) collective-permute-start(f32[4,4,128]{2,1,0:T(4,128)S(1)} %get-tuple-element.75), channel_id=1, source_target_pairs={{0,1},{1,2},{2,3},{3,4},{4,5},{5,6},{6,7},{7,8},{8,9},{9,10},{10,1... | collective-permute-start | bytes 24584 | tf_op jit(solution)/shard_map/ppermute | solution.py:29
  117.9 5.3 %collective-permute-start.7 = (f32[4,4,128]{2,1,0:T(4,128)S(1)}, f32[4,4,128]{2,1,0:T(4,128)S(1)}, u32[]{:S(2)}, u32[]{:S(2)}) collective-permute-start(f32[4,4,128]{2,1,0:T(4,128)S(1)} %get-tuple-element.76), channel_id=1, source_target_pairs={{1,0},{2,1},{3,2},{4,3},{5,4},{6,5},{7,6},{8,7},{9,8},{10,9},{11,1... | collective-permute-start | bytes 24584 | tf_op jit(solution)/shard_map/ppermute | solution.py:31

commit v10 on v9

--- a/solution.py
+++ b/solution.py
@@ -280,10 +280,10 @@
     fields = case_count * 3
 
     slot_ids = jnp.arange(size_x * size_y, dtype=jnp.int32)
-    matches = (load_nodes[0, 0][:, :, None] == slot_ids).astype(jnp.float32)
-    top_plane = jnp.einsum("cls,ckl->cks", matches, load_forces[0, 0], precision=highest).reshape(
-        fields, size_x, size_y
-    )
+    matches = load_nodes[0, 0][:, None, :, None] == slot_ids
+    top_plane = jnp.sum(
+        jnp.where(matches, load_forces[0, 0][:, :, :, None], 0.0), axis=2
+    ).reshape(fields, size_x, size_y)
     packed_loads = jnp.pad(top_plane.transpose(1, 2, 0), ((0, 0), (0, 0), (0, size_z - fields)))
     packed = jnp.concatenate(
         [start_disp.reshape(fields, size_x, size_y, size_z), modulus[None], packed_loads[None]],

time: 125 us -> 125 us (level)
    unnamed x31 -> x32, local copies, waits for them, and re-layouts: 5.35 us -> 6.05 us
where the time goes in v10:
time: 125 us; the launch traced here: 124 us
  blocking collectives  31.6 us (25%)
  starting transfers between devices  30.2 us (24%)
  other arithmetic  18.3 us (15%)
  local copies, waits for them, and re-layouts  15.6 us (12%)
  matrix products  15.1 us (12%)
  waiting for transfers between devices  9.78 us (8%)
  between operations  3.24 us (3%)
    all_to_all x2, blocking collectives, tree_sum(): value = jnp.sum(lax.all_to_all(copies, axis, 0, 0, tiled=False), axis=0)  31.6 us
    ppermute x2, starting transfers between devices, halo_both(): above = lax.ppermute(head, axis, [(i + 1, i) for i in range(count - 1)])  10.5 us
    dot_general x2, matrix products, node_forces(): jnp.einsum('ij,cjabd->ciabd', stiffness, local_disp, precision=highest)  9.98 us
    ppermute x2, starting transfers between devices, halo_both(): below = lax.ppermute(tail, axis, [(i, i + 1) for i in range(count - 1)])  8.64 us
    ppermute x2, starting transfers between devices, with_halo(): lax.ppermute(tail, axis, [(i, (i + 1) % count) for i in range(ends)])  6.15 us
    unnamed x32, local copies, waits for them, and re-layouts  6.05 us
    ppermute x2, waiting for transfers between devices, halo_both(): above = lax.ppermute(head, axis, [(i + 1, i) for i in range(count - 1)])  5.26 us
    ppermute x2, starting transfers between devices, with_halo(): lax.ppermute(head, axis, [((i + 1) % count, i) for i in range(ends)])  4.95 us
  transfers between devices with their start and end apart: 8, of which 5 were waited for; matrix products, arithmetic and copies ran while one was open for 3% of the time, Pallas kernels for 0%

profile of v10, /device:TPU:3, one launch (start us, length us, event | category | flops | bytes accessed | tf_op | source)
XLA Modules:
  0.0 123.9 jit_solution(6056888948741660754)
XLA Ops:
  0.7 0.7 copy.212
  1.4 0.7 copy.211
  2.5 0.8 multiply_multiply_fusion.1
  3.4 1.1 copy.143
  4.7 4.0 %collective-permute-start = (f32[20,2,8,128]{3,1,2,0:T(2,128)S(1)}, f32[20,2,8,128]{3,1,2,0:T(2,128)S(1)}, u32[]{:S(2)}, u32[]{:S(2)}) collective-permute-start(f32[20,2,8,128]{3,1,2,0:T(2,128)S(1)} %get-tuple-element.68), channel_id=1, source_target_pairs={{0,16},{16,32},{32,48},{48,64},{64,80},{80,96},{96,112},{112,128},... | collective-permute-start | bytes 491528 | tf_op jit(solution)/shard_map/ppermute | solution.py:246
  8.7 8.6 %collective-permute-start.1 = (f32[20,2,8,128]{3,1,2,0:T(2,128)S(1)}, f32[20,2,8,128]{3,1,2,0:T(2,128)S(1)}, u32[]{:S(2)}, u32[]{:S(2)}) collective-permute-start(f32[20,2,8,128]{3,1,2,0:T(2,128)S(1)} %get-tuple-element.69), channel_id=1, source_target_pairs={{16,0},{32,16},{48,32},{64,48},{80,64},{96,80},{112,96},{128,112},... | collective-permute-start | bytes 491528 | tf_op jit(solution)/shard_map/ppermute | solution.py:247
  17.3 0.7 and_convert_fusion.1
  17.9 0.7 and_convert_fusion
  18.6 0.7 collective-permute-done
  19.3 0.9 collective-permute-done.1
  20.2 4.6 %collective-permute-start.2 = (f32[20,8,2,128]{3,1,2,0:T(8,128)S(1)}, f32[20,8,2,128]{3,1,2,0:T(8,128)S(1)}, u32[]{:S(2)}, u32[]{:S(2)}) collective-permute-start(f32[20,8,2,128]{3,1,2,0:T(8,128)S(1)} %get-tuple-element.63), channel_id=1, source_target_pairs={{0,1},{1,2},{2,3},{3,4},{4,5},{5,6},{6,7},{7,8},{8,9},{9,10},{10,1... | collective-permute-start | bytes 491528 | tf_op jit(solution)/shard_map/ppermute | solution.py:246
  24.9 1.9 %collective-permute-start.3 = (f32[20,8,2,128]{3,1,2,0:T(8,128)S(1)}, f32[20,8,2,128]{3,1,2,0:T(8,128)S(1)}, u32[]{:S(2)}, u32[]{:S(2)}) collective-permute-start(f32[20,8,2,128]{3,1,2,0:T(8,128)S(1)} %get-tuple-element.64), channel_id=1, source_target_pairs={{1,0},{2,1},{3,2},{4,3},{5,4},{6,5},{7,6},{8,7},{9,8},{10,9},{11,1... | collective-permute-start | bytes 491528 | tf_op jit(solution)/shard_map/ppermute | solution.py:247
  27.1 4.4 %collective-permute-done.3 = f32[20,8,2,128]{3,1,2,0:T(8,128)S(1)} collective-permute-done((f32[20,8,2,128]{3,1,2,0:T(8,128)S(1)}, f32[20,8,2,128]{3,1,2,0:T(8,128)S(1)}, u32[]{:S(2)}, u32[]{:S(2)}) %collective-permute-start.3) | collective-permute-done | bytes 163872 | tf_op jit(solution)/shard_map/ppermute | solution.py:247
  32.1 0.5 copy.146
  32.6 1.0 copy.165
  35.1 1.1 copy.152
  36.2 7.0 %broadcast_multiply_fusion = (f32[6,24,7,11,128]{4,1,3,2,0:T(8,128)S(1)}, f32[6,24,7,11,128]{4,1,3,2,0:T(8,128)}) fusion(f32[7,11,128]{2,1,0:T(8,128)S(1)} %copy.153, f32[6,24,7,11,128]{4,1,3,2,0:T(8,128)S(1)} %copy.152, f32[24,24,1,1,1]{1,0,4,3,2:T(8,128)S(1)} %copy-done.3), kind=kOutput, calls=%fused_computation.7 | convolution fusion | flops 410167296 | bytes 17072896 | tf_op jit(solution)/shard_map/ij,cjabd->ciabd/dot_general | solution.py:259
  43.2 1.5 %copy.187 = f32[6,24,7,11,128]{4,0,3,2,1:T(8,128)S(1)} copy(f32[6,24,7,11,128]{4,1,3,2,0:T(8,128)S(1)} %get-tuple-element.78) | data formatting | bytes 11354112 | tf_op jit(solution)/shard_map/reshape | solution.py:260
  44.7 0.5 slice_bitcast_fusion.5
  45.2 0.9 fusion.23
  46.7 1.0 fusion.3
  48.8 0.6 copy.195
  49.4 2.5 %fusion.1 = (f32[6]{0:T(128)S(1)}, f32[6,24,4,8,128]{4,1,3,2,0:T(8,128)S(1)}, f32[6,24,4,8,128]{4,1,3,2,0:T(8,128)S(1)}) fusion(f32[6,24,7,11,128]{4,1,3,2,0:T(8,128)S(1)} %copy.152, f32[4,8,128]{2,1,0:T(8,128)S(1)} %get-tuple-element.70, f32[6,24,7,11,128]{4,1,3,2,0:T(8,128)} %get-tuple-element.79, f32[6,24,5,9,128]{4,1,3,2,0:T(8,128)S(1)} %copy.195), kind=kLoop, calls=%fused_computation.16 | loop fusion | flops 2359290 | bytes 11812888 | tf_op jit(solution)/shard_map/reduce_sum | solution.py:339
  52.7 3.0 %broadcast_multiply_fusion.1 = (f32[6,24,5,9,128]{4,1,3,2,0:T(8,128)S(1)}, f32[6,24,5,9,128]{4,1,3,2,0:T(8,128)S(1)}) fusion(f32[5,9,128]{2,1,0:T(8,128)S(1)} %copy.167, f32[6,24,5,9,128]{4,1,3,2,0:T(8,128)S(1)} %copy.195, f32[24,24,1,1,1]{1,0,4,3,2:T(8,128)S(1)} %copy-done.3), kind=kOutput, calls=%fused_computation.21 | convolution fusion | flops 239708160 | bytes 9978624 | tf_op jit(solution)/shard_map/ij,cjabd->ciabd/dot_general | solution.py:259
  55.7 0.9 copy.168
  57.6 2.9 %multiply_reduce_fusion = (f32[6,6]{1,0:T(8,128)S(1)}, f32[6,6]{1,0:T(8,128)S(1)}) fusion(f32[6,24,4,8,128]{4,3,2,1,0:T(8,128)S(1)} %copy.171, f32[6,24,4,8,128]{4,3,2,1,0:T(8,128)S(1)} %copy.169, f32[6,24,4,8,128]{4,3,2,1,0:T(8,128)S(1)} %copy.170), kind=kLoop, calls=%fused_computation | loop fusion | flops 14155704 | bytes 7078176 | tf_op jit(solution)/shard_map/reduce_sum | solution.py:344
  60.5 1.2 fusion.2
  62.1 16.1 %all_to_all.10 = f32[32,1,180]{2,1,0:T(1,128)S(1)} all-to-all(f32[32,1,180]{2,1,0:T(1,128)S(1)} %reshape.325), channel_id=1, replica_groups=mesh['gx'=32,'gy'=16] {'gx'}, dimensions={0} | all-to-all | bytes 46080 | tf_op jit(solution)/shard_map/all_to_all | solution.py:149
  78.2 0.5 broadcast.979
  78.7 0.7 reduce.7
  79.9 15.5 %all_to_all.11 = f32[16,1,180]{2,1,0:T(1,128)S(1)} all-to-all(f32[16,1,180]{2,1,0:T(1,128)S(1)} %reshape.327), channel_id=1, replica_groups=mesh['gx'=32,'gy'=16] {'gy'}, dimensions={0} | all-to-all | bytes 23040 | tf_op jit(solution)/shard_map/all_to_all | solution.py:149
  95.5 0.7 reduce.8
  96.4 0.6 slice_bitcast_fusion.24
  97.1 0.5 cholesky.15
  97.6 0.6 compare_reduce_fusion
  98.3 0.6 fusion.124
  98.9 0.5 custom-call.8
  99.6 0.8 fusion.126
  100.4 1.3 %convolution_add_fusion = f32[6,3,5,9,129]{4,0,3,2,1:T(8,128)S(1)} fusion(f32[6,3,6,10,128]{4,0,3,2,1:T(8,128)S(1)} %maximum_multiply_fusion, f32[6,3,8,12,128]{4,0,3,2,1:T(8,128)S(1)} %copy.146, f32[6,6]{1,0:T(8,128)S(1)} %get-tuple-element.83), kind=kOutput, calls=%fused_computation.24 | convolution fusion | flops 7627770 | bytes 1855800 | tf_op jit(solution)/shard_map/kabcd,kj->jabcd/dot_general | solution.py:154
  104.3 3.0 %collective-permute-start.5 = (f32[4,8,128]{2,1,0:T(8,128)S(1)}, f32[4,8,128]{2,1,0:T(8,128)S(1)}, u32[]{:S(2)}, u32[]{:S(2)}) collective-permute-start(f32[4,8,128]{2,1,0:T(8,128)S(1)} %add_multiply_fusion), channel_id=1, source_target_pairs={{16,0},{32,16},{48,32},{64,48},{80,64},{96,80},{112,96},{128,112},... | collective-permute-start | bytes 49160 | tf_op jit(solution)/shard_map/ppermute | solution.py:31
  107.4 2.3 %collective-permute-start.4 = (f32[4,8,128]{2,1,0:T(8,128)S(1)}, f32[4,8,128]{2,1,0:T(8,128)S(1)}, u32[]{:S(2)}, u32[]{:S(2)}) collective-permute-start(f32[4,8,128]{2,1,0:T(8,128)S(1)} %add_multiply_fusion), channel_id=1, source_target_pairs={{0,16},{16,32},{32,48},{48,64},{64,80},{80,96},{96,112},{112,128},... | collective-permute-start | bytes 49160 | tf_op jit(solution)/shard_map/ppermute | solution.py:29
  109.6 0.7 convolution_add_fusion.1
  110.3 3.6 %collective-permute-done.4 = f32[4,8,128]{2,1,0:T(8,128)S(1)} collective-permute-done((f32[4,8,128]{2,1,0:T(8,128)S(1)}, f32[4,8,128]{2,1,0:T(8,128)S(1)}, u32[]{:S(2)}, u32[]{:S(2)}) %collective-permute-start.4) | collective-permute-done | bytes 16416 | tf_op jit(solution)/shard_map/ppermute | solution.py:29
  114.0 3.9 %collective-permute-start.6 = (f32[4,4,128]{2,1,0:T(4,128)S(1)}, f32[4,4,128]{2,1,0:T(4,128)S(1)}, u32[]{:S(2)}, u32[]{:S(2)}) collective-permute-start(f32[4,4,128]{2,1,0:T(4,128)S(1)} %get-tuple-element.75), channel_id=1, source_target_pairs={{0,1},{1,2},{2,3},{3,4},{4,5},{5,6},{6,7},{7,8},{8,9},{9,10},{10,1... | collective-permute-start | bytes 24584 | tf_op jit(solution)/shard_map/ppermute | solution.py:29
  117.9 1.9 %collective-permute-start.7 = (f32[4,4,128]{2,1,0:T(4,128)S(1)}, f32[4,4,128]{2,1,0:T(4,128)S(1)}, u32[]{:S(2)}, u32[]{:S(2)}) collective-permute-start(f32[4,4,128]{2,1,0:T(4,128)S(1)} %get-tuple-element.76), channel_id=1, source_target_pairs={{1,0},{2,1},{3,2},{4,3},{5,4},{6,5},{7,6},{8,7},{9,8},{10,9},{11,1... | collective-permute-start | bytes 24584 | tf_op jit(solution)/shard_map/ppermute | solution.py:31
  119.8 0.7 multiply_reduce_fusion.3
  120.5 0.8 copy.180
  123.2 0.7 multiply_minimum_fusion
  (92 shorter events, 10.6 us)
Async XLA Ops:
  4.7 14.6 %collective-permute-start = (f32[20,2,8,128]{3,1,2,0:T(2,128)S(1)}, f32[20,2,8,128]{3,1,2,0:T(2,128)S(1)}, u32[]{:S(2)}, u32[]{:S(2)}) collective-permute-start(f32[20,2,8,128]{3,1,2,0:T(2,128)S(1)} %get-tuple-element.68), channel_id=1, source_target_pairs={{0,16},{16,32},{32,48},{48,64},{64,80},{80,96},{96,112},{112,128},... | collective-permute-start | bytes 491528 | tf_op jit(solution)/shard_map/ppermute | solution.py:246
  8.7 11.4 %collective-permute-start.1 = (f32[20,2,8,128]{3,1,2,0:T(2,128)S(1)}, f32[20,2,8,128]{3,1,2,0:T(2,128)S(1)}, u32[]{:S(2)}, u32[]{:S(2)}) collective-permute-start(f32[20,2,8,128]{3,1,2,0:T(2,128)S(1)} %get-tuple-element.69), channel_id=1, source_target_pairs={{16,0},{32,16},{48,32},{64,48},{80,64},{96,80},{112,96},{128,112},... | collective-permute-start | bytes 491528 | tf_op jit(solution)/shard_map/ppermute | solution.py:247
  20.2 6.9 %collective-permute-start.2 = (f32[20,8,2,128]{3,1,2,0:T(8,128)S(1)}, f32[20,8,2,128]{3,1,2,0:T(8,128)S(1)}, u32[]{:S(2)}, u32[]{:S(2)}) collective-permute-start(f32[20,8,2,128]{3,1,2,0:T(8,128)S(1)} %get-tuple-element.63), channel_id=1, source_target_pairs={{0,1},{1,2},{2,3},{3,4},{4,5},{5,6},{6,7},{7,8},{8,9},{9,10},{10,1... | collective-permute-start | bytes 491528 | tf_op jit(solution)/shard_map/ppermute | solution.py:246
  24.9 6.6 %collective-permute-start.3 = (f32[20,8,2,128]{3,1,2,0:T(8,128)S(1)}, f32[20,8,2,128]{3,1,2,0:T(8,128)S(1)}, u32[]{:S(2)}, u32[]{:S(2)}) collective-permute-start(f32[20,8,2,128]{3,1,2,0:T(8,128)S(1)} %get-tuple-element.64), channel_id=1, source_target_pairs={{1,0},{2,1},{3,2},{4,3},{5,4},{6,5},{7,6},{8,7},{9,8},{10,9},{11,1... | collective-permute-start | bytes 491528 | tf_op jit(solution)/shard_map/ppermute | solution.py:247
  35.1 1.1 copy-start.3
  103.1 1.1 copy-start.1
  103.2 1.1 copy-start.2
  103.2 6.5 %copy-start = (f32[6,3,4,8,128]{4,3,2,1,0:T(8,128)S(1)}, f32[6,3,4,8,128]{4,3,2,1,0:T(8,128)}, u32[]{:S(2)}) copy-start(f32[6,3,4,8,128]{4,3,2,1,0:T(8,128)} %param.8) | copy-start | bytes 884740
  104.3 6.0 %collective-permute-start.5 = (f32[4,8,128]{2,1,0:T(8,128)S(1)}, f32[4,8,128]{2,1,0:T(8,128)S(1)}, u32[]{:S(2)}, u32[]{:S(2)}) collective-permute-start(f32[4,8,128]{2,1,0:T(8,128)S(1)} %add_multiply_fusion), channel_id=1, source_target_pairs={{16,0},{32,16},{48,32},{64,48},{80,64},{96,80},{112,96},{128,112},... | collective-permute-start | bytes 49160 | tf_op jit(solution)/shard_map/ppermute | solution.py:31
  107.4 6.6 %collective-permute-start.4 = (f32[4,8,128]{2,1,0:T(8,128)S(1)}, f32[4,8,128]{2,1,0:T(8,128)S(1)}, u32[]{:S(2)}, u32[]{:S(2)}) collective-permute-start(f32[4,8,128]{2,1,0:T(8,128)S(1)} %add_multiply_fusion), channel_id=1, source_target_pairs={{0,16},{16,32},{32,48},{48,64},{64,80},{80,96},{96,112},{112,128},... | collective-permute-start | bytes 49160 | tf_op jit(solution)/shard_map/ppermute | solution.py:29
  114.0 9.2 %collective-permute-start.6 = (f32[4,4,128]{2,1,0:T(4,128)S(1)}, f32[4,4,128]{2,1,0:T(4,128)S(1)}, u32[]{:S(2)}, u32[]{:S(2)}) collective-permute-start(f32[4,4,128]{2,1,0:T(4,128)S(1)} %get-tuple-element.75), channel_id=1, source_target_pairs={{0,1},{1,2},{2,3},{3,4},{4,5},{5,6},{6,7},{7,8},{8,9},{9,10},{10,1... | collective-permute-start | bytes 24584 | tf_op jit(solution)/shard_map/ppermute | solution.py:29
  117.9 5.3 %collective-permute-start.7 = (f32[4,4,128]{2,1,0:T(4,128)S(1)}, f32[4,4,128]{2,1,0:T(4,128)S(1)}, u32[]{:S(2)}, u32[]{:S(2)}) collective-permute-start(f32[4,4,128]{2,1,0:T(4,128)S(1)} %get-tuple-element.76), channel_id=1, source_target_pairs={{1,0},{2,1},{3,2},{4,3},{5,4},{6,5},{7,6},{8,7},{9,8},{10,9},{11,1... | collective-permute-start | bytes 24584 | tf_op jit(solution)/shard_map/ppermute | solution.py:31

commit v11 on v9

--- a/solution.py
+++ b/solution.py
@@ -151,7 +151,7 @@
 
 
 def mix_cases(field, coeffs):
-    return jnp.einsum("kabcd,kj->jabcd", field, coeffs, precision=highest)
+    return jnp.sum(field[:, None] * coeffs[:, :, None, None, None, None], axis=0)
 
 
 def solve_spd(matrix, rhs_matrix):

time: 125 us -> 125 us (level)
  blocking collectives: 31.6 us -> 16.1 us
  starting transfers between devices: 30.2 us -> 38.6 us
  waiting for transfers between devices: 9.78 us -> 17.1 us
  other arithmetic: 18.1 us -> 20.1 us
  matrix products: 16 us -> 14.1 us
    all_to_all x2 -> x1, blocking collectives: 31.6 us -> 16.1 us  [tree_sum(): value = jnp.sum(lax.all_to_all(copies, axis, 0, 0, tiled=False), axis=0)]
    all_to_all x0 -> x1, starting transfers between devices: none -> 8.41 us  [tree_sum(): value = jnp.sum(lax.all_to_all(copies, axis, 0, 0, tiled=False), axis=0)]
    all_to_all x0 -> x1, waiting for transfers between devices: none -> 6.81 us  [tree_sum(): value = jnp.sum(lax.all_to_all(copies, axis, 0, 0, tiled=False), axis=0)]
    dot_general x2 -> x0, matrix products: 1.94 us -> none  [mix_cases(): return jnp.einsum('kabcd,kj->jabcd', field, coeffs, precision=highest)]
    unnamed x31 -> x30, local copies, waits for them, and re-layouts: 5.35 us -> 5.19 us
  transfers between devices with their start and end apart: 8 -> 9, of which waited for: 5 -> 6; matrix products, arithmetic and copies ran while one was open for 3% -> 3% of each run, Pallas kernels for 0% -> 0%
where the time goes in v11:
time: 125 us; the launch traced here: 124 us
  starting transfers between devices  38.6 us (31%)
  other arithmetic  20.1 us (16%)
  waiting for transfers between devices  17.1 us (14%)
  blocking collectives  16.1 us (13%)
  local copies, waits for them, and re-layouts  15.3 us (12%)
  matrix products  14.1 us (11%)
  between operations  3.26 us (3%)
    all_to_all x1, blocking collectives, tree_sum(): value = jnp.sum(lax.all_to_all(copies, axis, 0, 0, tiled=False), axis=0)  16.1 us
    ppermute x2, starting transfers between devices, halo_both(): above = lax.ppermute(head, axis, [(i + 1, i) for i in range(count - 1)])  10.5 us
    dot_general x2, matrix products, node_forces(): jnp.einsum('ij,cjabd->ciabd', stiffness, local_disp, precision=highest)  9.98 us
    ppermute x2, starting transfers between devices, halo_both(): below = lax.ppermute(tail, axis, [(i, i + 1) for i in range(count - 1)])  8.64 us
    all_to_all x1, starting transfers between devices, tree_sum(): value = jnp.sum(lax.all_to_all(copies, axis, 0, 0, tiled=False), axis=0)  8.41 us
    all_to_all x1, waiting for transfers between devices, tree_sum(): value = jnp.sum(lax.all_to_all(copies, axis, 0, 0, tiled=False), axis=0)  6.81 us
    ppermute x2, starting transfers between devices, with_halo(): lax.ppermute(tail, axis, [(i, (i + 1) % count) for i in range(ends)])  6.15 us
    ppermute x2, waiting for transfers between devices, halo_both(): above = lax.ppermute(head, axis, [(i + 1, i) for i in range(count - 1)])  5.26 us
  transfers between devices with their start and end apart: 9, of which 6 were waited for; matrix products, arithmetic and copies ran while one was open for 3% of the time, Pallas kernels for 0%

profile of v11, /device:TPU:3, one launch (start us, length us, event | category | flops | bytes accessed | tf_op | source)
XLA Modules:
  0.0 124.5 jit_solution(17041047055992255454)
XLA Ops:
  0.7 0.7 copy.166
  1.4 0.9 convolution_bitcast_fusion.2
  2.4 0.8 multiply_multiply_fusion.1
  3.4 1.1 copy.102
  4.7 4.0 %collective-permute-start = (f32[20,2,8,128]{3,1,2,0:T(2,128)S(1)}, f32[20,2,8,128]{3,1,2,0:T(2,128)S(1)}, u32[]{:S(2)}, u32[]{:S(2)}) collective-permute-start(f32[20,2,8,128]{3,1,2,0:T(2,128)S(1)} %get-tuple-element.62), channel_id=1, source_target_pairs={{0,16},{16,32},{32,48},{48,64},{64,80},{80,96},{96,112},{112,128},... | collective-permute-start | bytes 491528 | tf_op jit(solution)/shard_map/ppermute | solution.py:246
  8.7 8.6 %collective-permute-start.1 = (f32[20,2,8,128]{3,1,2,0:T(2,128)S(1)}, f32[20,2,8,128]{3,1,2,0:T(2,128)S(1)}, u32[]{:S(2)}, u32[]{:S(2)}) collective-permute-start(f32[20,2,8,128]{3,1,2,0:T(2,128)S(1)} %get-tuple-element.63), channel_id=1, source_target_pairs={{16,0},{32,16},{48,32},{64,48},{80,64},{96,80},{112,96},{128,112},... | collective-permute-start | bytes 491528 | tf_op jit(solution)/shard_map/ppermute | solution.py:247
  17.2 0.7 and_convert_fusion.1
  17.9 0.7 and_convert_fusion
  18.6 0.7 collective-permute-done
  19.2 0.9 collective-permute-done.1
  20.2 4.6 %collective-permute-start.2 = (f32[20,8,2,128]{3,1,2,0:T(8,128)S(1)}, f32[20,8,2,128]{3,1,2,0:T(8,128)S(1)}, u32[]{:S(2)}, u32[]{:S(2)}) collective-permute-start(f32[20,8,2,128]{3,1,2,0:T(8,128)S(1)} %get-tuple-element.57), channel_id=1, source_target_pairs={{0,1},{1,2},{2,3},{3,4},{4,5},{5,6},{6,7},{7,8},{8,9},{9,10},{10,1... | collective-permute-start | bytes 491528 | tf_op jit(solution)/shard_map/ppermute | solution.py:246
  24.8 1.9 %collective-permute-start.3 = (f32[20,8,2,128]{3,1,2,0:T(8,128)S(1)}, f32[20,8,2,128]{3,1,2,0:T(8,128)S(1)}, u32[]{:S(2)}, u32[]{:S(2)}) collective-permute-start(f32[20,8,2,128]{3,1,2,0:T(8,128)S(1)} %get-tuple-element.58), channel_id=1, source_target_pairs={{1,0},{2,1},{3,2},{4,3},{5,4},{6,5},{7,6},{8,7},{9,8},{10,9},{11,1... | collective-permute-start | bytes 491528 | tf_op jit(solution)/shard_map/ppermute | solution.py:247
  27.1 4.4 %collective-permute-done.3 = f32[20,8,2,128]{3,1,2,0:T(8,128)S(1)} collective-permute-done((f32[20,8,2,128]{3,1,2,0:T(8,128)S(1)}, f32[20,8,2,128]{3,1,2,0:T(8,128)S(1)}, u32[]{:S(2)}, u32[]{:S(2)}) %collective-permute-start.3) | collective-permute-done | bytes 163872 | tf_op jit(solution)/shard_map/ppermute | solution.py:247
  32.0 0.5 copy.105
  32.5 1.0 copy.124
  35.1 1.1 copy.111
  36.2 7.0 %broadcast_multiply_fusion = (f32[6,24,7,11,128]{4,1,3,2,0:T(8,128)S(1)}, f32[6,24,7,11,128]{4,1,3,2,0:T(8,128)}) fusion(f32[7,11,128]{2,1,0:T(8,128)S(1)} %copy.112, f32[6,24,7,11,128]{4,1,3,2,0:T(8,128)S(1)} %copy.111, f32[24,24,1,1,1]{1,0,4,3,2:T(8,128)S(1)} %copy-done.3), kind=kOutput, calls=%fused_computation.8 | convolution fusion | flops 410167296 | bytes 17072896 | tf_op jit(solution)/shard_map/ij,cjabd->ciabd/dot_general | solution.py:259
  43.2 1.5 %copy.142 = f32[6,24,7,11,128]{4,0,3,2,1:T(8,128)S(1)} copy(f32[6,24,7,11,128]{4,1,3,2,0:T(8,128)S(1)} %get-tuple-element.72) | data formatting | bytes 11354112 | tf_op jit(solution)/shard_map/reshape | solution.py:260
  44.6 0.5 slice_bitcast_fusion.5
  45.1 0.9 fusion.24
  46.7 1.0 fusion.3
  48.7 0.6 copy.150
  49.4 2.5 %fusion.1 = (f32[6]{0:T(128)S(1)}, f32[6,24,4,8,128]{4,1,3,2,0:T(8,128)S(1)}, f32[6,24,4,8,128]{4,1,3,2,0:T(8,128)S(1)}) fusion(f32[6,24,7,11,128]{4,1,3,2,0:T(8,128)S(1)} %copy.111, f32[4,8,128]{2,1,0:T(8,128)S(1)} %get-tuple-element.64, f32[6,24,7,11,128]{4,1,3,2,0:T(8,128)} %get-tuple-element.73, f32[6,24,5,9,128]{4,1,3,2,0:T(8,128)S(1)} %copy.150), kind=kLoop, calls=%fused_computation.17 | loop fusion | flops 2359290 | bytes 11812888 | tf_op jit(solution)/shard_map/reduce_sum | solution.py:339
  52.7 3.0 %broadcast_multiply_fusion.1 = (f32[6,24,5,9,128]{4,1,3,2,0:T(8,128)S(1)}, f32[6,24,5,9,128]{4,1,3,2,0:T(8,128)S(1)}) fusion(f32[5,9,128]{2,1,0:T(8,128)S(1)} %copy.127, f32[6,24,5,9,128]{4,1,3,2,0:T(8,128)S(1)} %copy.150, f32[24,24,1,1,1]{1,0,4,3,2:T(8,128)S(1)} %copy-done.3), kind=kOutput, calls=%fused_computation.23 | convolution fusion | flops 239708160 | bytes 9978624 | tf_op jit(solution)/shard_map/ij,cjabd->ciabd/dot_general | solution.py:259
  55.7 0.9 copy.128
  57.5 2.9 %multiply_reduce_fusion = (f32[6,6]{1,0:T(8,128)S(1)}, f32[6,6]{1,0:T(8,128)S(1)}) fusion(f32[6,24,4,8,128]{4,3,2,1,0:T(8,128)S(1)} %copy.131, f32[6,24,4,8,128]{4,3,2,1,0:T(8,128)S(1)} %copy.129, f32[6,24,4,8,128]{4,3,2,1,0:T(8,128)S(1)} %copy.130), kind=kLoop, calls=%fused_computation | loop fusion | flops 14155704 | bytes 7078176 | tf_op jit(solution)/shard_map/reduce_sum | solution.py:344
  60.4 1.2 fusion.2
  62.1 16.1 %all_to_all.10 = f32[32,1,180]{2,1,0:T(1,128)S(1)} all-to-all(f32[32,1,180]{2,1,0:T(1,128)S(1)} %reshape.318), channel_id=1, replica_groups=mesh['gx'=32,'gy'=16] {'gx'}, dimensions={0} | all-to-all | bytes 46080 | tf_op jit(solution)/shard_map/all_to_all | solution.py:149
  78.2 0.5 broadcast.977
  78.7 0.7 reduce.7
  79.7 0.8 reshape.320
  80.5 8.4 %all-to-all-start.1 = ((f32[16,1,180]{2,1,0:T(1,128)}), f32[16,1,180]{2,1,0:T(1,128)S(1)}, u32[]{:S(2)}, u32[]{:S(2)}) async-start(f32[16,1,180]{2,1,0:T(1,128)} %reshape.320), calls=%async_computation.1 | async-start | bytes 32768 | tf_op jit(solution)/shard_map/all_to_all | solution.py:149
  89.4 6.8 %all-to-all-done.1 = f32[16,1,180]{2,1,0:T(1,128)S(1)} async-done(((f32[16,1,180]{2,1,0:T(1,128)}), f32[16,1,180]{2,1,0:T(1,128)S(1)}, u32[]{:S(2)}, u32[]{:S(2)}) %all-to-all-start.1) | async-done | bytes 11552 | tf_op jit(solution)/shard_map/all_to_all | solution.py:149
  96.3 0.7 reduce.8
  97.1 0.6 slice_bitcast_fusion.24
  97.8 0.5 cholesky.15
  98.4 0.6 compare_reduce_fusion
  99.1 0.6 fusion.125
  100.4 0.8 fusion.127
  101.2 0.9 multiply_reduce_fusion.2
  104.9 3.0 %collective-permute-start.5 = (f32[4,8,128]{2,1,0:T(8,128)S(1)}, f32[4,8,128]{2,1,0:T(8,128)S(1)}, u32[]{:S(2)}, u32[]{:S(2)}) collective-permute-start(f32[4,8,128]{2,1,0:T(8,128)S(1)} %add_multiply_fusion), channel_id=1, source_target_pairs={{16,0},{32,16},{48,32},{64,48},{80,64},{96,80},{112,96},{128,112},... | collective-permute-start | bytes 49160 | tf_op jit(solution)/shard_map/ppermute | solution.py:31
  107.9 2.3 %collective-permute-start.4 = (f32[4,8,128]{2,1,0:T(8,128)S(1)}, f32[4,8,128]{2,1,0:T(8,128)S(1)}, u32[]{:S(2)}, u32[]{:S(2)}) collective-permute-start(f32[4,8,128]{2,1,0:T(8,128)S(1)} %add_multiply_fusion), channel_id=1, source_target_pairs={{0,16},{16,32},{32,48},{48,64},{64,80},{80,96},{96,112},{112,128},... | collective-permute-start | bytes 49160 | tf_op jit(solution)/shard_map/ppermute | solution.py:29
  110.4 4.1 %collective-permute-done.4 = f32[4,8,128]{2,1,0:T(8,128)S(1)} collective-permute-done((f32[4,8,128]{2,1,0:T(8,128)S(1)}, f32[4,8,128]{2,1,0:T(8,128)S(1)}, u32[]{:S(2)}, u32[]{:S(2)}) %collective-permute-start.4) | collective-permute-done | bytes 16416 | tf_op jit(solution)/shard_map/ppermute | solution.py:29
  114.5 3.9 %collective-permute-start.6 = (f32[4,4,128]{2,1,0:T(4,128)S(1)}, f32[4,4,128]{2,1,0:T(4,128)S(1)}, u32[]{:S(2)}, u32[]{:S(2)}) collective-permute-start(f32[4,4,128]{2,1,0:T(4,128)S(1)} %get-tuple-element.69), channel_id=1, source_target_pairs={{0,1},{1,2},{2,3},{3,4},{4,5},{5,6},{6,7},{7,8},{8,9},{9,10},{10,1... | collective-permute-start | bytes 24584 | tf_op jit(solution)/shard_map/ppermute | solution.py:29
  118.4 1.9 %collective-permute-start.7 = (f32[4,4,128]{2,1,0:T(4,128)S(1)}, f32[4,4,128]{2,1,0:T(4,128)S(1)}, u32[]{:S(2)}, u32[]{:S(2)}) collective-permute-start(f32[4,4,128]{2,1,0:T(4,128)S(1)} %get-tuple-element.70), channel_id=1, source_target_pairs={{1,0},{2,1},{3,2},{4,3},{5,4},{6,5},{7,6},{8,7},{9,8},{10,9},{11,1... | collective-permute-start | bytes 24584 | tf_op jit(solution)/shard_map/ppermute | solution.py:31
  120.4 0.7 multiply_reduce_fusion.5
  121.0 0.8 add.785
  123.8 0.7 multiply_minimum_fusion
  (96 shorter events, 11.4 us)
Async XLA Ops:
  4.7 14.6 %collective-permute-start = (f32[20,2,8,128]{3,1,2,0:T(2,128)S(1)}, f32[20,2,8,128]{3,1,2,0:T(2,128)S(1)}, u32[]{:S(2)}, u32[]{:S(2)}) collective-permute-start(f32[20,2,8,128]{3,1,2,0:T(2,128)S(1)} %get-tuple-element.62), channel_id=1, source_target_pairs={{0,16},{16,32},{32,48},{48,64},{64,80},{80,96},{96,112},{112,128},... | collective-permute-start | bytes 491528 | tf_op jit(solution)/shard_map/ppermute | solution.py:246
  8.7 11.4 %collective-permute-start.1 = (f32[20,2,8,128]{3,1,2,0:T(2,128)S(1)}, f32[20,2,8,128]{3,1,2,0:T(2,128)S(1)}, u32[]{:S(2)}, u32[]{:S(2)}) collective-permute-start(f32[20,2,8,128]{3,1,2,0:T(2,128)S(1)} %get-tuple-element.63), channel_id=1, source_target_pairs={{16,0},{32,16},{48,32},{64,48},{80,64},{96,80},{112,96},{128,112},... | collective-permute-start | bytes 491528 | tf_op jit(solution)/shard_map/ppermute | solution.py:247
  20.2 6.9 %collective-permute-start.2 = (f32[20,8,2,128]{3,1,2,0:T(8,128)S(1)}, f32[20,8,2,128]{3,1,2,0:T(8,128)S(1)}, u32[]{:S(2)}, u32[]{:S(2)}) collective-permute-start(f32[20,8,2,128]{3,1,2,0:T(8,128)S(1)} %get-tuple-element.57), channel_id=1, source_target_pairs={{0,1},{1,2},{2,3},{3,4},{4,5},{5,6},{6,7},{7,8},{8,9},{9,10},{10,1... | collective-permute-start | bytes 491528 | tf_op jit(solution)/shard_map/ppermute | solution.py:246
  24.8 6.6 %collective-permute-start.3 = (f32[20,8,2,128]{3,1,2,0:T(8,128)S(1)}, f32[20,8,2,128]{3,1,2,0:T(8,128)S(1)}, u32[]{:S(2)}, u32[]{:S(2)}) collective-permute-start(f32[20,8,2,128]{3,1,2,0:T(8,128)S(1)} %get-tuple-element.58), channel_id=1, source_target_pairs={{1,0},{2,1},{3,2},{4,3},{5,4},{6,5},{7,6},{8,7},{9,8},{10,9},{11,1... | collective-permute-start | bytes 491528 | tf_op jit(solution)/shard_map/ppermute | solution.py:247
  35.1 1.1 copy-start.3
  80.5 15.7 %all-to-all-start.1 = ((f32[16,1,180]{2,1,0:T(1,128)}), f32[16,1,180]{2,1,0:T(1,128)S(1)}, u32[]{:S(2)}, u32[]{:S(2)}) async-start(f32[16,1,180]{2,1,0:T(1,128)} %reshape.320), calls=%async_computation.1 | async-start | bytes 32768 | tf_op jit(solution)/shard_map/all_to_all | solution.py:149
  103.7 1.1 copy-start.1
  103.7 1.1 copy-start.2
  103.9 17.1 %copy-start = (f32[6,3,4,8,128]{4,3,2,1,0:T(8,128)S(1)}, f32[6,3,4,8,128]{4,3,2,1,0:T(8,128)}, u32[]{:S(2)}) copy-start(f32[6,3,4,8,128]{4,3,2,1,0:T(8,128)} %param.8) | copy-start | bytes 884740
  104.9 5.5 %collective-permute-start.5 = (f32[4,8,128]{2,1,0:T(8,128)S(1)}, f32[4,8,128]{2,1,0:T(8,128)S(1)}, u32[]{:S(2)}, u32[]{:S(2)}) collective-permute-start(f32[4,8,128]{2,1,0:T(8,128)S(1)} %add_multiply_fusion), channel_id=1, source_target_pairs={{16,0},{32,16},{48,32},{64,48},{80,64},{96,80},{112,96},{128,112},... | collective-permute-start | bytes 49160 | tf_op jit(solution)/shard_map/ppermute | solution.py:31
  107.9 6.6 %collective-permute-start.4 = (f32[4,8,128]{2,1,0:T(8,128)S(1)}, f32[4,8,128]{2,1,0:T(8,128)S(1)}, u32[]{:S(2)}, u32[]{:S(2)}) collective-permute-start(f32[4,8,128]{2,1,0:T(8,128)S(1)} %add_multiply_fusion), channel_id=1, source_target_pairs={{0,16},{16,32},{32,48},{48,64},{64,80},{80,96},{96,112},{112,128},... | collective-permute-start | bytes 49160 | tf_op jit(solution)/shard_map/ppermute | solution.py:29
  114.5 9.2 %collective-permute-start.6 = (f32[4,4,128]{2,1,0:T(4,128)S(1)}, f32[4,4,128]{2,1,0:T(4,128)S(1)}, u32[]{:S(2)}, u32[]{:S(2)}) collective-permute-start(f32[4,4,128]{2,1,0:T(4,128)S(1)} %get-tuple-element.69), channel_id=1, source_target_pairs={{0,1},{1,2},{2,3},{3,4},{4,5},{5,6},{6,7},{7,8},{8,9},{9,10},{10,1... | collective-permute-start | bytes 24584 | tf_op jit(solution)/shard_map/ppermute | solution.py:29
  118.4 5.3 %collective-permute-start.7 = (f32[4,4,128]{2,1,0:T(4,128)S(1)}, f32[4,4,128]{2,1,0:T(4,128)S(1)}, u32[]{:S(2)}, u32[]{:S(2)}) collective-permute-start(f32[4,4,128]{2,1,0:T(4,128)S(1)} %get-tuple-element.70), channel_id=1, source_target_pairs={{1,0},{2,1},{3,2},{4,3},{5,4},{6,5},{7,6},{8,7},{9,8},{10,9},{11,1... | collective-permute-start | bytes 24584 | tf_op jit(solution)/shard_map/ppermute | solution.py:31

commit v12 on v9

--- a/solution.py
+++ b/solution.py
@@ -139,7 +139,7 @@
 
 
 def local_gram(left_field, right_field):
-    return jnp.einsum("iabcd,jabcd->ij", left_field, right_field, precision=highest)
+    return jnp.sum(left_field[:, None] * right_field[None, :], axis=(2, 3, 4, 5))
 
 
 def tree_sum(value):

time: 125 us -> 123 us (0.984)
  matrix products: 16 us -> 13.8 us
    dot_general x2 -> x0, matrix products: 2.16 us -> none  [local_gram(): jnp.einsum('iabcd,jabcd->ij', left_field, right_field, precision=highest)]
    unnamed x31 -> x33, local copies, waits for them, and re-layouts: 5.35 us -> 5.35 us
where the time goes in v12:
time: 123 us
  blocking collectives  31.6 us (26%)
  starting transfers between devices  30.2 us (25%)
  other arithmetic  18.8 us (15%)
  local copies, waits for them, and re-layouts  15.3 us (12%)
  matrix products  13.8 us (11%)
  waiting for transfers between devices  9.78 us (8%)
  between operations  3.26 us (3%)
    all_to_all x2, blocking collectives, tree_sum(): value = jnp.sum(lax.all_to_all(copies, axis, 0, 0, tiled=False), axis=0)  31.6 us
    ppermute x2, starting transfers between devices, halo_both(): above = lax.ppermute(head, axis, [(i + 1, i) for i in range(count - 1)])  10.5 us
    dot_general x2, matrix products, node_forces(): jnp.einsum('ij,cjabd->ciabd', stiffness, local_disp, precision=highest)  9.95 us
    ppermute x2, starting transfers between devices, halo_both(): below = lax.ppermute(tail, axis, [(i, i + 1) for i in range(count - 1)])  8.64 us
    ppermute x2, starting transfers between devices, with_halo(): lax.ppermute(tail, axis, [(i, (i + 1) % count) for i in range(ends)])  6.15 us
    unnamed x33, local copies, waits for them, and re-layouts  5.35 us
    ppermute x2, waiting for transfers between devices, halo_both(): above = lax.ppermute(head, axis, [(i + 1, i) for i in range(count - 1)])  5.26 us
    ppermute x2, starting transfers between devices, with_halo(): lax.ppermute(head, axis, [((i + 1) % count, i) for i in range(ends)])  4.95 us
  transfers between devices with their start and end apart: 8, of which 5 were waited for; matrix products, arithmetic and copies ran while one was open for 3% of the time, Pallas kernels for 0%

profile of v12, /device:TPU:3, one launch (start us, length us, event | category | flops | bytes accessed | tf_op | source)
XLA Modules:
  0.0 122.8 jit_solution(7199305677588041329)
XLA Ops:
  0.7 0.7 copy.264
  1.4 0.9 convolution_bitcast_fusion.2
  2.4 0.8 multiply_multiply_fusion.1
  3.4 1.1 copy.184
  4.7 4.0 %collective-permute-start = (f32[20,2,8,128]{3,1,2,0:T(2,128)S(1)}, f32[20,2,8,128]{3,1,2,0:T(2,128)S(1)}, u32[]{:S(2)}, u32[]{:S(2)}) collective-permute-start(f32[20,2,8,128]{3,1,2,0:T(2,128)S(1)} %get-tuple-element.72), channel_id=1, source_target_pairs={{0,16},{16,32},{32,48},{48,64},{64,80},{80,96},{96,112},{112,128},... | collective-permute-start | bytes 491528 | tf_op jit(solution)/shard_map/ppermute | solution.py:246
  8.7 8.6 %collective-permute-start.1 = (f32[20,2,8,128]{3,1,2,0:T(2,128)S(1)}, f32[20,2,8,128]{3,1,2,0:T(2,128)S(1)}, u32[]{:S(2)}, u32[]{:S(2)}) collective-permute-start(f32[20,2,8,128]{3,1,2,0:T(2,128)S(1)} %get-tuple-element.73), channel_id=1, source_target_pairs={{16,0},{32,16},{48,32},{64,48},{80,64},{96,80},{112,96},{128,112},... | collective-permute-start | bytes 491528 | tf_op jit(solution)/shard_map/ppermute | solution.py:247
  17.2 0.7 and_convert_fusion.1
  17.9 0.7 and_convert_fusion
  18.6 0.7 collective-permute-done
  19.2 0.9 collective-permute-done.1
  20.2 4.6 %collective-permute-start.2 = (f32[20,8,2,128]{3,1,2,0:T(8,128)S(1)}, f32[20,8,2,128]{3,1,2,0:T(8,128)S(1)}, u32[]{:S(2)}, u32[]{:S(2)}) collective-permute-start(f32[20,8,2,128]{3,1,2,0:T(8,128)S(1)} %get-tuple-element.67), channel_id=1, source_target_pairs={{0,1},{1,2},{2,3},{3,4},{4,5},{5,6},{6,7},{7,8},{8,9},{9,10},{10,1... | collective-permute-start | bytes 491528 | tf_op jit(solution)/shard_map/ppermute | solution.py:246
  24.8 1.9 %collective-permute-start.3 = (f32[20,8,2,128]{3,1,2,0:T(8,128)S(1)}, f32[20,8,2,128]{3,1,2,0:T(8,128)S(1)}, u32[]{:S(2)}, u32[]{:S(2)}) collective-permute-start(f32[20,8,2,128]{3,1,2,0:T(8,128)S(1)} %get-tuple-element.68), channel_id=1, source_target_pairs={{1,0},{2,1},{3,2},{4,3},{5,4},{6,5},{7,6},{8,7},{9,8},{10,9},{11,1... | collective-permute-start | bytes 491528 | tf_op jit(solution)/shard_map/ppermute | solution.py:247
  27.1 4.4 %collective-permute-done.3 = f32[20,8,2,128]{3,1,2,0:T(8,128)S(1)} collective-permute-done((f32[20,8,2,128]{3,1,2,0:T(8,128)S(1)}, f32[20,8,2,128]{3,1,2,0:T(8,128)S(1)}, u32[]{:S(2)}, u32[]{:S(2)}) %collective-permute-start.3) | collective-permute-done | bytes 163872 | tf_op jit(solution)/shard_map/ppermute | solution.py:247
  32.0 0.5 copy.187
  32.6 1.0 copy.206
  35.1 1.1 copy.193
  36.2 7.0 %broadcast_multiply_fusion = (f32[6,24,7,11,128]{4,1,3,2,0:T(8,128)S(1)}, f32[6,24,7,11,128]{4,1,3,2,0:T(8,128)}) fusion(f32[7,11,128]{2,1,0:T(8,128)S(1)} %copy.194, f32[6,24,7,11,128]{4,1,3,2,0:T(8,128)S(1)} %copy.193, f32[24,24,1,1,1]{1,0,4,3,2:T(8,128)S(1)} %copy-done.3), kind=kOutput, calls=%fused_computation.7 | convolution fusion | flops 410167296 | bytes 17072896 | tf_op jit(solution)/shard_map/ij,cjabd->ciabd/dot_general | solution.py:259
  43.2 1.5 %copy.236 = f32[6,24,7,11,128]{4,0,3,2,1:T(8,128)S(1)} copy(f32[6,24,7,11,128]{4,1,3,2,0:T(8,128)S(1)} %get-tuple-element.82) | data formatting | bytes 11354112 | tf_op jit(solution)/shard_map/reshape | solution.py:260
  44.7 0.5 slice_bitcast_fusion.5
  45.2 0.9 fusion.21
  47.7 0.6 copy.244
  48.4 2.5 %fusion.1 = (f32[6]{0:T(128)S(1)}, f32[6,24,4,8,128]{4,1,3,2,0:T(8,128)S(1)}, f32[6,24,4,8,128]{4,1,3,2,0:T(8,128)S(1)}) fusion(f32[6,24,7,11,128]{4,1,3,2,0:T(8,128)S(1)} %copy.193, f32[4,8,128]{2,1,0:T(8,128)S(1)} %get-tuple-element.74, f32[6,24,7,11,128]{4,1,3,2,0:T(8,128)} %get-tuple-element.83, f32[6,24,5,9,128]{4,1,3,2,0:T(8,128)S(1)} %copy.244), kind=kLoop, calls=%fused_computation.16 | loop fusion | flops 2359290 | bytes 11812888 | tf_op jit(solution)/shard_map/reduce_sum | solution.py:339
  51.7 3.0 %broadcast_multiply_fusion.1 = (f32[6,24,5,9,128]{4,1,3,2,0:T(8,128)S(1)}, f32[6,24,5,9,128]{4,1,3,2,0:T(8,128)S(1)}) fusion(f32[5,9,128]{2,1,0:T(8,128)S(1)} %copy.210, f32[6,24,5,9,128]{4,1,3,2,0:T(8,128)S(1)} %copy.244, f32[24,24,1,1,1]{1,0,4,3,2:T(8,128)S(1)} %copy-done.3), kind=kOutput, calls=%fused_computation.23 | convolution fusion | flops 239708160 | bytes 9978624 | tf_op jit(solution)/shard_map/ij,cjabd->ciabd/dot_general | solution.py:259
  54.7 0.9 copy.248
  55.8 0.5 fusion.151
  57.1 0.6 copy.222
  57.8 2.7 %multiply_reduce_fusion = (f32[6,6]{1,0:T(8,128)S(1)}, f32[6,6]{1,0:T(8,128)S(1)}) fusion(f32[6,24,4,8,128]{4,3,2,1,0:T(8,128)S(1)} %copy.222, f32[6,24,4,8,128]{4,3,2,1,0:T(8,128)S(1)} %copy.220, f32[6,24,4,8,128]{4,3,2,1,0:T(8,128)S(1)} %copy.221), kind=kLoop, calls=%fused_computation | loop fusion | flops 14155704 | bytes 7078176 | tf_op jit(solution)/shard_map/reduce_sum | solution.py:344
  60.9 16.1 %all_to_all.10 = f32[32,1,180]{2,1,0:T(1,128)S(1)} all-to-all(f32[32,1,180]{2,1,0:T(1,128)S(1)} %reshape.318), channel_id=1, replica_groups=mesh['gx'=32,'gy'=16] {'gx'}, dimensions={0} | all-to-all | bytes 46080 | tf_op jit(solution)/shard_map/all_to_all | solution.py:149
  77.0 0.5 broadcast.973
  77.5 0.7 reduce.7
  78.8 15.5 %all_to_all.11 = f32[16,1,180]{2,1,0:T(1,128)S(1)} all-to-all(f32[16,1,180]{2,1,0:T(1,128)S(1)} %reshape.320), channel_id=1, replica_groups=mesh['gx'=32,'gy'=16] {'gy'}, dimensions={0} | all-to-all | bytes 23040 | tf_op jit(solution)/shard_map/all_to_all | solution.py:149
  94.3 0.7 reduce.8
  95.2 0.6 slice_bitcast_fusion.24
  95.9 0.5 cholesky.15
  96.4 0.6 compare_reduce_fusion
  97.1 0.6 fusion.113
  97.8 0.5 custom-call.8
  98.4 0.8 fusion.115
  99.2 1.3 %convolution_add_fusion = f32[6,3,5,9,129]{4,0,3,2,1:T(8,128)S(1)} fusion(f32[6,3,6,10,128]{4,0,3,2,1:T(8,128)S(1)} %maximum_multiply_fusion, f32[6,3,8,12,128]{4,0,3,2,1:T(8,128)S(1)} %copy.187, f32[6,6]{1,0:T(8,128)S(1)} %get-tuple-element.87), kind=kOutput, calls=%fused_computation.26 | convolution fusion | flops 7627770 | bytes 1855800 | tf_op jit(solution)/shard_map/kabcd,kj->jabcd/dot_general | solution.py:154
  103.1 3.0 %collective-permute-start.5 = (f32[4,8,128]{2,1,0:T(8,128)S(1)}, f32[4,8,128]{2,1,0:T(8,128)S(1)}, u32[]{:S(2)}, u32[]{:S(2)}) collective-permute-start(f32[4,8,128]{2,1,0:T(8,128)S(1)} %add_multiply_fusion), channel_id=1, source_target_pairs={{16,0},{32,16},{48,32},{64,48},{80,64},{96,80},{112,96},{128,112},... | collective-permute-start | bytes 49160 | tf_op jit(solution)/shard_map/ppermute | solution.py:31
  106.2 2.3 %collective-permute-start.4 = (f32[4,8,128]{2,1,0:T(8,128)S(1)}, f32[4,8,128]{2,1,0:T(8,128)S(1)}, u32[]{:S(2)}, u32[]{:S(2)}) collective-permute-start(f32[4,8,128]{2,1,0:T(8,128)S(1)} %add_multiply_fusion), channel_id=1, source_target_pairs={{0,16},{16,32},{32,48},{48,64},{64,80},{80,96},{96,112},{112,128},... | collective-permute-start | bytes 49160 | tf_op jit(solution)/shard_map/ppermute | solution.py:29
  108.5 0.7 convolution_add_fusion.1
  109.2 3.6 %collective-permute-done.4 = f32[4,8,128]{2,1,0:T(8,128)S(1)} collective-permute-done((f32[4,8,128]{2,1,0:T(8,128)S(1)}, f32[4,8,128]{2,1,0:T(8,128)S(1)}, u32[]{:S(2)}, u32[]{:S(2)}) %collective-permute-start.4) | collective-permute-done | bytes 16416 | tf_op jit(solution)/shard_map/ppermute | solution.py:29
  112.8 3.9 %collective-permute-start.6 = (f32[4,4,128]{2,1,0:T(4,128)S(1)}, f32[4,4,128]{2,1,0:T(4,128)S(1)}, u32[]{:S(2)}, u32[]{:S(2)}) collective-permute-start(f32[4,4,128]{2,1,0:T(4,128)S(1)} %get-tuple-element.79), channel_id=1, source_target_pairs={{0,1},{1,2},{2,3},{3,4},{4,5},{5,6},{6,7},{7,8},{8,9},{9,10},{10,1... | collective-permute-start | bytes 24584 | tf_op jit(solution)/shard_map/ppermute | solution.py:29
  116.7 1.9 %collective-permute-start.7 = (f32[4,4,128]{2,1,0:T(4,128)S(1)}, f32[4,4,128]{2,1,0:T(4,128)S(1)}, u32[]{:S(2)}, u32[]{:S(2)}) collective-permute-start(f32[4,4,128]{2,1,0:T(4,128)S(1)} %get-tuple-element.80), channel_id=1, source_target_pairs={{1,0},{2,1},{3,2},{4,3},{5,4},{6,5},{7,6},{8,7},{9,8},{10,9},{11,1... | collective-permute-start | bytes 24584 | tf_op jit(solution)/shard_map/ppermute | solution.py:31
  118.6 0.7 multiply_reduce_fusion.5
  119.3 0.8 copy.231
  122.0 0.7 multiply_minimum_fusion
  (94 shorter events, 10.4 us)
Async XLA Ops:
  4.7 14.6 %collective-permute-start = (f32[20,2,8,128]{3,1,2,0:T(2,128)S(1)}, f32[20,2,8,128]{3,1,2,0:T(2,128)S(1)}, u32[]{:S(2)}, u32[]{:S(2)}) collective-permute-start(f32[20,2,8,128]{3,1,2,0:T(2,128)S(1)} %get-tuple-element.72), channel_id=1, source_target_pairs={{0,16},{16,32},{32,48},{48,64},{64,80},{80,96},{96,112},{112,128},... | collective-permute-start | bytes 491528 | tf_op jit(solution)/shard_map/ppermute | solution.py:246
  8.7 11.4 %collective-permute-start.1 = (f32[20,2,8,128]{3,1,2,0:T(2,128)S(1)}, f32[20,2,8,128]{3,1,2,0:T(2,128)S(1)}, u32[]{:S(2)}, u32[]{:S(2)}) collective-permute-start(f32[20,2,8,128]{3,1,2,0:T(2,128)S(1)} %get-tuple-element.73), channel_id=1, source_target_pairs={{16,0},{32,16},{48,32},{64,48},{80,64},{96,80},{112,96},{128,112},... | collective-permute-start | bytes 491528 | tf_op jit(solution)/shard_map/ppermute | solution.py:247
  20.2 6.9 %collective-permute-start.2 = (f32[20,8,2,128]{3,1,2,0:T(8,128)S(1)}, f32[20,8,2,128]{3,1,2,0:T(8,128)S(1)}, u32[]{:S(2)}, u32[]{:S(2)}) collective-permute-start(f32[20,8,2,128]{3,1,2,0:T(8,128)S(1)} %get-tuple-element.67), channel_id=1, source_target_pairs={{0,1},{1,2},{2,3},{3,4},{4,5},{5,6},{6,7},{7,8},{8,9},{9,10},{10,1... | collective-permute-start | bytes 491528 | tf_op jit(solution)/shard_map/ppermute | solution.py:246
  24.8 6.6 %collective-permute-start.3 = (f32[20,8,2,128]{3,1,2,0:T(8,128)S(1)}, f32[20,8,2,128]{3,1,2,0:T(8,128)S(1)}, u32[]{:S(2)}, u32[]{:S(2)}) collective-permute-start(f32[20,8,2,128]{3,1,2,0:T(8,128)S(1)} %get-tuple-element.68), channel_id=1, source_target_pairs={{1,0},{2,1},{3,2},{4,3},{5,4},{6,5},{7,6},{8,7},{9,8},{10,9},{11,1... | collective-permute-start | bytes 491528 | tf_op jit(solution)/shard_map/ppermute | solution.py:247
  35.1 1.1 copy-start.3
  102.0 1.1 copy-start.1
  102.0 1.1 copy-start.2
  102.0 6.5 %copy-start = (f32[6,3,4,8,128]{4,3,2,1,0:T(8,128)S(1)}, f32[6,3,4,8,128]{4,3,2,1,0:T(8,128)}, u32[]{:S(2)}) copy-start(f32[6,3,4,8,128]{4,3,2,1,0:T(8,128)} %param.8) | copy-start | bytes 884740
  103.1 6.0 %collective-permute-start.5 = (f32[4,8,128]{2,1,0:T(8,128)S(1)}, f32[4,8,128]{2,1,0:T(8,128)S(1)}, u32[]{:S(2)}, u32[]{:S(2)}) collective-permute-start(f32[4,8,128]{2,1,0:T(8,128)S(1)} %add_multiply_fusion), channel_id=1, source_target_pairs={{16,0},{32,16},{48,32},{64,48},{80,64},{96,80},{112,96},{128,112},... | collective-permute-start | bytes 49160 | tf_op jit(solution)/shard_map/ppermute | solution.py:31
  106.2 6.6 %collective-permute-start.4 = (f32[4,8,128]{2,1,0:T(8,128)S(1)}, f32[4,8,128]{2,1,0:T(8,128)S(1)}, u32[]{:S(2)}, u32[]{:S(2)}) collective-permute-start(f32[4,8,128]{2,1,0:T(8,128)S(1)} %add_multiply_fusion), channel_id=1, source_target_pairs={{0,16},{16,32},{32,48},{48,64},{64,80},{80,96},{96,112},{112,128},... | collective-permute-start | bytes 49160 | tf_op jit(solution)/shard_map/ppermute | solution.py:29
  112.8 9.2 %collective-permute-start.6 = (f32[4,4,128]{2,1,0:T(4,128)S(1)}, f32[4,4,128]{2,1,0:T(4,128)S(1)}, u32[]{:S(2)}, u32[]{:S(2)}) collective-permute-start(f32[4,4,128]{2,1,0:T(4,128)S(1)} %get-tuple-element.79), channel_id=1, source_target_pairs={{0,1},{1,2},{2,3},{3,4},{4,5},{5,6},{6,7},{7,8},{8,9},{9,10},{10,1... | collective-permute-start | bytes 24584 | tf_op jit(solution)/shard_map/ppermute | solution.py:29
  116.7 5.3 %collective-permute-start.7 = (f32[4,4,128]{2,1,0:T(4,128)S(1)}, f32[4,4,128]{2,1,0:T(4,128)S(1)}, u32[]{:S(2)}, u32[]{:S(2)}) collective-permute-start(f32[4,4,128]{2,1,0:T(4,128)S(1)} %get-tuple-element.80), channel_id=1, source_target_pairs={{1,0},{2,1},{3,2},{4,3},{5,4},{6,5},{7,6},{8,7},{9,8},{10,9},{11,1... | collective-permute-start | bytes 24584 | tf_op jit(solution)/shard_map/ppermute | solution.py:31
